TPU v7x, 256 devices: a whole 4x4x8 slice. The times are simulated.
256 devices in a mesh: rep: 16 (over x, y_lo, core), blk: 16 (over y_hi, z).
Axes of the slice: x: 4, y: 4 (y_hi: 2, y_lo: 2; y = y_hi * 2 + y_lo), z: 8, core: 2. Of those that a mesh axis runs over, the one named last changes fastest.
Arguments:
- features: bfloat16 [65536, 1024], P(('rep', 'blk')), may hold values from -6 to 6
- weight: bfloat16 [1024, 1024], replicated, may hold values from -0.1875 to 0.1875
- bias: bfloat16 [1024], replicated, may hold values from -3 to 3
- tile_vals: bfloat16 [16, 16, 32, 4, 128, 128], P('rep', 'blk'), may hold values from -0.125 to 0.125
- tile_col: int32 [16, 16, 32, 4], P('rep', 'blk'), may hold values from 0 to 31
- tile_count: int32 [16, 16, 32], P('rep', 'blk'), may hold values from 0 to 4, as said below
Outputs:
- hidden: bfloat16 [65536, 1024], P(('rep', 'blk'))
Inputs may be any that keep to these rules, and one draw needn't show every extreme that they name: The first tile_count slots are the live ones; some entry equals 4 in every draw.
All inputs are finite; a program needn't handle non-finite values.
Results may differ from a plain program's by a relative error of at most 0.014.
Values may be sent and summed in bfloat16 or wider, within the bound.
No kernel may reach another device: no remote copies, remote signals or barrier semaphores. Data moves between devices by JAX's collectives and lax.ppermute only.
A program may use at most 64 MiB of HBM per device.

v0:
```python
import jax
import jax.numpy as jnp
from jax import lax
from jax.sharding import PartitionSpec as P


def term_maker(gathered, tile_block, col_index, live_count):
    tile_side = tile_block.shape[-1]
    slot_total = tile_block.shape[1]
    sources = gathered.reshape(-1, tile_side, gathered.shape[1])

    def block_sum(blk_id):
        block_tiles = tile_block[blk_id]
        block_cols = col_index[blk_id]
        block_live = live_count[blk_id]
        keep_mask = (jnp.arange(slot_total, dtype=jnp.int32) < block_live).astype(jnp.bfloat16)
        masked = block_tiles * keep_mask[:, None, None]
        picked = sources[block_cols]
        return jnp.einsum("kij,kjd->id", masked, picked, preferred_element_type=jnp.float32)

    def partial_term(start, count):
        block_ids = jnp.arange(count // tile_side, dtype=jnp.int32)
        return lax.map(block_sum, block_ids).reshape(count, -1)

    return partial_term


def body(features, weight, bias, tile_vals, tile_col, tile_count):
    tile_block = tile_vals[0, 0]
    col_index = tile_col[0, 0]
    live_count = tile_count[0, 0]
    row_total = features.shape[0]
    gathered = lax.all_gather(features, "rep", axis=0, tiled=True)
    summer = term_maker(gathered, tile_block, col_index, live_count)
    summed = lax.psum_scatter(
        summer(jnp.int32(0), row_total * lax.axis_size("blk")).astype(jnp.bfloat16),
        "blk",
        scatter_dimension=0,
        tiled=True,
    )
    mixed = jnp.dot(summed, weight, preferred_element_type=jnp.float32) + bias.astype(jnp.float32)
    return jnp.maximum(mixed, 0.0).astype(jnp.bfloat16)


def solution(mesh):
    return jax.shard_map(
        body,
        mesh=mesh,
        in_specs=(
            P(("rep", "blk"), None),
            P(),
            P(),
            P("rep", "blk", None, None, None, None),
            P("rep", "blk", None, None),
            P("rep", "blk", None),
        ),
        out_specs=P(("rep", "blk"), None),
        check_vma=False,
    )
```

profile of v0, /device:TPU:2, one launch (start us, length us, event | category | flops | bytes accessed | tf_op | source)
XLA Modules:
  0.0 625.8 jit_solution(16292536515272177173)
XLA Ops:
  8.1 58.6 %all-gather.2.cloned.1.call-done = bf16[4096,1024]{1,0:T(8,128)(2,1)} async-done(((bf16[256,1024]{1,0:T(8,128)(2,1)}), bf16[4096,1024]{1,0:T(8,128)(2,1)}) %all-gather.2.cloned.1.call-update) | async-done | bytes 8388624 | tf_op jit(solution)/shard_map/all_gather | solution.py:33
  66.7 322.8 %while.10 = (s32[]{:T(128)}, bf16[32,128,1024]{2,1,0:T(8,128)(2,1)}, s32[32]{0:T(128)S(1)}, bf16[32,4,128,128]{3,2,1,0:T(8,128)(2,1)}, s32[32]{0:T(128)}, /*inde...) while((s32[]{:T(128)}, bf16[32,128,1024]{2,1,0:T(8,128)(2,1)}, ...), condition=%wide.region_1.2_spmd, body=%wide.region_0.1_spmd.sunk | while | flops 134284320 | bytes 3805947 | solution.py:23
  69.0 4.0 gather_fusion
  74.8 2.0 fusion.16
  79.1 4.0 gather_fusion
  84.9 2.0 fusion.16
  89.2 4.0 gather_fusion
  95.0 2.0 fusion.16
  99.3 4.0 gather_fusion
  105.1 2.0 fusion.16
  109.4 4.0 gather_fusion
  119.4 4.0 gather_fusion
  125.3 2.0 fusion.16
  129.5 4.0 gather_fusion
  135.3 2.0 fusion.16
  139.6 4.0 gather_fusion
  145.4 2.0 fusion.16
  149.7 4.0 gather_fusion
  155.5 2.0 fusion.16
  159.8 4.0 gather_fusion
  165.6 2.0 fusion.16
  169.9 4.0 gather_fusion
  175.7 2.0 fusion.16
  179.9 4.0 gather_fusion
  185.8 2.0 fusion.16
  190.0 4.0 gather_fusion
  195.8 2.0 fusion.16
  200.1 4.0 gather_fusion
  205.9 2.0 fusion.16
  210.2 4.0 gather_fusion
  220.3 4.0 gather_fusion
  226.1 2.0 fusion.16
  230.3 4.0 gather_fusion
  236.2 2.0 fusion.16
  240.4 4.0 gather_fusion
  246.2 2.0 fusion.16
  250.5 4.0 gather_fusion
  256.4 2.0 fusion.16
  260.7 4.0 gather_fusion
  266.5 2.0 fusion.16
  270.7 4.0 gather_fusion
  276.6 2.0 fusion.16
  280.8 4.0 gather_fusion
  286.6 2.0 fusion.16
  290.9 4.0 gather_fusion
  301.0 4.0 gather_fusion
  311.0 4.0 gather_fusion
  316.9 2.0 fusion.16
  321.1 4.0 gather_fusion
  327.0 2.0 fusion.16
  331.2 4.0 gather_fusion
  337.0 2.0 fusion.16
  341.3 4.0 gather_fusion
  347.1 2.0 fusion.16
  351.4 4.0 gather_fusion
  357.2 2.0 fusion.16
  361.5 4.0 gather_fusion
  367.3 2.0 fusion.16
  371.6 4.0 gather_fusion
  377.4 2.0 fusion.16
  381.6 4.0 gather_fusion
  387.4 2.0 fusion.16
  390.1 226.2 %reduce-scatter.2.cloned.1.call-done = bf16[256,1024]{1,0:T(8,128)(2,1)} async-done(((bf16[4096,1024]{1,0:T(8,128)(2,1)}), bf16[256,1024]{1,0:T(8,128)(2,1)}) %reduce-scatter.2.cloned.1.call-update) | async-done | bytes 524304 | tf_op jit(solution)/shard_map/reduce_scatter | solution.py:35
  616.4 2.5 fusion.7
  (176 shorter events, 86.8 us)
Async XLA Ops:
  6.5 609.8 %copy-start = (bf16[1024,1024]{1,0:T(8,128)(2,1)S(1)}, bf16[1024,1024]{1,0:T(8,128)(2,1)}, u32[]{:S(2)}) copy-start(bf16[1024,1024]{1,0:T(8,128)(2,1)} %param.9) | copy-start | bytes 6291460
  6.5 60.1 %all-gather.2.cloned.1.call-start = ((), (), s32[]{:S(2)}) async-start(), calls=%async_computation.1 | async-start | bytes 8912896 | tf_op jit(solution)/shard_map/all_gather | solution.py:33
  7.3 609.1 %reduce-scatter.2.cloned.1.call-start = ((), (), s32[]{:S(2)}) async-start(), calls=%async_computation.2 | async-start | bytes 8912896 | tf_op jit(solution)/shard_map/reduce_scatter | solution.py:35
  389.4 0.7 copy-start.1
Sparse Core Ops, SparseCore 0:
  9.2 57.4 all-gather.1
  389.6 226.7 reduce-scatter.1
where the time goes:
time: 629 us; the launch traced here: 626 us
  waiting for transfers between devices  286 us (45%)
  local copies, waits for them, and re-layouts  187 us (30%)
  matrix products  65.6 us (10%)
  loops' own time  55.1 us (9%)
  other arithmetic  18.6 us (3%)
  between operations  13.4 us (2%)
    reduce_scatter x1, waiting for transfers between devices, body(): lax.psum_scatter(summer(jnp.int32(0), row_total * lax.axis_size('blk')).a...  226 us
    gather x32, local copies, waits for them, and re-layouts, block_sum(): picked = sources[block_cols]  128 us
    dot_general x32, matrix products, block_sum(): jnp.einsum('kij,kjd->id', masked, picked, preferred_element_type=jnp.floa...  63.1 us
    all_gather x1, waiting for transfers between devices, body(): gathered = lax.all_gather(features, 'rep', axis=0, tiled=True)  58.6 us
    another operation x1, loops' own time, partial_term(): return lax.map(block_sum, block_ids).reshape(count, -1)  55.1 us
    dynamic_slice x32, local copies, waits for them, and re-layouts, block_sum(): block_live = live_count[blk_id]  39.6 us
    dynamic_slice x32, local copies, waits for them, and re-layouts, partial_term(): return lax.map(block_sum, block_ids).reshape(count, -1)  18.5 us
    convert_element_type x32, other arithmetic, block_sum(): (jnp.arange(slot_total, dtype=jnp.int32) < block_live).astype(jnp.bfloat16)  18 us
  transfers between devices with their start and end apart: 2, of which 2 were waited for; matrix products, arithmetic and copies ran while one was open for 0% of the time, Pallas kernels for 0%

commit v1 on v0

v1 whole, which is shorter than its diff:
```python
import jax
import jax.numpy as jnp
from jax import lax
from jax.experimental import pallas as pl
from jax.experimental.pallas import tpu as pltpu
from jax.sharding import PartitionSpec as P


def sparse_partial(gathered, tiles, cols, counts):
    n_blocks, slots, side, _ = tiles.shape
    width = gathered.shape[1]
    n_src = gathered.shape[0]

    def kernel(cols_ref, counts_ref, tile_ref, src_ref, out_ref, acc_ref):
        b = pl.program_id(0)
        live = counts_ref[b]
        acc_ref[...] = jnp.zeros_like(acc_ref)
        for k in range(slots):
            @pl.when(k < live)
            def _():
                start = pl.multiple_of(cols_ref[b * slots + k] * side, side)
                src = src_ref[pl.ds(start, side), :]
                acc_ref[...] += jnp.dot(tile_ref[0, k], src, preferred_element_type=jnp.float32)
        out_ref[...] = acc_ref[...].astype(out_ref.dtype)

    grid_spec = pltpu.PrefetchScalarGridSpec(
        num_scalar_prefetch=2,
        grid=(n_blocks,),
        in_specs=[
            pl.BlockSpec((1, slots, side, side), lambda b, c, n: (b, 0, 0, 0)),
            pl.BlockSpec((n_src, width), lambda b, c, n: (0, 0)),
        ],
        out_specs=pl.BlockSpec((side, width), lambda b, c, n: (b, 0)),
        scratch_shapes=[pltpu.VMEM((side, width), jnp.float32)],
    )
    return pl.pallas_call(
        kernel,
        grid_spec=grid_spec,
        out_shape=jax.ShapeDtypeStruct((n_blocks * side, width), jnp.bfloat16),
        compiler_params=pltpu.CompilerParams(
            dimension_semantics=("arbitrary",), vmem_limit_bytes=48 * 1024 * 1024
        ),
    )(cols.reshape(-1), counts, tiles, gathered)


def body(features, weight, bias, tile_vals, tile_col, tile_count):
    gathered = lax.all_gather(features, "rep", axis=0, tiled=True)
    partial = sparse_partial(gathered, tile_vals[0, 0], tile_col[0, 0], tile_count[0, 0])
    summed = lax.psum_scatter(partial, "blk", scatter_dimension=0, tiled=True)
    mixed = jnp.dot(summed, weight, preferred_element_type=jnp.float32) + bias.astype(jnp.float32)
    return jnp.maximum(mixed, 0.0).astype(jnp.bfloat16)


def solution(mesh):
    return jax.shard_map(
        body,
        mesh=mesh,
        in_specs=(
            P(("rep", "blk"), None),
            P(),
            P(),
            P("rep", "blk", None, None, None, None),
            P("rep", "blk", None, None),
            P("rep", "blk", None),
        ),
        out_specs=P(("rep", "blk"), None),
        check_vma=False,
    )
```

time: 629 us -> 330 us (0.52)
  local copies, waits for them, and re-layouts: 187 us -> 4.37 us
  matrix products: 65.6 us -> 2.55 us
  loops' own time: 55.1 us -> 0 us
  Pallas kernels: 0 us -> 18.7 us
  other arithmetic: 18.6 us -> 0.01 us
    gather x32 -> x0, local copies, waits for them, and re-layouts: 128 us -> none  [block_sum(): picked = sources[block_cols]]
    dot_general x32 -> x0, matrix products: 63.1 us -> none  [block_sum(): jnp.einsum('kij,kjd->id', masked, picked, preferred_element_type=jnp.floa...]
    dynamic_slice x64 -> x0, local copies, waits for them, and re-layouts: 58.1 us -> none  [the longest x32 39.6 us: block_sum(): block_live = live_count[blk_id]]
    another operation x1 -> x0, loops' own time: 55.1 us -> none  [partial_term(): return lax.map(block_sum, block_ids).reshape(count, -1)]
    pallas_call x0 -> x1, Pallas kernels: none -> 18.7 us  [sparse_partial(): pl.pallas_call(kernel, grid_spec=grid_spec, out_shape=jax.ShapeDtypeStruc...]
    convert_element_type x32 -> x0, other arithmetic: 18 us -> none  [block_sum(): (jnp.arange(slot_total, dtype=jnp.int32) < block_live).astype(jnp.bfloat16)]
where the time goes in v1:
time: 330 us; the launch traced here: 329 us
  waiting for transfers between devices  290 us (88%)
  Pallas kernels  18.7 us (6%)
  between operations  13.4 us (4%)
  local copies, waits for them, and re-layouts  4.37 us (1%)
    reduce_scatter x1, waiting for transfers between devices, body(): summed = lax.psum_scatter(partial, 'blk', scatter_dimension=0, tiled=True)  231 us
    all_gather x1, waiting for transfers between devices, body(): gathered = lax.all_gather(features, 'rep', axis=0, tiled=True)  58.5 us
    pallas_call x1, Pallas kernels, sparse_partial(): pl.pallas_call(kernel, grid_spec=grid_spec, out_shape=jax.ShapeDtypeStruc...  18.7 us
  transfers between devices with their start and end apart: 2, of which 2 were waited for; matrix products, arithmetic and copies ran while one was open for 0% of the time, Pallas kernels for 0%

profile of v1, /device:TPU:2, one launch (start us, length us, event | category | flops | bytes accessed | tf_op | source)
XLA Modules:
  0.0 329.2 jit_solution(4045949423133570625)
XLA Ops:
  6.5 0.0 copy-start
  6.5 0.0 all-gather.2.cloned.1.call-start
  6.5 0.7 all-gather.2.cloned.1.call-update
  7.3 0.0 reduce-scatter.2.cloned.1.call-start
  7.3 0.8 copy.8
  8.1 0.1 reshape_squeeze.3.cols_ref
  8.2 58.5 %all-gather.2.cloned.1.call-done.src_ref = bf16[4096,1024]{1,0:T(8,128)(2,1)} async-done(((bf16[256,1024]{1,0:T(8,128)(2,1)}), bf16[4096,1024]{1,0:T(8,128)(2,1)}) %all-gather.2.cloned.1.call-update) | async-done | bytes 8388624 | tf_op jit(solution)/shard_map/all_gather | solution.py:47
  66.7 0.0 copy-start.1
  66.7 2.2 copy-done.1
  68.8 0.0 copy-start.2
  68.9 0.7 copy-done.2
  69.5 18.7 %shard_map.64 = bf16[4096,1024]{1,0:T(8,128)(2,1)} custom-call(s32[128]{0:T(128)S(1)} %reshape_squeeze.3.cols_ref, s32[32]{0:T(128)S(1)} %bitcast.7, bf16[32,4,128,128]{3,2,1,0:T(8,128)(2,1)S(1)} %bitcast.6, bf16[4096,1024]{1,0:T(8,128)(2,1)} %all-gather.2.cloned.1.call-done.src_ref), custom_call_target="tpu_custom_call" | custom-call | tf_op jit(solution)/shard_map/pallas_call | solution.py:36
  88.2 0.0 copy-start.3
  88.2 0.0 reduce-scatter.2.cloned.1.call-update
  88.3 0.7 copy-done.3
  88.9 230.9 %reduce-scatter.2.cloned.1.call-done = bf16[256,1024]{1,0:T(8,128)(2,1)} async-done(((bf16[4096,1024]{1,0:T(8,128)(2,1)}), bf16[256,1024]{1,0:T(8,128)(2,1)}) %reduce-scatter.2.cloned.1.call-update) | async-done | bytes 524304 | tf_op jit(solution)/shard_map/reduce_scatter | solution.py:49
  319.9 0.0 copy-done
  319.9 2.5 fusion.1
  (1 shorter events, 0.0 us)
Async XLA Ops:
  6.5 313.3 %copy-start = (bf16[1024,1024]{1,0:T(8,128)(2,1)S(1)}, bf16[1024,1024]{1,0:T(8,128)(2,1)}, u32[]{:S(2)}) copy-start(bf16[1024,1024]{1,0:T(8,128)(2,1)} %param.7) | copy-start | bytes 6291460
  6.5 60.1 %all-gather.2.cloned.1.call-start = ((), (), s32[]{:S(2)}) async-start(), calls=%async_computation.1 | async-start | bytes 8912896 | tf_op jit(solution)/shard_map/all_gather | solution.py:47
  7.3 312.6 %reduce-scatter.2.cloned.1.call-start = ((), (), s32[]{:S(2)}) async-start(), calls=%async_computation.2 | async-start | bytes 8912896 | tf_op jit(solution)/shard_map/reduce_scatter | solution.py:49
  66.7 2.2 copy-start.1
  68.8 0.7 copy-start.2
  88.2 0.7 copy-start.3
Sparse Core Ops, SparseCore 0:
  9.2 57.4 all-gather.1
  88.4 231.4 reduce-scatter.1

commit v2 on v1

--- a/solution.py
+++ b/solution.py
@@ -3,10 +3,10 @@
 from jax import lax
 from jax.experimental import pallas as pl
 from jax.experimental.pallas import tpu as pltpu
-from jax.sharding import PartitionSpec as P
+from jax.sharding import Mesh, PartitionSpec as P
 
 
-def sparse_partial(gathered, tiles, cols, counts):
+def sparse_partial(gathered, tiles, cols, counts, out_pos):
     n_blocks, slots, side, _ = tiles.shape
     width = gathered.shape[1]
     n_src = gathered.shape[0]
@@ -30,7 +30,7 @@
             pl.BlockSpec((1, slots, side, side), lambda b, c, n: (b, 0, 0, 0)),
             pl.BlockSpec((n_src, width), lambda b, c, n: (0, 0)),
         ],
-        out_specs=pl.BlockSpec((side, width), lambda b, c, n: (b, 0)),
+        out_specs=pl.BlockSpec((side, width), lambda b, c, n: (out_pos(b), 0)),
         scratch_shapes=[pltpu.VMEM((side, width), jnp.float32)],
     )
     return pl.pallas_call(
@@ -44,25 +44,38 @@
 
 
 def body(features, weight, bias, tile_vals, tile_col, tile_count):
+    n_hi = lax.axis_size("yh")
+    n_lo = lax.axis_size("z")
+    per_dev = features.shape[0] // tile_vals.shape[-1]
+
+    def out_pos(b):
+        j = b // per_dev
+        return ((j % n_lo) * n_hi + j // n_lo) * per_dev + b % per_dev
+
     gathered = lax.all_gather(features, "rep", axis=0, tiled=True)
-    partial = sparse_partial(gathered, tile_vals[0, 0], tile_col[0, 0], tile_count[0, 0])
-    summed = lax.psum_scatter(partial, "blk", scatter_dimension=0, tiled=True)
+    partial = sparse_partial(gathered, tile_vals[0, 0], tile_col[0, 0], tile_count[0, 0], out_pos)
+    summed = lax.psum_scatter(partial, "z", scatter_dimension=0, tiled=True)
+    summed = lax.psum_scatter(summed, "yh", scatter_dimension=0, tiled=True)
     mixed = jnp.dot(summed, weight, preferred_element_type=jnp.float32) + bias.astype(jnp.float32)
     return jnp.maximum(mixed, 0.0).astype(jnp.bfloat16)
 
 
 def solution(mesh):
+    n_rep, n_blk = mesh.devices.shape
+    n_hi = 2
+    split = Mesh(mesh.devices.reshape(n_rep, n_hi, n_blk // n_hi), ("rep", "yh", "z"))
+    blk = ("yh", "z")
     return jax.shard_map(
         body,
-        mesh=mesh,
+        mesh=split,
         in_specs=(
-            P(("rep", "blk"), None),
+            P(("rep",) + blk, None),
             P(),
             P(),
-            P("rep", "blk", None, None, None, None),
-            P("rep", "blk", None, None),
-            P("rep", "blk", None),
+            P("rep", blk, None, None, None, None),
+            P("rep", blk, None, None),
+            P("rep", blk, None),
         ),
-        out_specs=P(("rep", "blk"), None),
+        out_specs=P(("rep",) + blk, None),
         check_vma=False,
     )

time: 330 us -> 229 us (0.69)
  waiting for transfers between devices: 290 us -> 190 us
    reduce_scatter x1 -> x2, waiting for transfers between devices: 231 us -> 130 us  [the longest x1 102 us: body(): summed = lax.psum_scatter(partial, 'z', scatter_dimension=0, tiled=True)]
  transfers between devices with their start and end apart: 2 -> 3, of which waited for: 2 -> 3; matrix products, arithmetic and copies ran while one was open for 0% -> 0% of each run, Pallas kernels for 0% -> 0%
where the time goes in v2:
time: 229 us; the launch traced here: 228 us
  waiting for transfers between devices  190 us (83%)
  Pallas kernels  18.6 us (8%)
  between operations  13.1 us (6%)
  local copies, waits for them, and re-layouts  3.72 us (2%)
  matrix products  2.55 us (1%)
    reduce_scatter x1, waiting for transfers between devices, body(): summed = lax.psum_scatter(partial, 'z', scatter_dimension=0, tiled=True)  102 us
    all_gather x1, waiting for transfers between devices, body(): gathered = lax.all_gather(features, 'rep', axis=0, tiled=True)  58.5 us
    reduce_scatter x1, waiting for transfers between devices, body(): summed = lax.psum_scatter(summed, 'yh', scatter_dimension=0, tiled=True)  28.1 us
    pallas_call x1, Pallas kernels, sparse_partial(): pl.pallas_call(kernel, grid_spec=grid_spec, out_shape=jax.ShapeDtypeStruc...  18.6 us
  transfers between devices with their start and end apart: 3, of which 3 were waited for; matrix products, arithmetic and copies ran while one was open for 0% of the time, Pallas kernels for 0%

profile of v2, /device:TPU:2, one launch (start us, length us, event | category | flops | bytes accessed | tf_op | source)
XLA Modules:
  0.0 227.8 jit_solution(39507462470563791)
XLA Ops:
  6.5 0.0 copy-start
  6.5 0.0 all-gather.2.cloned.1.call-start
  6.5 0.7 all-gather.2.cloned.1.call-update
  7.3 0.0 reduce-scatter.3.cloned.1.call-start
  7.3 0.8 copy.8
  8.1 0.1 reshape_squeeze.3.cols_ref
  8.2 58.5 %all-gather.2.cloned.1.call-done.src_ref = bf16[4096,1024]{1,0:T(8,128)(2,1)} async-done(((bf16[256,1024]{1,0:T(8,128)(2,1)}), bf16[4096,1024]{1,0:T(8,128)(2,1)}) %all-gather.2.cloned.1.call-update) | async-done | bytes 8388624 | tf_op jit(solution)/shard_map/all_gather | solution.py:55
  66.7 0.0 copy-start.1
  66.7 2.2 copy-done.1
  68.8 0.0 copy-start.2
  68.9 0.7 copy-done.2
  69.5 18.6 %shard_map.64 = bf16[4096,1024]{1,0:T(8,128)(2,1)} custom-call(s32[128]{0:T(128)S(1)} %reshape_squeeze.3.cols_ref, s32[32]{0:T(128)S(1)} %bitcast.7, bf16[32,4,128,128]{3,2,1,0:T(8,128)(2,1)S(1)} %bitcast.6, bf16[4096,1024]{1,0:T(8,128)(2,1)} %all-gather.2.cloned.1.call-done.src_ref), custom_call_target="tpu_custom_call" | custom-call | tf_op jit(solution)/shard_map/pallas_call | solution.py:36
  88.1 0.0 copy-start.3
  88.1 0.0 reduce-scatter.3.cloned.1.call-update
  88.1 0.0 reduce-scatter.5.cloned.1.call-start
  88.2 102.3 %reduce-scatter.3.cloned.1.call-done = bf16[512,1024]{1,0:T(8,128)(2,1)} async-done(((bf16[4096,1024]{1,0:T(8,128)(2,1)}), bf16[512,1024]{1,0:T(8,128)(2,1)}) %reduce-scatter.3.cloned.1.call-update) | async-done | bytes 1048592 | tf_op jit(solution)/shard_map/reduce_scatter | solution.py:57
  190.5 0.0 reduce-scatter.5.cloned.1.call-update
  190.5 0.0 copy-done.3
  190.6 28.1 %reduce-scatter.5.cloned.1.call-done = bf16[256,1024]{1,0:T(8,128)(2,1)} async-done(((bf16[512,1024]{1,0:T(8,128)(2,1)}), bf16[256,1024]{1,0:T(8,128)(2,1)}) %reduce-scatter.5.cloned.1.call-update) | async-done | bytes 524304 | tf_op jit(solution)/shard_map/reduce_scatter | solution.py:58
  218.7 0.0 copy-done
  218.7 2.5 %fusion.1 = bf16[256,1024]{1,0:T(8,128)(2,1)} fusion(bf16[256,1024]{1,0:T(8,128)(2,1)} %reduce-scatter.5.cloned.1.call-done, bf16[1024,1024]{1,0:T(8,128)(2,1)S(1)} %copy-done, f32[1024]{0:T(1024)S(1)} %convert_element_type.6), kind=kOutput, calls=%fused_computation.2 | convolution fusion | flops 537657344 | bytes 3149824 | tf_op jit(solution)/shard_map/dot_general | solution.py:59
  (1 shorter events, 0.0 us)
Async XLA Ops:
  6.5 212.1 %copy-start = (bf16[1024,1024]{1,0:T(8,128)(2,1)S(1)}, bf16[1024,1024]{1,0:T(8,128)(2,1)}, u32[]{:S(2)}) copy-start(bf16[1024,1024]{1,0:T(8,128)(2,1)} %param.7) | copy-start | bytes 6291460
  6.5 60.1 %all-gather.2.cloned.1.call-start = ((), (), s32[]{:S(2)}) async-start(), calls=%async_computation.2 | async-start | bytes 8912896 | tf_op jit(solution)/shard_map/all_gather | solution.py:55
  7.3 183.3 %reduce-scatter.3.cloned.1.call-start = ((), (), s32[]{:S(2)}) async-start(), calls=%async_computation.3 | async-start | bytes 9437184 | tf_op jit(solution)/shard_map/reduce_scatter | solution.py:57
  66.7 2.2 copy-start.1
  68.8 0.7 copy-start.2
  88.1 102.4 %copy-start.3 = (bf16[1024]{0:T(1024)(128)(2,1)S(1)}, bf16[1024]{0:T(1024)(128)(2,1)}, u32[]{:S(2)}) copy-start(bf16[1024]{0:T(1024)(128)(2,1)} %param.8) | copy-start | bytes 6148
  88.1 130.5 %reduce-scatter.5.cloned.1.call-start = ((), (), s32[]{:S(2)}) async-start(), calls=%async_computation.4 | async-start | bytes 1572864 | tf_op jit(solution)/shard_map/reduce_scatter | solution.py:58
Sparse Core Ops, SparseCore 0:
  9.2 57.4 all-gather.1
  88.2 102.2 reduce-scatter.2
  193.0 25.6 reduce-scatter.4

commit v3 on v2

--- a/solution.py
+++ b/solution.py
@@ -43,6 +43,9 @@
     )(cols.reshape(-1), counts, tiles, gathered)
 
 
+N_CHUNKS = 4
+
+
 def body(features, weight, bias, tile_vals, tile_col, tile_count):
     n_hi = lax.axis_size("yh")
     n_lo = lax.axis_size("z")
@@ -52,10 +55,18 @@
         j = b // per_dev
         return ((j % n_lo) * n_hi + j // n_lo) * per_dev + b % per_dev
 
-    gathered = lax.all_gather(features, "rep", axis=0, tiled=True)
-    partial = sparse_partial(gathered, tile_vals[0, 0], tile_col[0, 0], tile_count[0, 0], out_pos)
-    summed = lax.psum_scatter(partial, "z", scatter_dimension=0, tiled=True)
-    summed = lax.psum_scatter(summed, "yh", scatter_dimension=0, tiled=True)
+    n_rep = lax.axis_size("rep")
+    width = features.shape[1]
+    chunk = width // N_CHUNKS
+    pieces = []
+    for i in range(N_CHUNKS):
+        cols = features[:, i * chunk:(i + 1) * chunk]
+        copies = jnp.broadcast_to(cols[None], (n_rep,) + cols.shape).reshape(-1, chunk)
+        gathered = lax.all_to_all(copies, "rep", 0, 0, tiled=True)
+        partial = sparse_partial(gathered, tile_vals[0, 0], tile_col[0, 0], tile_count[0, 0], out_pos)
+        part = lax.psum_scatter(partial, "z", scatter_dimension=0, tiled=True)
+        pieces.append(lax.psum_scatter(part, "yh", scatter_dimension=0, tiled=True))
+    summed = jnp.concatenate(pieces, axis=1)
     mixed = jnp.dot(summed, weight, preferred_element_type=jnp.float32) + bias.astype(jnp.float32)
     return jnp.maximum(mixed, 0.0).astype(jnp.bfloat16)
 

time: 229 us -> 365 us (1.59)
  blocking collectives: 0 us -> 102 us
  Pallas kernels: 18.6 us -> 69.2 us
  waiting for transfers between devices: 190 us -> 160 us
  starting transfers between devices: 0.08 us -> 6.86 us
  local copies, waits for them, and re-layouts: 3.72 us -> 8.89 us
    all_to_all x0 -> x3, blocking collectives: none -> 102 us  [body(): gathered = lax.all_to_all(copies, 'rep', 0, 0, tiled=True)]
    all_gather x1 -> x0, waiting for transfers between devices: 58.5 us -> none  [body(): gathered = lax.all_gather(features, 'rep', axis=0, tiled=True)]
    pallas_call x1 -> x4, Pallas kernels: 18.6 us -> 69.2 us  [sparse_partial(): pl.pallas_call(kernel, grid_spec=grid_spec, out_shape=jax.ShapeDtypeStruc...]
    all_to_all x0 -> x1, waiting for transfers between devices: none -> 26 us  [body(): gathered = lax.all_to_all(copies, 'rep', 0, 0, tiled=True)]
    all_to_all x0 -> x1, starting transfers between devices: none -> 6.54 us  [body(): gathered = lax.all_to_all(copies, 'rep', 0, 0, tiled=True)]
    reduce_scatter x2 -> x8, waiting for transfers between devices: 130 us -> 132 us  [the longest x4 80 us: body(): pieces.append(lax.psum_scatter(part, 'yh', scatter_dimension=0, tiled=True))]
  transfers between devices with their start and end apart: 3 -> 9, of which waited for: 3 -> 6; matrix products, arithmetic and copies ran while one was open for 0% -> 0% of each run, Pallas kernels for 0% -> 14%
where the time goes in v3:
time: 365 us; the launch traced here: 363 us
  waiting for transfers between devices  160 us (44%)
  blocking collectives  102 us (28%)
  Pallas kernels  69.2 us (19%)
  between operations  13.7 us (4%)
  local copies, waits for them, and re-layouts  8.89 us (2%)
  starting transfers between devices  6.86 us (2%)
    all_to_all x3, blocking collectives, body(): gathered = lax.all_to_all(copies, 'rep', 0, 0, tiled=True)  102 us
    reduce_scatter x4, waiting for transfers between devices, body(): pieces.append(lax.psum_scatter(part, 'yh', scatter_dimension=0, tiled=True))  80 us
    pallas_call x4, Pallas kernels, sparse_partial(): pl.pallas_call(kernel, grid_spec=grid_spec, out_shape=jax.ShapeDtypeStruc...  69.2 us
    reduce_scatter x4, waiting for transfers between devices, body(): part = lax.psum_scatter(partial, 'z', scatter_dimension=0, tiled=True)  52.1 us
    all_to_all x1, waiting for transfers between devices, body(): gathered = lax.all_to_all(copies, 'rep', 0, 0, tiled=True)  26 us
  transfers between devices with their start and end apart: 9, of which 6 were waited for; matrix products, arithmetic and copies ran while one was open for 0% of the time, Pallas kernels for 14%

profile of v3, /device:TPU:2, one launch (start us, length us, event | category | flops | bytes accessed | tf_op | source)
XLA Modules:
  0.0 363.2 jit_solution(12392826506726383030)
XLA Ops:
  6.5 0.0 copy-start
  6.5 1.3 fusion.10
  7.8 1.5 broadcast_in_dim.8
  9.3 0.0 copy-start.6
  9.3 0.0 copy-start.5
  9.4 6.5 %all-to-all-start = ((bf16[16,256,256]{2,1,0:T(8,128)(2,1)}), bf16[16,256,256]{2,1,0:T(8,128)(2,1)}, u32[]{:S(2)}, u32[]{:S(2)}) async-start(bf16[16,256,256]{2,1,0:T(8,128)(2,1)} %broadcast_in_dim.8), calls=%async_computation | async-start | bytes 4194304 | tf_op jit(solution)/shard_map/all_to_all | solution.py:65
  15.9 0.0 reduce-scatter.9.cloned.1.call-start
  15.9 0.0 copy-done.6
  15.9 0.1 copy.8
  16.0 0.1 reshape_squeeze.2.cols_ref
  16.1 26.0 %all-to-all-done = bf16[16,256,256]{2,1,0:T(8,128)(2,1)} async-done(((bf16[16,256,256]{2,1,0:T(8,128)(2,1)}), bf16[16,256,256]{2,1,0:T(8,128)(2,1)}, u32[]{:S(2)}, u32[]{:S(2)}) %all-to-all-start) | async-done | bytes 2097184 | tf_op jit(solution)/shard_map/all_to_all | solution.py:65
  42.1 0.0 copy-done.5
  42.1 17.9 %shard_map.64 = bf16[4096,256]{1,0:T(8,128)(2,1)S(1)} custom-call(s32[128]{0:T(128)S(1)} %reshape_squeeze.2.cols_ref, s32[32]{0:T(128)S(1)} %bitcast.12, bf16[32,4,128,128]{3,2,1,0:T(8,128)(2,1)} %bitcast.16, bf16[4096,256]{1,0:T(8,128)(2,1)} %bitcast.2.src_ref), custom_call_target="tpu_custom_call" | custom-call | tf_op jit(solution)/shard_map/pallas_call | solution.py:36
  60.0 0.0 copy-start.1
  60.0 1.3 copy-done.1
  61.4 0.0 reduce-scatter.9.cloned.1.call-update
  61.4 0.0 reduce-scatter.13.cloned.1.call-start
  61.4 0.2 broadcast_in_dim.9
  61.6 33.7 %all_to_all.32 = bf16[16,256,256]{2,1,0:T(8,128)(2,1)S(1)} all-to-all(bf16[16,256,256]{2,1,0:T(8,128)(2,1)S(1)} %broadcast_in_dim.9), channel_id=1, replica_groups=mesh['rep'=16,'yh'=2,'z'=8] {'rep'}, dimensions={0} | all-to-all | bytes 4194304 | tf_op jit(solution)/shard_map/all_to_all | solution.py:65
  95.4 17.1 %shard_map.65 = bf16[4096,256]{1,0:T(8,128)(2,1)S(1)} custom-call(s32[128]{0:T(128)S(1)} %reshape_squeeze.2.cols_ref, s32[32]{0:T(128)S(1)} %bitcast.13, bf16[32,4,128,128]{3,2,1,0:T(8,128)(2,1)} %bitcast.17, bf16[4096,256]{1,0:T(8,128)(2,1)S(1)} %bitcast.10), custom_call_target="tpu_custom_call" | custom-call | tf_op jit(solution)/shard_map/pallas_call | solution.py:36
  112.5 0.0 copy-start.2
  112.5 1.3 copy-done.2
  113.8 0.0 reduce-scatter.13.cloned.1.call-update
  113.8 0.0 reduce-scatter.17.cloned.1.call-start
  113.9 0.2 broadcast_in_dim.10
  114.1 34.2 %all_to_all.33 = bf16[16,256,256]{2,1,0:T(8,128)(2,1)S(1)} all-to-all(bf16[16,256,256]{2,1,0:T(8,128)(2,1)S(1)} %broadcast_in_dim.10), channel_id=1, replica_groups=mesh['rep'=16,'yh'=2,'z'=8] {'rep'}, dimensions={0} | all-to-all | bytes 4194304 | tf_op jit(solution)/shard_map/all_to_all | solution.py:65
  148.3 17.1 %shard_map.66 = bf16[4096,256]{1,0:T(8,128)(2,1)S(1)} custom-call(s32[128]{0:T(128)S(1)} %reshape_squeeze.2.cols_ref, s32[32]{0:T(128)S(1)} %bitcast.14, bf16[32,4,128,128]{3,2,1,0:T(8,128)(2,1)} %bitcast.18, bf16[4096,256]{1,0:T(8,128)(2,1)S(1)} %bitcast.11), custom_call_target="tpu_custom_call" | custom-call | tf_op jit(solution)/shard_map/pallas_call | solution.py:36
  165.4 0.0 copy-start.3
  165.4 1.3 copy-done.3
  166.8 0.0 reduce-scatter.17.cloned.1.call-update
  166.8 0.0 reduce-scatter.21.cloned.1.call-start
  166.8 0.2 broadcast_in_dim.11
  167.0 34.2 %all_to_all.34 = bf16[16,256,256]{2,1,0:T(8,128)(2,1)S(1)} all-to-all(bf16[16,256,256]{2,1,0:T(8,128)(2,1)S(1)} %broadcast_in_dim.11), channel_id=1, replica_groups=mesh['rep'=16,'yh'=2,'z'=8] {'rep'}, dimensions={0} | all-to-all | bytes 4194304 | tf_op jit(solution)/shard_map/all_to_all | solution.py:65
  201.3 17.1 %shard_map.67 = bf16[4096,256]{1,0:T(8,128)(2,1)S(1)} custom-call(s32[128]{0:T(128)S(1)} %reshape_squeeze.2.cols_ref, s32[32]{0:T(128)S(1)} %bitcast.15, bf16[32,4,128,128]{3,2,1,0:T(8,128)(2,1)} %bitcast.19, bf16[4096,256]{1,0:T(8,128)(2,1)S(1)} %bitcast.9), custom_call_target="tpu_custom_call" | custom-call | tf_op jit(solution)/shard_map/pallas_call | solution.py:36
  218.4 0.0 copy-start.4
  218.4 1.3 copy-done.4
  219.7 0.0 copy-start.7
  219.7 0.0 reduce-scatter.21.cloned.1.call-update
  219.7 0.0 reduce-scatter.11.cloned.1.call-start
  219.8 0.0 reduce-scatter.9.cloned.1.call-done
  219.8 0.5 reduce-scatter.11.cloned.1.call-update
  220.3 0.0 reduce-scatter.15.cloned.1.call-start
  220.4 0.0 reduce-scatter.13.cloned.1.call-done
  220.4 0.5 reduce-scatter.15.cloned.1.call-update
  220.9 0.0 reduce-scatter.19.cloned.1.call-start
  221.0 0.0 reduce-scatter.17.cloned.1.call-done
  221.0 0.7 reduce-scatter.19.cloned.1.call-update
  221.7 0.0 reduce-scatter.23.cloned.1.call-start
  221.7 52.0 %reduce-scatter.21.cloned.1.call-done = bf16[512,256]{1,0:T(8,128)(2,1)} async-done(((bf16[4096,256]{1,0:T(8,128)(2,1)}), bf16[512,256]{1,0:T(8,128)(2,1)}) %reduce-scatter.21.cloned.1.call-update) | async-done | bytes 262160 | tf_op jit(solution)/shard_map/reduce_scatter | solution.py:67
  273.7 0.0 reduce-scatter.23.cloned.1.call-update
  273.8 0.0 copy-done.7
  273.8 19.2 %reduce-scatter.11.cloned.1.call-done = bf16[256,256]{1,0:T(8,128)(2,1)} async-done(((bf16[512,256]{1,0:T(8,128)(2,1)}), bf16[256,256]{1,0:T(8,128)(2,1)}) %reduce-scatter.11.cloned.1.call-update) | async-done | bytes 131088 | tf_op jit(solution)/shard_map/reduce_scatter | solution.py:68
  293.0 20.2 %reduce-scatter.15.cloned.1.call-done = bf16[256,256]{1,0:T(8,128)(2,1)} async-done(((bf16[512,256]{1,0:T(8,128)(2,1)}), bf16[256,256]{1,0:T(8,128)(2,1)}) %reduce-scatter.15.cloned.1.call-update) | async-done | bytes 131088 | tf_op jit(solution)/shard_map/reduce_scatter | solution.py:68
  313.2 20.3 %reduce-scatter.19.cloned.1.call-done = bf16[256,256]{1,0:T(8,128)(2,1)} async-done(((bf16[512,256]{1,0:T(8,128)(2,1)}), bf16[256,256]{1,0:T(8,128)(2,1)}) %reduce-scatter.19.cloned.1.call-update) | async-done | bytes 131088 | tf_op jit(solution)/shard_map/reduce_scatter | solution.py:68
  333.5 20.3 %reduce-scatter.23.cloned.1.call-done = bf16[256,256]{1,0:T(8,128)(2,1)} async-done(((bf16[512,256]{1,0:T(8,128)(2,1)}), bf16[256,256]{1,0:T(8,128)(2,1)}) %reduce-scatter.23.cloned.1.call-update) | async-done | bytes 131088 | tf_op jit(solution)/shard_map/reduce_scatter | solution.py:68
  353.8 0.0 copy-done
  353.8 2.6 fusion.1
  (1 shorter events, 0.0 us)
Async XLA Ops:
  6.5 347.3 %copy-start = (bf16[1024,1024]{1,0:T(8,128)(2,1)S(1)}, bf16[1024,1024]{1,0:T(8,128)(2,1)}, u32[]{:S(2)}) copy-start(bf16[1024,1024]{1,0:T(8,128)(2,1)} %param.7) | copy-start | bytes 6291460
  9.3 6.6 %copy-start.6 = (s32[1,1,32,4]{2,3,1,0:T(4,128)S(1)}, s32[1,1,32,4]{2,3,1,0:T(4,128)}, u32[]{:S(2)}) copy-start(s32[1,1,32,4]{2,3,1,0:T(4,128)} %param.10) | copy-start | bytes 1540
  9.3 32.8 %copy-start.5 = (s32[1,1,32]{2,1,0:T(1,128)S(1)}, s32[1,1,32]{2,1,0:T(1,128)}, u32[]{:S(2)}) copy-start(s32[1,1,32]{2,1,0:T(1,128)} %param.11) | copy-start | bytes 388
  9.4 32.8 %all-to-all-start = ((bf16[16,256,256]{2,1,0:T(8,128)(2,1)}), bf16[16,256,256]{2,1,0:T(8,128)(2,1)}, u32[]{:S(2)}, u32[]{:S(2)}) async-start(bf16[16,256,256]{2,1,0:T(8,128)(2,1)} %broadcast_in_dim.8), calls=%async_computation | async-start | bytes 4194304 | tf_op jit(solution)/shard_map/all_to_all | solution.py:65
  15.9 203.9 %reduce-scatter.9.cloned.1.call-start = ((), (), s32[]{:S(2)}) async-start(), calls=%async_computation.12 | async-start | bytes 2359296 | tf_op jit(solution)/shard_map/reduce_scatter | solution.py:67
  60.0 1.3 copy-start.1
  61.4 159.0 %reduce-scatter.13.cloned.1.call-start = ((), (), s32[]{:S(2)}) async-start(), calls=%async_computation.14 | async-start | bytes 2359296 | tf_op jit(solution)/shard_map/reduce_scatter | solution.py:67
  112.5 1.3 copy-start.2
  113.8 107.1 %reduce-scatter.17.cloned.1.call-start = ((), (), s32[]{:S(2)}) async-start(), calls=%async_computation.16 | async-start | bytes 2359296 | tf_op jit(solution)/shard_map/reduce_scatter | solution.py:67
  165.4 1.3 copy-start.3
  166.8 107.0 %reduce-scatter.21.cloned.1.call-start = ((), (), s32[]{:S(2)}) async-start(), calls=%async_computation.18 | async-start | bytes 2359296 | tf_op jit(solution)/shard_map/reduce_scatter | solution.py:67
  218.4 1.3 copy-start.4
  219.7 54.1 %copy-start.7 = (bf16[1024]{0:T(1024)(128)(2,1)S(1)}, bf16[1024]{0:T(1024)(128)(2,1)}, u32[]{:S(2)}) copy-start(bf16[1024]{0:T(1024)(128)(2,1)} %param.8) | copy-start | bytes 6148
  219.7 73.3 %reduce-scatter.11.cloned.1.call-start = ((), (), s32[]{:S(2)}) async-start(), calls=%async_computation.13 | async-start | bytes 393216 | tf_op jit(solution)/shard_map/reduce_scatter | solution.py:68
  220.3 92.9 %reduce-scatter.15.cloned.1.call-start = ((), (), s32[]{:S(2)}) async-start(), calls=%async_computation.15 | async-start | bytes 393216 | tf_op jit(solution)/shard_map/reduce_scatter | solution.py:68
  220.9 112.6 %reduce-scatter.19.cloned.1.call-start = ((), (), s32[]{:S(2)}) async-start(), calls=%async_computation.17 | async-start | bytes 393216 | tf_op jit(solution)/shard_map/reduce_scatter | solution.py:68
  221.7 132.1 %reduce-scatter.23.cloned.1.call-start = ((), (), s32[]{:S(2)}) async-start(), calls=%async_computation.19 | async-start | bytes 393216 | tf_op jit(solution)/shard_map/reduce_scatter | solution.py:68
Sparse Core Ops, SparseCore 0:
  61.5 48.7 reduce-scatter.8
  114.0 50.0 reduce-scatter.12
  166.9 52.2 reduce-scatter.16
  221.6 52.1 reduce-scatter.20
  276.1 16.9 reduce-scatter.10
  295.4 17.7 reduce-scatter.14
  315.7 17.7 reduce-scatter.18
  336.0 17.7 reduce-scatter.22

commit v4 on v2

--- a/solution.py
+++ b/solution.py
@@ -55,7 +55,12 @@
     gathered = lax.all_gather(features, "rep", axis=0, tiled=True)
     partial = sparse_partial(gathered, tile_vals[0, 0], tile_col[0, 0], tile_count[0, 0], out_pos)
     summed = lax.psum_scatter(partial, "z", scatter_dimension=0, tiled=True)
-    summed = lax.psum_scatter(summed, "yh", scatter_dimension=0, tiled=True)
+    hi = lax.axis_index("yh")
+    rows = summed.shape[0] // n_hi
+    mine = lax.dynamic_slice_in_dim(summed, hi * rows, rows, axis=0)
+    theirs = lax.dynamic_slice_in_dim(summed, (1 - hi) * rows, rows, axis=0)
+    got = lax.ppermute(theirs, "yh", [(0, 1), (1, 0)])
+    summed = (mine.astype(jnp.float32) + got.astype(jnp.float32)).astype(jnp.bfloat16)
     mixed = jnp.dot(summed, weight, preferred_element_type=jnp.float32) + bias.astype(jnp.float32)
     return jnp.maximum(mixed, 0.0).astype(jnp.bfloat16)
 

time: 229 us -> 217 us (0.948)
  waiting for transfers between devices: 190 us -> 173 us
  starting transfers between devices: 0.08 us -> 3.15 us
    reduce_scatter x1 -> x0, waiting for transfers between devices: 28.1 us -> none  [body(): summed = lax.psum_scatter(summed, 'yh', scatter_dimension=0, tiled=True)]
    ppermute x0 -> x1, waiting for transfers between devices: none -> 12.1 us  [body(): got = lax.ppermute(theirs, 'yh', [(0, 1), (1, 0)])]
    ppermute x0 -> x1, starting transfers between devices: none -> 3.11 us  [body(): got = lax.ppermute(theirs, 'yh', [(0, 1), (1, 0)])]
where the time goes in v4:
time: 217 us; the launch traced here: 216 us
  waiting for transfers between devices  173 us (80%)
  Pallas kernels  18.9 us (9%)
  between operations  13.4 us (6%)
  local copies, waits for them, and re-layouts  4.79 us (2%)
  starting transfers between devices  3.15 us (1%)
  matrix products  2.56 us (1%)
    reduce_scatter x1, waiting for transfers between devices, body(): summed = lax.psum_scatter(partial, 'z', scatter_dimension=0, tiled=True)  102 us
    all_gather x1, waiting for transfers between devices, body(): gathered = lax.all_gather(features, 'rep', axis=0, tiled=True)  58.5 us
    pallas_call x1, Pallas kernels, sparse_partial(): pl.pallas_call(kernel, grid_spec=grid_spec, out_shape=jax.ShapeDtypeStruc...  18.9 us
    ppermute x1, waiting for transfers between devices, body(): got = lax.ppermute(theirs, 'yh', [(0, 1), (1, 0)])  12.1 us
  transfers between devices with their start and end apart: 3, of which 3 were waited for; matrix products, arithmetic and copies ran while one was open for 0% of the time, Pallas kernels for 0%

profile of v4, /device:TPU:2, one launch (start us, length us, event | category | flops | bytes accessed | tf_op | source)
XLA Modules:
  0.0 216.1 jit_solution(3313818261890330464)
XLA Ops:
  6.5 0.0 copy-start
  6.5 0.0 all-gather.2.cloned.1.call-start
  6.5 0.7 all-gather.2.cloned.1.call-update
  7.3 0.0 reduce-scatter.2.cloned.1.call-start
  7.3 0.8 copy.8
  8.1 0.1 reshape_squeeze.3.cols_ref
  8.2 58.5 %all-gather.2.cloned.1.call-done.src_ref = bf16[4096,1024]{1,0:T(8,128)(2,1)} async-done(((bf16[256,1024]{1,0:T(8,128)(2,1)}), bf16[4096,1024]{1,0:T(8,128)(2,1)}) %all-gather.2.cloned.1.call-update) | async-done | bytes 8388624 | tf_op jit(solution)/shard_map/all_gather | solution.py:55
  66.7 0.0 copy-start.1
  66.7 2.2 %copy-done.1 = bf16[1,1,32,4,128,128]{5,4,3,2,1,0:T(8,128)(2,1)S(1)} copy-done((bf16[1,1,32,4,128,128]{5,4,3,2,1,0:T(8,128)(2,1)S(1)}, bf16[1,1,32,4,128,128]{5,4,3,2,1,0:T(8,128)(2,1)}, u32[]{:S(2)}) %copy-start.1) | copy-done | bytes 4194328
  68.8 0.0 copy-start.2
  68.9 0.7 copy-done.2
  69.5 18.9 %shard_map.64 = bf16[4096,1024]{1,0:T(8,128)(2,1)} custom-call(s32[128]{0:T(128)S(1)} %reshape_squeeze.3.cols_ref, s32[32]{0:T(128)S(1)} %bitcast.6, bf16[32,4,128,128]{3,2,1,0:T(8,128)(2,1)S(1)} %bitcast.5, bf16[4096,1024]{1,0:T(8,128)(2,1)} %all-gather.2.cloned.1.call-done.src_ref), custom_call_target="tpu_custom_call" | custom-call | tf_op jit(solution)/shard_map/pallas_call | solution.py:36
  88.4 0.0 copy-start.3
  88.4 0.0 reduce-scatter.2.cloned.1.call-update
  88.4 102.0 %reduce-scatter.2.cloned.1.call-done = bf16[512,1024]{1,0:T(8,128)(2,1)} async-done(((bf16[4096,1024]{1,0:T(8,128)(2,1)}), bf16[512,1024]{1,0:T(8,128)(2,1)}) %reduce-scatter.2.cloned.1.call-update) | async-done | bytes 1048592 | tf_op jit(solution)/shard_map/reduce_scatter | solution.py:57
  190.4 1.1 constant_dynamic-slice_fusion
  191.5 3.1 %collective-permute-start = (bf16[256,1024]{1,0:T(8,128)(2,1)S(1)}, bf16[256,1024]{1,0:T(8,128)(2,1)S(1)}, u32[]{:S(2)}, u32[]{:S(2)}) collective-permute-start(bf16[256,1024]{1,0:T(8,128)(2,1)S(1)} %constant_dynamic-slice_fusion), channel_id=1, source_target_pairs={{0,8},{8,0},{1,9},{9,1},{2,10},{10,2},{3,11},{11,3},{4,12},{12,4},... | collective-permute-start | bytes 1572872 | tf_op jit(solution)/shard_map/ppermute | solution.py:62
  194.6 0.0 copy-done.3
  194.6 12.1 %collective-permute-done = bf16[256,1024]{1,0:T(8,128)(2,1)S(1)} collective-permute-done((bf16[256,1024]{1,0:T(8,128)(2,1)S(1)}, bf16[256,1024]{1,0:T(8,128)(2,1)S(1)}, u32[]{:S(2)}, u32[]{:S(2)}) %collective-permute-start) | collective-permute-done | bytes 524320 | tf_op jit(solution)/shard_map/ppermute | solution.py:62
  206.7 0.0 copy-done
  206.7 2.6 %fusion.1 = bf16[256,1024]{1,0:T(8,128)(2,1)} fusion(bf16[1024,1024]{1,0:T(8,128)(2,1)S(1)} %copy-done, bf16[256,1024]{1,0:T(8,128)(2,1)S(1)} %collective-permute-done, f32[1024]{0:T(1024)S(1)} %convert_element_type.18, bf16[512,1024]{1,0:T(8,128)(2,1)} %reduce-scatter.2.cloned.1.call-done, s32[]{:T(128)S(6)} %select_n.6), kind=kOutput, calls=%fused_computation.2 | convolution fusion | flops 538705920 | bytes 3674116 | tf_op jit(solution)/shard_map/dot_general | solution.py:64
  (1 shorter events, 0.0 us)
Async XLA Ops:
  6.5 200.1 %copy-start = (bf16[1024,1024]{1,0:T(8,128)(2,1)S(1)}, bf16[1024,1024]{1,0:T(8,128)(2,1)}, u32[]{:S(2)}) copy-start(bf16[1024,1024]{1,0:T(8,128)(2,1)} %param.7) | copy-start | bytes 6291460
  6.5 60.1 %all-gather.2.cloned.1.call-start = ((), (), s32[]{:S(2)}) async-start(), calls=%async_computation.1 | async-start | bytes 8912896 | tf_op jit(solution)/shard_map/all_gather | solution.py:55
  7.3 183.1 %reduce-scatter.2.cloned.1.call-start = ((), (), s32[]{:S(2)}) async-start(), calls=%async_computation.2 | async-start | bytes 9437184 | tf_op jit(solution)/shard_map/reduce_scatter | solution.py:57
  66.7 2.2 %copy-start.1 = (bf16[1,1,32,4,128,128]{5,4,3,2,1,0:T(8,128)(2,1)S(1)}, bf16[1,1,32,4,128,128]{5,4,3,2,1,0:T(8,128)(2,1)}, u32[]{:S(2)}) copy-start(bf16[1,1,32,4,128,128]{5,4,3,2,1,0:T(8,128)(2,1)} %param.9) | copy-start | bytes 12582916
  68.8 0.7 copy-start.2
  88.4 106.2 %copy-start.3 = (bf16[1024]{0:T(1024)(128)(2,1)S(1)}, bf16[1024]{0:T(1024)(128)(2,1)}, u32[]{:S(2)}) copy-start(bf16[1024]{0:T(1024)(128)(2,1)} %param.8) | copy-start | bytes 6148
  191.5 15.2 %collective-permute-start = (bf16[256,1024]{1,0:T(8,128)(2,1)S(1)}, bf16[256,1024]{1,0:T(8,128)(2,1)S(1)}, u32[]{:S(2)}, u32[]{:S(2)}) collective-permute-start(bf16[256,1024]{1,0:T(8,128)(2,1)S(1)} %constant_dynamic-slice_fusion), channel_id=1, source_target_pairs={{0,8},{8,0},{1,9},{9,1},{2,10},{10,2},{3,11},{11,3},{4,12},{12,4},... | collective-permute-start | bytes 1572872 | tf_op jit(solution)/shard_map/ppermute | solution.py:62
Sparse Core Ops, SparseCore 0:
  9.2 57.4 all-gather.1
  88.5 101.8 reduce-scatter.1

commit v5 on v2

--- a/solution.py
+++ b/solution.py
@@ -6,13 +6,13 @@
 from jax.sharding import Mesh, PartitionSpec as P
 
 
-def sparse_partial(gathered, tiles, cols, counts, out_pos):
+def sparse_partial(gathered, tiles, cols, counts, n_steps, block_of, out_pos):
     n_blocks, slots, side, _ = tiles.shape
     width = gathered.shape[1]
     n_src = gathered.shape[0]
 
     def kernel(cols_ref, counts_ref, tile_ref, src_ref, out_ref, acc_ref):
-        b = pl.program_id(0)
+        b = block_of(pl.program_id(0))
         live = counts_ref[b]
         acc_ref[...] = jnp.zeros_like(acc_ref)
         for k in range(slots):
@@ -25,9 +25,9 @@
 
     grid_spec = pltpu.PrefetchScalarGridSpec(
         num_scalar_prefetch=2,
-        grid=(n_blocks,),
+        grid=(n_steps,),
         in_specs=[
-            pl.BlockSpec((1, slots, side, side), lambda b, c, n: (b, 0, 0, 0)),
+            pl.BlockSpec((1, slots, side, side), lambda i, c, n: (block_of(i), 0, 0, 0)),
             pl.BlockSpec((n_src, width), lambda b, c, n: (0, 0)),
         ],
         out_specs=pl.BlockSpec((side, width), lambda b, c, n: (out_pos(b), 0)),
@@ -36,7 +36,7 @@
     return pl.pallas_call(
         kernel,
         grid_spec=grid_spec,
-        out_shape=jax.ShapeDtypeStruct((n_blocks * side, width), jnp.bfloat16),
+        out_shape=jax.ShapeDtypeStruct((n_steps * side, width), jnp.bfloat16),
         compiler_params=pltpu.CompilerParams(
             dimension_semantics=("arbitrary",), vmem_limit_bytes=48 * 1024 * 1024
         ),
@@ -46,16 +46,29 @@
 def body(features, weight, bias, tile_vals, tile_col, tile_count):
     n_hi = lax.axis_size("yh")
     n_lo = lax.axis_size("z")
-    per_dev = features.shape[0] // tile_vals.shape[-1]
-
-    def out_pos(b):
-        j = b // per_dev
-        return ((j % n_lo) * n_hi + j // n_lo) * per_dev + b % per_dev
+    side = tile_vals.shape[-1]
+    per_dev = features.shape[0] // side
+    n_dest = n_hi * n_lo
+    hi = lax.axis_index("yh")
 
     gathered = lax.all_gather(features, "rep", axis=0, tiled=True)
-    partial = sparse_partial(gathered, tile_vals[0, 0], tile_col[0, 0], tile_count[0, 0], out_pos)
-    summed = lax.psum_scatter(partial, "z", scatter_dimension=0, tiled=True)
-    summed = lax.psum_scatter(summed, "yh", scatter_dimension=0, tiled=True)
+    outs = []
+    for sub in range(per_dev):
+        def block_of(i, sub=sub):
+            return i * per_dev + sub
+
+        def out_pos(i):
+            return (i % n_lo) * n_hi + i // n_lo
+
+        partial = sparse_partial(
+            gathered, tile_vals[0, 0], tile_col[0, 0], tile_count[0, 0], n_dest, block_of, out_pos
+        )
+        part = lax.psum_scatter(partial, "z", scatter_dimension=0, tiled=True)
+        mine = lax.dynamic_slice_in_dim(part, hi * side, side, axis=0)
+        theirs = lax.dynamic_slice_in_dim(part, (1 - hi) * side, side, axis=0)
+        got = lax.ppermute(theirs, "yh", [(0, 1), (1, 0)])
+        outs.append((mine.astype(jnp.float32) + got.astype(jnp.float32)).astype(jnp.bfloat16))
+    summed = jnp.concatenate(outs, axis=0)
     mixed = jnp.dot(summed, weight, preferred_element_type=jnp.float32) + bias.astype(jnp.float32)
     return jnp.maximum(mixed, 0.0).astype(jnp.bfloat16)
 

time: 229 us -> 217 us (0.948)
  waiting for transfers between devices: 190 us -> 161 us
  Pallas kernels: 18.6 us -> 25.2 us
  starting transfers between devices: 0.08 us -> 6.3 us
  local copies, waits for them, and re-layouts: 3.72 us -> 7.95 us
    reduce_scatter x2, waiting for transfers between devices: 130 us -> 96.2 us  [body(): part = lax.psum_scatter(partial, 'z', scatter_dimension=0, tiled=True)]
    pallas_call x1 -> x2, Pallas kernels: 18.6 us -> 25.2 us  [sparse_partial(): pl.pallas_call(kernel, grid_spec=grid_spec, out_shape=jax.ShapeDtypeStruc...]
    ppermute x0 -> x2, starting transfers between devices: none -> 6.22 us  [body(): got = lax.ppermute(theirs, 'yh', [(0, 1), (1, 0)])]
    ppermute x0 -> x2, waiting for transfers between devices: none -> 5.47 us  [body(): got = lax.ppermute(theirs, 'yh', [(0, 1), (1, 0)])]
    unnamed x9 -> x13, local copies, waits for them, and re-layouts: 3.61 us -> 5.91 us
  transfers between devices with their start and end apart: 3 -> 5, of which waited for: 3 -> 4; matrix products, arithmetic and copies ran while one was open for 0% -> 2% of each run, Pallas kernels for 0% -> 6%
where the time goes in v5:
time: 217 us
  waiting for transfers between devices  161 us (74%)
  Pallas kernels  25.2 us (12%)
  between operations  13.2 us (6%)
  local copies, waits for them, and re-layouts  7.95 us (4%)
  starting transfers between devices  6.3 us (3%)
    reduce_scatter x2, waiting for transfers between devices, body(): part = lax.psum_scatter(partial, 'z', scatter_dimension=0, tiled=True)  96.2 us
    all_gather x1, waiting for transfers between devices, body(): gathered = lax.all_gather(features, 'rep', axis=0, tiled=True)  58.5 us
    pallas_call x2, Pallas kernels, sparse_partial(): pl.pallas_call(kernel, grid_spec=grid_spec, out_shape=jax.ShapeDtypeStruc...  25.2 us
    ppermute x2, starting transfers between devices, body(): got = lax.ppermute(theirs, 'yh', [(0, 1), (1, 0)])  6.22 us
    unnamed x13, local copies, waits for them, and re-layouts  5.91 us
    ppermute x2, waiting for transfers between devices, body(): got = lax.ppermute(theirs, 'yh', [(0, 1), (1, 0)])  5.47 us
  transfers between devices with their start and end apart: 5, of which 4 were waited for; matrix products, arithmetic and copies ran while one was open for 2% of the time, Pallas kernels for 6%

profile of v5, /device:TPU:2, one launch (start us, length us, event | category | flops | bytes accessed | tf_op | source)
XLA Modules:
  0.0 217.0 jit_solution(3400781822969158965)
XLA Ops:
  6.5 0.0 copy-start
  6.5 0.0 all-gather.2.cloned.1.call-start
  6.5 0.7 all-gather.2.cloned.1.call-update
  7.3 0.0 reduce-scatter.5.cloned.1.call-start
  7.3 0.8 copy.8
  8.1 0.1 reshape_squeeze.4.cols_ref
  8.2 58.5 %all-gather.2.cloned.1.call-done.src_ref = bf16[4096,1024]{1,0:T(8,128)(2,1)} async-done(((bf16[256,1024]{1,0:T(8,128)(2,1)}), bf16[4096,1024]{1,0:T(8,128)(2,1)}) %all-gather.2.cloned.1.call-update) | async-done | bytes 8388624 | tf_op jit(solution)/shard_map/all_gather | solution.py:54
  66.7 0.0 copy-start.3
  66.7 0.7 copy-done.3
  67.3 12.6 %shard_map.65 = bf16[2048,1024]{1,0:T(8,128)(2,1)S(1)} custom-call(s32[128]{0:T(128)S(1)} %reshape_squeeze.4.cols_ref, s32[32]{0:T(128)S(1)} %bitcast.5, bf16[32,4,128,128]{3,2,1,0:T(8,128)(2,1)} %bitcast.7, bf16[4096,1024]{1,0:T(8,128)(2,1)} %all-gather.2.cloned.1.call-done.src_ref), custom_call_target="tpu_custom_call" | custom-call | tf_op jit(solution)/shard_map/pallas_call | solution.py:36
  79.9 0.0 copy-start.1
  79.9 2.0 copy-done.1
  81.9 0.0 copy-start.4
  81.9 0.0 reduce-scatter.5.cloned.1.call-update
  81.9 0.0 reduce-scatter.3.cloned.1.call-start
  81.9 0.6 copy-done.4
  82.5 12.6 %shard_map.64 = bf16[2048,1024]{1,0:T(8,128)(2,1)S(1)} custom-call(s32[128]{0:T(128)S(1)} %reshape_squeeze.4.cols_ref, s32[32]{0:T(128)S(1)} %bitcast.6, bf16[32,4,128,128]{3,2,1,0:T(8,128)(2,1)} %bitcast.8, bf16[4096,1024]{1,0:T(8,128)(2,1)} %all-gather.2.cloned.1.call-done.src_ref), custom_call_target="tpu_custom_call" | custom-call | tf_op jit(solution)/shard_map/pallas_call | solution.py:36
  95.1 0.0 copy-start.2
  95.1 1.9 copy-done.2
  97.1 0.0 copy-start.5
  97.1 0.0 reduce-scatter.3.cloned.1.call-update
  97.1 43.7 %reduce-scatter.5.cloned.1.call-done = bf16[256,1024]{1,0:T(8,128)(2,1)} async-done(((bf16[2048,1024]{1,0:T(8,128)(2,1)}), bf16[256,1024]{1,0:T(8,128)(2,1)}) %reduce-scatter.5.cloned.1.call-update) | async-done | bytes 524304 | tf_op jit(solution)/shard_map/reduce_scatter | solution.py:66
  140.8 1.0 constant_dynamic-slice_fusion
  141.8 3.1 %collective-permute-start.1 = (bf16[128,1024]{1,0:T(8,128)(2,1)S(1)}, bf16[128,1024]{1,0:T(8,128)(2,1)S(1)}, u32[]{:S(2)}, u32[]{:S(2)}) collective-permute-start(bf16[128,1024]{1,0:T(8,128)(2,1)S(1)} %constant_dynamic-slice_fusion), channel_id=1, source_target_pairs={{0,8},{8,0},{1,9},{9,1},{2,10},{10,2},{3,11},{11,3},{4,12},{12,4},... | collective-permute-start | bytes 786440 | tf_op jit(solution)/shard_map/ppermute | solution.py:69
  144.9 52.5 %reduce-scatter.3.cloned.1.call-done = bf16[256,1024]{1,0:T(8,128)(2,1)} async-done(((bf16[2048,1024]{1,0:T(8,128)(2,1)}), bf16[256,1024]{1,0:T(8,128)(2,1)}) %reduce-scatter.3.cloned.1.call-update) | async-done | bytes 524304 | tf_op jit(solution)/shard_map/reduce_scatter | solution.py:66
  197.4 1.0 constant_dynamic-slice_fusion.1
  198.4 3.1 %collective-permute-start = (bf16[128,1024]{1,0:T(8,128)(2,1)S(1)}, bf16[128,1024]{1,0:T(8,128)(2,1)S(1)}, u32[]{:S(2)}, u32[]{:S(2)}) collective-permute-start(bf16[128,1024]{1,0:T(8,128)(2,1)S(1)} %constant_dynamic-slice_fusion.1), channel_id=1, source_target_pairs={{0,8},{8,0},{1,9},{9,1},{2,10},{10,2},{3,11},{11,3},{4,12},{12,4},... | collective-permute-start | bytes 786440 | tf_op jit(solution)/shard_map/ppermute | solution.py:69
  201.4 0.0 copy-done.5
  201.5 0.0 collective-permute-done.1
  201.5 1.0 add_convert_fusion
  202.5 5.5 %collective-permute-done = bf16[128,1024]{1,0:T(8,128)(2,1)S(1)} collective-permute-done((bf16[128,1024]{1,0:T(8,128)(2,1)S(1)}, bf16[128,1024]{1,0:T(8,128)(2,1)S(1)}, u32[]{:S(2)}, u32[]{:S(2)}) %collective-permute-start) | collective-permute-done | bytes 262176 | tf_op jit(solution)/shard_map/ppermute | solution.py:69
  208.0 1.0 add_convert_fusion.1
  209.0 0.0 copy-done
  209.0 1.5 fusion.1
  (1 shorter events, 0.0 us)
Async XLA Ops:
  6.5 202.4 %copy-start = (bf16[1024,1024]{1,0:T(8,128)(2,1)S(1)}, bf16[1024,1024]{1,0:T(8,128)(2,1)}, u32[]{:S(2)}) copy-start(bf16[1024,1024]{1,0:T(8,128)(2,1)} %param.7) | copy-start | bytes 6291460
  6.5 60.1 %all-gather.2.cloned.1.call-start = ((), (), s32[]{:S(2)}) async-start(), calls=%async_computation.2 | async-start | bytes 8912896 | tf_op jit(solution)/shard_map/all_gather | solution.py:54
  7.3 133.6 %reduce-scatter.5.cloned.1.call-start = ((), (), s32[]{:S(2)}) async-start(), calls=%async_computation.4 | async-start | bytes 4718592 | tf_op jit(solution)/shard_map/reduce_scatter | solution.py:66
  66.7 0.7 copy-start.3
  79.9 2.0 copy-start.1
  81.9 0.7 copy-start.4
  81.9 115.5 %reduce-scatter.3.cloned.1.call-start = ((), (), s32[]{:S(2)}) async-start(), calls=%async_computation.3 | async-start | bytes 4718592 | tf_op jit(solution)/shard_map/reduce_scatter | solution.py:66
  95.1 2.0 copy-start.2
  97.1 104.4 %copy-start.5 = (bf16[1024]{0:T(1024)(128)(2,1)S(1)}, bf16[1024]{0:T(1024)(128)(2,1)}, u32[]{:S(2)}) copy-start(bf16[1024]{0:T(1024)(128)(2,1)} %param.8) | copy-start | bytes 6148
  141.8 59.7 %collective-permute-start.1 = (bf16[128,1024]{1,0:T(8,128)(2,1)S(1)}, bf16[128,1024]{1,0:T(8,128)(2,1)S(1)}, u32[]{:S(2)}, u32[]{:S(2)}) collective-permute-start(bf16[128,1024]{1,0:T(8,128)(2,1)S(1)} %constant_dynamic-slice_fusion), channel_id=1, source_target_pairs={{0,8},{8,0},{1,9},{9,1},{2,10},{10,2},{3,11},{11,3},{4,12},{12,4},... | collective-permute-start | bytes 786440 | tf_op jit(solution)/shard_map/ppermute | solution.py:69
  198.4 9.6 %collective-permute-start = (bf16[128,1024]{1,0:T(8,128)(2,1)S(1)}, bf16[128,1024]{1,0:T(8,128)(2,1)S(1)}, u32[]{:S(2)}, u32[]{:S(2)}) collective-permute-start(bf16[128,1024]{1,0:T(8,128)(2,1)S(1)} %constant_dynamic-slice_fusion.1), channel_id=1, source_target_pairs={{0,8},{8,0},{1,9},{9,1},{2,10},{10,2},{3,11},{11,3},{4,12},{12,4},... | collective-permute-start | bytes 786440 | tf_op jit(solution)/shard_map/ppermute | solution.py:69
Sparse Core Ops, SparseCore 0:
  9.2 57.4 all-gather.1
  82.0 58.7 reduce-scatter.4
  143.4 53.9 reduce-scatter.2

commit v6 on v4

--- a/solution.py
+++ b/solution.py
@@ -6,7 +6,7 @@
 from jax.sharding import Mesh, PartitionSpec as P
 
 
-def sparse_partial(gathered, tiles, cols, counts, out_pos):
+def sparse_partial(gathered, tiles, cols, counts, out_pos, src_pos):
     n_blocks, slots, side, _ = tiles.shape
     width = gathered.shape[1]
     n_src = gathered.shape[0]
@@ -18,7 +18,7 @@
         for k in range(slots):
             @pl.when(k < live)
             def _():
-                start = pl.multiple_of(cols_ref[b * slots + k] * side, side)
+                start = pl.multiple_of(src_pos(cols_ref[b * slots + k]) * side, side)
                 src = src_ref[pl.ds(start, side), :]
                 acc_ref[...] += jnp.dot(tile_ref[0, k], src, preferred_element_type=jnp.float32)
         out_ref[...] = acc_ref[...].astype(out_ref.dtype)
@@ -52,8 +52,16 @@
         j = b // per_dev
         return ((j % n_lo) * n_hi + j // n_lo) * per_dev + b % per_dev
 
-    gathered = lax.all_gather(features, "rep", axis=0, tiled=True)
-    partial = sparse_partial(gathered, tile_vals[0, 0], tile_col[0, 0], tile_count[0, 0], out_pos)
+    n_xy = lax.axis_size("rxy")
+    n_core = lax.axis_size("core")
+
+    def src_pos(c):
+        r = c // per_dev
+        return ((r % n_core) * n_xy + r // n_core) * per_dev + c % per_dev
+
+    gathered = lax.all_gather(features, "rxy", axis=0, tiled=True)
+    gathered = lax.all_gather(gathered, "core", axis=0, tiled=True)
+    partial = sparse_partial(gathered, tile_vals[0, 0], tile_col[0, 0], tile_count[0, 0], out_pos, src_pos)
     summed = lax.psum_scatter(partial, "z", scatter_dimension=0, tiled=True)
     hi = lax.axis_index("yh")
     rows = summed.shape[0] // n_hi
@@ -68,19 +76,23 @@
 def solution(mesh):
     n_rep, n_blk = mesh.devices.shape
     n_hi = 2
-    split = Mesh(mesh.devices.reshape(n_rep, n_hi, n_blk // n_hi), ("rep", "yh", "z"))
+    n_core = 2
+    split = Mesh(
+        mesh.devices.reshape(n_rep // n_core, n_core, n_hi, n_blk // n_hi), ("rxy", "core", "yh", "z")
+    )
+    rep = ("rxy", "core")
     blk = ("yh", "z")
     return jax.shard_map(
         body,
         mesh=split,
         in_specs=(
-            P(("rep",) + blk, None),
+            P(rep + blk, None),
             P(),
             P(),
-            P("rep", blk, None, None, None, None),
-            P("rep", blk, None, None),
-            P("rep", blk, None),
+            P(rep, blk, None, None, None, None),
+            P(rep, blk, None, None),
+            P(rep, blk, None),
         ),
-        out_specs=P(("rep",) + blk, None),
+        out_specs=P(rep + blk, None),
         check_vma=False,
     )

time: 217 us -> 283 us (1.30)
  waiting for transfers between devices: 173 us -> 240 us
    all_gather x1 -> x2, waiting for transfers between devices: 58.5 us -> 125 us  [the longest x1 97 us: body(): gathered = lax.all_gather(features, 'rxy', axis=0, tiled=True)]
  transfers between devices with their start and end apart: 3 -> 4, of which waited for: 3 -> 4; matrix products, arithmetic and copies ran while one was open for 0% -> 0% of each run, Pallas kernels for 0% -> 0%
where the time goes in v6:
time: 283 us; the launch traced here: 282 us
  waiting for transfers between devices  240 us (85%)
  Pallas kernels  19.1 us (7%)
  between operations  13.1 us (5%)
  local copies, waits for them, and re-layouts  3.47 us (1%)
  starting transfers between devices  3.18 us (1%)
    reduce_scatter x1, waiting for transfers between devices, body(): summed = lax.psum_scatter(partial, 'z', scatter_dimension=0, tiled=True)  103 us
    all_gather x1, waiting for transfers between devices, body(): gathered = lax.all_gather(features, 'rxy', axis=0, tiled=True)  97 us
    all_gather x1, waiting for transfers between devices, body(): gathered = lax.all_gather(gathered, 'core', axis=0, tiled=True)  27.7 us
    pallas_call x1, Pallas kernels, sparse_partial(): pl.pallas_call(kernel, grid_spec=grid_spec, out_shape=jax.ShapeDtypeStruc...  19.1 us
    ppermute x1, waiting for transfers between devices, body(): got = lax.ppermute(theirs, 'yh', [(0, 1), (1, 0)])  12.1 us
  transfers between devices with their start and end apart: 4, of which 4 were waited for; matrix products, arithmetic and copies ran while one was open for 0% of the time, Pallas kernels for 0%

profile of v6, /device:TPU:2, one launch (start us, length us, event | category | flops | bytes accessed | tf_op | source)
XLA Modules:
  0.0 281.6 jit_solution(15347596324430382400)
XLA Ops:
  6.5 0.0 copy-start
  6.5 0.0 copy-start.3
  6.5 0.0 copy-start.2
  6.5 0.0 all-gather.3.cloned.1.call-start
  6.5 0.7 all-gather.3.cloned.1.call-update
  7.3 0.0 all-gather.5.cloned.1.call-start
  7.3 97.0 %all-gather.3.cloned.1.call-done = bf16[2048,1024]{1,0:T(8,128)(2,1)} async-done(((bf16[256,1024]{1,0:T(8,128)(2,1)}), bf16[2048,1024]{1,0:T(8,128)(2,1)}) %all-gather.3.cloned.1.call-update) | async-done | bytes 4194320 | tf_op jit(solution)/shard_map/all_gather | solution.py:62
  104.3 0.0 all-gather.5.cloned.1.call-update
  104.3 0.0 reduce-scatter.2.cloned.1.call-start
  104.4 0.0 copy-done.3
  104.4 0.1 copy.8
  104.5 0.1 reshape_squeeze.3.cols_ref
  104.6 27.7 %all-gather.5.cloned.1.call-done.src_ref = bf16[4096,1024]{1,0:T(8,128)(2,1)} async-done(((bf16[2048,1024]{1,0:T(8,128)(2,1)}), bf16[4096,1024]{1,0:T(8,128)(2,1)}) %all-gather.5.cloned.1.call-update) | async-done | bytes 8388624 | tf_op jit(solution)/shard_map/all_gather | solution.py:63
  132.3 0.0 copy-done.2
  132.3 0.0 copy-start.1
  132.3 2.2 copy-done.1
  134.5 19.1 %shard_map.64 = bf16[4096,1024]{1,0:T(8,128)(2,1)} custom-call(s32[128]{0:T(128)S(1)} %reshape_squeeze.3.cols_ref, s32[32]{0:T(128)S(1)} %bitcast.6, bf16[32,4,128,128]{3,2,1,0:T(8,128)(2,1)S(1)} %bitcast.5, bf16[4096,1024]{1,0:T(8,128)(2,1)} %all-gather.5.cloned.1.call-done.src_ref), custom_call_target="tpu_custom_call" | custom-call | tf_op jit(solution)/shard_map/pallas_call | solution.py:36
  153.6 0.0 copy-start.4
  153.6 0.0 reduce-scatter.2.cloned.1.call-update
  153.7 102.6 %reduce-scatter.2.cloned.1.call-done = bf16[512,1024]{1,0:T(8,128)(2,1)} async-done(((bf16[4096,1024]{1,0:T(8,128)(2,1)}), bf16[512,1024]{1,0:T(8,128)(2,1)}) %reduce-scatter.2.cloned.1.call-update) | async-done | bytes 1048592 | tf_op jit(solution)/shard_map/reduce_scatter | solution.py:65
  256.3 1.1 constant_dynamic-slice_fusion
  257.4 3.1 %collective-permute-start = (bf16[256,1024]{1,0:T(8,128)(2,1)S(1)}, bf16[256,1024]{1,0:T(8,128)(2,1)S(1)}, u32[]{:S(2)}, u32[]{:S(2)}) collective-permute-start(bf16[256,1024]{1,0:T(8,128)(2,1)S(1)} %constant_dynamic-slice_fusion), channel_id=1, source_target_pairs={{0,8},{8,0},{1,9},{9,1},{2,10},{10,2},{3,11},{11,3},{4,12},{12,4},... | collective-permute-start | bytes 1572872 | tf_op jit(solution)/shard_map/ppermute | solution.py:70
  260.5 0.0 copy-done.4
  260.5 12.1 %collective-permute-done = bf16[256,1024]{1,0:T(8,128)(2,1)S(1)} collective-permute-done((bf16[256,1024]{1,0:T(8,128)(2,1)S(1)}, bf16[256,1024]{1,0:T(8,128)(2,1)S(1)}, u32[]{:S(2)}, u32[]{:S(2)}) %collective-permute-start) | collective-permute-done | bytes 524320 | tf_op jit(solution)/shard_map/ppermute | solution.py:70
  272.6 0.0 copy-done
  272.6 2.6 fusion.1
  (1 shorter events, 0.0 us)
Async XLA Ops:
  6.5 266.0 %copy-start = (bf16[1024,1024]{1,0:T(8,128)(2,1)S(1)}, bf16[1024,1024]{1,0:T(8,128)(2,1)}, u32[]{:S(2)}) copy-start(bf16[1024,1024]{1,0:T(8,128)(2,1)} %param.7) | copy-start | bytes 6291460
  6.5 97.8 %copy-start.3 = (s32[1,1,32,4]{2,3,1,0:T(4,128)S(1)}, s32[1,1,32,4]{2,3,1,0:T(4,128)}, u32[]{:S(2)}) copy-start(s32[1,1,32,4]{2,3,1,0:T(4,128)} %param.10) | copy-start | bytes 1540
  6.5 125.8 %copy-start.2 = (s32[1,1,32]{2,1,0:T(1,128)S(1)}, s32[1,1,32]{2,1,0:T(1,128)}, u32[]{:S(2)}) copy-start(s32[1,1,32]{2,1,0:T(1,128)} %param.11) | copy-start | bytes 388
  6.5 97.8 %all-gather.3.cloned.1.call-start = ((), (), s32[]{:S(2)}) async-start(), calls=%async_computation.1 | async-start | bytes 4718592 | tf_op jit(solution)/shard_map/all_gather | solution.py:62
  7.3 125.1 %all-gather.5.cloned.1.call-start = ((), (), s32[]{:S(2)}) async-start(), calls=%async_computation.2 | async-start | bytes 12582912 | tf_op jit(solution)/shard_map/all_gather | solution.py:63
  104.3 151.9 %reduce-scatter.2.cloned.1.call-start = ((), (), s32[]{:S(2)}) async-start(), calls=%async_computation.3 | async-start | bytes 9437184 | tf_op jit(solution)/shard_map/reduce_scatter | solution.py:65
  132.3 2.2 copy-start.1
  153.6 106.8 %copy-start.4 = (bf16[1024]{0:T(1024)(128)(2,1)S(1)}, bf16[1024]{0:T(1024)(128)(2,1)}, u32[]{:S(2)}) copy-start(bf16[1024]{0:T(1024)(128)(2,1)} %param.8) | copy-start | bytes 6148
  257.4 15.2 %collective-permute-start = (bf16[256,1024]{1,0:T(8,128)(2,1)S(1)}, bf16[256,1024]{1,0:T(8,128)(2,1)S(1)}, u32[]{:S(2)}, u32[]{:S(2)}) collective-permute-start(bf16[256,1024]{1,0:T(8,128)(2,1)S(1)} %constant_dynamic-slice_fusion), channel_id=1, source_target_pairs={{0,8},{8,0},{1,9},{9,1},{2,10},{10,2},{3,11},{11,3},{4,12},{12,4},... | collective-permute-start | bytes 1572872 | tf_op jit(solution)/shard_map/ppermute | solution.py:70
Sparse Core Ops, SparseCore 0:
  9.1 95.1 all-gather.2
  106.1 26.1 all-gather.4
  153.8 102.4 reduce-scatter.1

commit v7 on v4

--- a/solution.py
+++ b/solution.py
@@ -6,32 +6,39 @@
 from jax.sharding import Mesh, PartitionSpec as P
 
 
-def sparse_partial(gathered, tiles, cols, counts, out_pos):
+def sparse_partial(gathered, tiles, cols, counts, out_pos, group=2):
     n_blocks, slots, side, _ = tiles.shape
     width = gathered.shape[1]
     n_src = gathered.shape[0]
 
-    def kernel(cols_ref, counts_ref, tile_ref, src_ref, out_ref, acc_ref):
-        b = pl.program_id(0)
-        live = counts_ref[b]
-        acc_ref[...] = jnp.zeros_like(acc_ref)
-        for k in range(slots):
-            @pl.when(k < live)
-            def _():
-                start = pl.multiple_of(cols_ref[b * slots + k] * side, side)
-                src = src_ref[pl.ds(start, side), :]
-                acc_ref[...] += jnp.dot(tile_ref[0, k], src, preferred_element_type=jnp.float32)
-        out_ref[...] = acc_ref[...].astype(out_ref.dtype)
+    def kernel(cols_ref, counts_ref, tile_ref, src_ref, out_ref):
+        step = pl.program_id(0)
+        for g in range(group):
+            b = step * group + g
+            live = counts_ref[b]
+            lhs = jnp.concatenate(
+                [jnp.where(k < live, tile_ref[g, k], jnp.zeros_like(tile_ref[g, k])) for k in range(slots)],
+                axis=1,
+            )
+            rhs = jnp.concatenate(
+                [
+                    src_ref[pl.ds(pl.multiple_of(cols_ref[b * slots + k] * side, side), side), :]
+                    for k in range(slots)
+                ],
+                axis=0,
+            )
+            out_ref[pl.ds(g * side, side), :] = jnp.dot(
+                lhs, rhs, preferred_element_type=jnp.float32
+            ).astype(out_ref.dtype)
 
     grid_spec = pltpu.PrefetchScalarGridSpec(
         num_scalar_prefetch=2,
-        grid=(n_blocks,),
+        grid=(n_blocks // group,),
         in_specs=[
-            pl.BlockSpec((1, slots, side, side), lambda b, c, n: (b, 0, 0, 0)),
-            pl.BlockSpec((n_src, width), lambda b, c, n: (0, 0)),
+            pl.BlockSpec((group, slots, side, side), lambda i, c, n: (i, 0, 0, 0)),
+            pl.BlockSpec((n_src, width), lambda i, c, n: (0, 0)),
         ],
-        out_specs=pl.BlockSpec((side, width), lambda b, c, n: (out_pos(b), 0)),
-        scratch_shapes=[pltpu.VMEM((side, width), jnp.float32)],
+        out_specs=pl.BlockSpec((group * side, width), lambda i, c, n: (out_pos(i * group) // group, 0)),
     )
     return pl.pallas_call(
         kernel,
@@ -53,7 +60,7 @@
         return ((j % n_lo) * n_hi + j // n_lo) * per_dev + b % per_dev
 
     gathered = lax.all_gather(features, "rep", axis=0, tiled=True)
-    partial = sparse_partial(gathered, tile_vals[0, 0], tile_col[0, 0], tile_count[0, 0], out_pos)
+    partial = sparse_partial(gathered, tile_vals[0, 0], tile_col[0, 0], tile_count[0, 0], out_pos, per_dev)
     summed = lax.psum_scatter(partial, "z", scatter_dimension=0, tiled=True)
     hi = lax.axis_index("yh")
     rows = summed.shape[0] // n_hi

time: 217 us -> 206 us (0.949)
  waiting for transfers between devices: 173 us -> 167 us
  Pallas kernels: 18.9 us -> 14.6 us
    reduce_scatter x1, waiting for transfers between devices: 102 us -> 96.1 us  [body(): summed = lax.psum_scatter(partial, 'z', scatter_dimension=0, tiled=True)]
    pallas_call x1, Pallas kernels: 18.9 us -> 14.6 us  [sparse_partial(): pl.pallas_call(kernel, grid_spec=grid_spec, out_shape=jax.ShapeDtypeStruc...]
where the time goes in v7:
time: 206 us
  waiting for transfers between devices  167 us (81%)
  Pallas kernels  14.6 us (7%)
  between operations  13.4 us (7%)
  local copies, waits for them, and re-layouts  4.79 us (2%)
  starting transfers between devices  3.14 us (2%)
  matrix products  2.56 us (1%)
    reduce_scatter x1, waiting for transfers between devices, body(): summed = lax.psum_scatter(partial, 'z', scatter_dimension=0, tiled=True)  96.1 us
    all_gather x1, waiting for transfers between devices, body(): gathered = lax.all_gather(features, 'rep', axis=0, tiled=True)  58.5 us
    pallas_call x1, Pallas kernels, sparse_partial(): pl.pallas_call(kernel, grid_spec=grid_spec, out_shape=jax.ShapeDtypeStruc...  14.6 us
    ppermute x1, waiting for transfers between devices, body(): got = lax.ppermute(theirs, 'yh', [(0, 1), (1, 0)])  12.1 us
  transfers between devices with their start and end apart: 3, of which 3 were waited for; matrix products, arithmetic and copies ran while one was open for 0% of the time, Pallas kernels for 0%

profile of v7, /device:TPU:2, one launch (start us, length us, event | category | flops | bytes accessed | tf_op | source)
XLA Modules:
  0.0 205.9 jit_solution(7134189500621309329)
XLA Ops:
  6.5 0.0 copy-start
  6.5 0.0 all-gather.2.cloned.1.call-start
  6.5 0.7 all-gather.2.cloned.1.call-update
  7.3 0.0 reduce-scatter.2.cloned.1.call-start
  7.3 0.8 copy.8
  8.1 0.1 reshape_squeeze.3.cols_ref
  8.2 58.5 %all-gather.2.cloned.1.call-done.src_ref = bf16[4096,1024]{1,0:T(8,128)(2,1)} async-done(((bf16[256,1024]{1,0:T(8,128)(2,1)}), bf16[4096,1024]{1,0:T(8,128)(2,1)}) %all-gather.2.cloned.1.call-update) | async-done | bytes 8388624 | tf_op jit(solution)/shard_map/all_gather | solution.py:62
  66.7 0.0 copy-start.1
  66.7 2.2 %copy-done.1 = bf16[1,1,32,4,128,128]{5,4,3,2,1,0:T(8,128)(2,1)S(1)} copy-done((bf16[1,1,32,4,128,128]{5,4,3,2,1,0:T(8,128)(2,1)S(1)}, bf16[1,1,32,4,128,128]{5,4,3,2,1,0:T(8,128)(2,1)}, u32[]{:S(2)}) %copy-start.1) | copy-done | bytes 4194328
  68.8 0.0 copy-start.2
  68.9 0.7 copy-done.2
  69.5 14.6 %shard_map.64 = bf16[4096,1024]{1,0:T(8,128)(2,1)} custom-call(s32[128]{0:T(128)S(1)} %reshape_squeeze.3.cols_ref, s32[32]{0:T(128)S(1)} %bitcast.6, bf16[32,4,128,128]{3,2,1,0:T(8,128)(2,1)S(1)} %bitcast.5, bf16[4096,1024]{1,0:T(8,128)(2,1)} %all-gather.2.cloned.1.call-done.src_ref), custom_call_target="tpu_custom_call" | custom-call | tf_op jit(solution)/shard_map/pallas_call | solution.py:43
  84.1 0.0 copy-start.3
  84.1 0.0 reduce-scatter.2.cloned.1.call-update
  84.2 96.1 %reduce-scatter.2.cloned.1.call-done = bf16[512,1024]{1,0:T(8,128)(2,1)} async-done(((bf16[4096,1024]{1,0:T(8,128)(2,1)}), bf16[512,1024]{1,0:T(8,128)(2,1)}) %reduce-scatter.2.cloned.1.call-update) | async-done | bytes 1048592 | tf_op jit(solution)/shard_map/reduce_scatter | solution.py:64
  180.3 1.1 constant_dynamic-slice_fusion
  181.3 3.1 %collective-permute-start = (bf16[256,1024]{1,0:T(8,128)(2,1)S(1)}, bf16[256,1024]{1,0:T(8,128)(2,1)S(1)}, u32[]{:S(2)}, u32[]{:S(2)}) collective-permute-start(bf16[256,1024]{1,0:T(8,128)(2,1)S(1)} %constant_dynamic-slice_fusion), channel_id=1, source_target_pairs={{0,8},{8,0},{1,9},{9,1},{2,10},{10,2},{3,11},{11,3},{4,12},{12,4},... | collective-permute-start | bytes 1572872 | tf_op jit(solution)/shard_map/ppermute | solution.py:69
  184.4 0.0 copy-done.3
  184.4 12.1 %collective-permute-done = bf16[256,1024]{1,0:T(8,128)(2,1)S(1)} collective-permute-done((bf16[256,1024]{1,0:T(8,128)(2,1)S(1)}, bf16[256,1024]{1,0:T(8,128)(2,1)S(1)}, u32[]{:S(2)}, u32[]{:S(2)}) %collective-permute-start) | collective-permute-done | bytes 524320 | tf_op jit(solution)/shard_map/ppermute | solution.py:69
  196.5 0.0 copy-done
  196.5 2.6 %fusion.1 = bf16[256,1024]{1,0:T(8,128)(2,1)} fusion(bf16[1024,1024]{1,0:T(8,128)(2,1)S(1)} %copy-done, bf16[256,1024]{1,0:T(8,128)(2,1)S(1)} %collective-permute-done, f32[1024]{0:T(1024)S(1)} %convert_element_type.18, bf16[512,1024]{1,0:T(8,128)(2,1)} %reduce-scatter.2.cloned.1.call-done, s32[]{:T(128)S(6)} %select_n.6), kind=kOutput, calls=%fused_computation.2 | convolution fusion | flops 538705920 | bytes 3674116 | tf_op jit(solution)/shard_map/dot_general | solution.py:71
  (1 shorter events, 0.0 us)
Async XLA Ops:
  6.5 190.0 %copy-start = (bf16[1024,1024]{1,0:T(8,128)(2,1)S(1)}, bf16[1024,1024]{1,0:T(8,128)(2,1)}, u32[]{:S(2)}) copy-start(bf16[1024,1024]{1,0:T(8,128)(2,1)} %param.7) | copy-start | bytes 6291460
  6.5 60.1 %all-gather.2.cloned.1.call-start = ((), (), s32[]{:S(2)}) async-start(), calls=%async_computation.1 | async-start | bytes 8912896 | tf_op jit(solution)/shard_map/all_gather | solution.py:62
  7.3 173.0 %reduce-scatter.2.cloned.1.call-start = ((), (), s32[]{:S(2)}) async-start(), calls=%async_computation.2 | async-start | bytes 9437184 | tf_op jit(solution)/shard_map/reduce_scatter | solution.py:64
  66.7 2.2 %copy-start.1 = (bf16[1,1,32,4,128,128]{5,4,3,2,1,0:T(8,128)(2,1)S(1)}, bf16[1,1,32,4,128,128]{5,4,3,2,1,0:T(8,128)(2,1)}, u32[]{:S(2)}) copy-start(bf16[1,1,32,4,128,128]{5,4,3,2,1,0:T(8,128)(2,1)} %param.9) | copy-start | bytes 12582916
  68.8 0.7 copy-start.2
  84.1 100.3 %copy-start.3 = (bf16[1024]{0:T(1024)(128)(2,1)S(1)}, bf16[1024]{0:T(1024)(128)(2,1)}, u32[]{:S(2)}) copy-start(bf16[1024]{0:T(1024)(128)(2,1)} %param.8) | copy-start | bytes 6148
  181.3 15.2 %collective-permute-start = (bf16[256,1024]{1,0:T(8,128)(2,1)S(1)}, bf16[256,1024]{1,0:T(8,128)(2,1)S(1)}, u32[]{:S(2)}, u32[]{:S(2)}) collective-permute-start(bf16[256,1024]{1,0:T(8,128)(2,1)S(1)} %constant_dynamic-slice_fusion), channel_id=1, source_target_pairs={{0,8},{8,0},{1,9},{9,1},{2,10},{10,2},{3,11},{11,3},{4,12},{12,4},... | collective-permute-start | bytes 1572872 | tf_op jit(solution)/shard_map/ppermute | solution.py:69
Sparse Core Ops, SparseCore 0:
  9.2 57.4 all-gather.1
  84.3 95.9 reduce-scatter.1

commit v8 on v7

--- a/solution.py
+++ b/solution.py
@@ -16,20 +16,24 @@
         for g in range(group):
             b = step * group + g
             live = counts_ref[b]
-            lhs = jnp.concatenate(
-                [jnp.where(k < live, tile_ref[g, k], jnp.zeros_like(tile_ref[g, k])) for k in range(slots)],
-                axis=1,
-            )
-            rhs = jnp.concatenate(
-                [
-                    src_ref[pl.ds(pl.multiple_of(cols_ref[b * slots + k] * side, side), side), :]
-                    for k in range(slots)
-                ],
-                axis=0,
-            )
-            out_ref[pl.ds(g * side, side), :] = jnp.dot(
-                lhs, rhs, preferred_element_type=jnp.float32
-            ).astype(out_ref.dtype)
+            rows = pl.ds(g * side, side)
+            for n in range(slots + 1):
+                @pl.when(live == n)
+                def _(n=n, b=b, g=g, rows=rows):
+                    if n == 0:
+                        out_ref[rows, :] = jnp.zeros((side, width), out_ref.dtype)
+                        return
+                    lhs = jnp.concatenate([tile_ref[g, k] for k in range(n)], axis=1)
+                    rhs = jnp.concatenate(
+                        [
+                            src_ref[pl.ds(pl.multiple_of(cols_ref[b * slots + k] * side, side), side), :]
+                            for k in range(n)
+                        ],
+                        axis=0,
+                    )
+                    out_ref[rows, :] = jnp.dot(lhs, rhs, preferred_element_type=jnp.float32).astype(
+                        out_ref.dtype
+                    )
 
     grid_spec = pltpu.PrefetchScalarGridSpec(
         num_scalar_prefetch=2,

time: 206 us -> 206 us (level)
  no operation moved by 1% of the time
where the time goes in v8:
time: 206 us; the launch traced here: 205 us
  waiting for transfers between devices  167 us (81%)
  Pallas kernels  13.9 us (7%)
  between operations  13.4 us (7%)
  local copies, waits for them, and re-layouts  4.79 us (2%)
  starting transfers between devices  3.16 us (2%)
  matrix products  2.56 us (1%)
    reduce_scatter x1, waiting for transfers between devices, body(): summed = lax.psum_scatter(partial, 'z', scatter_dimension=0, tiled=True)  96.2 us
    all_gather x1, waiting for transfers between devices, body(): gathered = lax.all_gather(features, 'rep', axis=0, tiled=True)  58.5 us
    pallas_call x1, Pallas kernels, sparse_partial(): pl.pallas_call(kernel, grid_spec=grid_spec, out_shape=jax.ShapeDtypeStruc...  13.9 us
    ppermute x1, waiting for transfers between devices, body(): got = lax.ppermute(theirs, 'yh', [(0, 1), (1, 0)])  12.1 us
  transfers between devices with their start and end apart: 3, of which 3 were waited for; matrix products, arithmetic and copies ran while one was open for 0% of the time, Pallas kernels for 0%

profile of v8, /device:TPU:2, one launch (start us, length us, event | category | flops | bytes accessed | tf_op | source)
XLA Modules:
  0.0 205.3 jit_solution(1248887642750826257)
XLA Ops:
  6.5 0.0 copy-start
  6.5 0.0 all-gather.2.cloned.1.call-start
  6.5 0.7 all-gather.2.cloned.1.call-update
  7.3 0.0 reduce-scatter.2.cloned.1.call-start
  7.3 0.8 copy.8
  8.1 0.1 reshape_squeeze.3.cols_ref
  8.2 58.5 %all-gather.2.cloned.1.call-done.src_ref = bf16[4096,1024]{1,0:T(8,128)(2,1)} async-done(((bf16[256,1024]{1,0:T(8,128)(2,1)}), bf16[4096,1024]{1,0:T(8,128)(2,1)}) %all-gather.2.cloned.1.call-update) | async-done | bytes 8388624 | tf_op jit(solution)/shard_map/all_gather | solution.py:66
  66.7 0.0 copy-start.1
  66.7 2.2 %copy-done.1 = bf16[1,1,32,4,128,128]{5,4,3,2,1,0:T(8,128)(2,1)S(1)} copy-done((bf16[1,1,32,4,128,128]{5,4,3,2,1,0:T(8,128)(2,1)S(1)}, bf16[1,1,32,4,128,128]{5,4,3,2,1,0:T(8,128)(2,1)}, u32[]{:S(2)}) %copy-start.1) | copy-done | bytes 4194328
  68.8 0.0 copy-start.2
  68.9 0.7 copy-done.2
  69.5 13.9 %shard_map.64 = bf16[4096,1024]{1,0:T(8,128)(2,1)} custom-call(s32[128]{0:T(128)S(1)} %reshape_squeeze.3.cols_ref, s32[32]{0:T(128)S(1)} %bitcast.6, bf16[32,4,128,128]{3,2,1,0:T(8,128)(2,1)S(1)} %bitcast.5, bf16[4096,1024]{1,0:T(8,128)(2,1)} %all-gather.2.cloned.1.call-done.src_ref), custom_call_target="tpu_custom_call" | custom-call | tf_op jit(solution)/shard_map/pallas_call | solution.py:47
  83.4 0.0 copy-start.3
  83.4 0.0 reduce-scatter.2.cloned.1.call-update
  83.5 96.2 %reduce-scatter.2.cloned.1.call-done = bf16[512,1024]{1,0:T(8,128)(2,1)} async-done(((bf16[4096,1024]{1,0:T(8,128)(2,1)}), bf16[512,1024]{1,0:T(8,128)(2,1)}) %reduce-scatter.2.cloned.1.call-update) | async-done | bytes 1048592 | tf_op jit(solution)/shard_map/reduce_scatter | solution.py:68
  179.7 1.1 constant_dynamic-slice_fusion
  180.7 3.1 %collective-permute-start = (bf16[256,1024]{1,0:T(8,128)(2,1)S(1)}, bf16[256,1024]{1,0:T(8,128)(2,1)S(1)}, u32[]{:S(2)}, u32[]{:S(2)}) collective-permute-start(bf16[256,1024]{1,0:T(8,128)(2,1)S(1)} %constant_dynamic-slice_fusion), channel_id=1, source_target_pairs={{0,8},{8,0},{1,9},{9,1},{2,10},{10,2},{3,11},{11,3},{4,12},{12,4},... | collective-permute-start | bytes 1572872 | tf_op jit(solution)/shard_map/ppermute | solution.py:73
  183.8 0.0 copy-done.3
  183.9 12.1 %collective-permute-done = bf16[256,1024]{1,0:T(8,128)(2,1)S(1)} collective-permute-done((bf16[256,1024]{1,0:T(8,128)(2,1)S(1)}, bf16[256,1024]{1,0:T(8,128)(2,1)S(1)}, u32[]{:S(2)}, u32[]{:S(2)}) %collective-permute-start) | collective-permute-done | bytes 524320 | tf_op jit(solution)/shard_map/ppermute | solution.py:73
  195.9 0.0 copy-done
  195.9 2.6 %fusion.1 = bf16[256,1024]{1,0:T(8,128)(2,1)} fusion(bf16[1024,1024]{1,0:T(8,128)(2,1)S(1)} %copy-done, bf16[256,1024]{1,0:T(8,128)(2,1)S(1)} %collective-permute-done, f32[1024]{0:T(1024)S(1)} %convert_element_type.18, bf16[512,1024]{1,0:T(8,128)(2,1)} %reduce-scatter.2.cloned.1.call-done, s32[]{:T(128)S(6)} %select_n.6), kind=kOutput, calls=%fused_computation.2 | convolution fusion | flops 538705920 | bytes 3674116 | tf_op jit(solution)/shard_map/dot_general | solution.py:75
  (1 shorter events, 0.0 us)
Async XLA Ops:
  6.5 189.4 %copy-start = (bf16[1024,1024]{1,0:T(8,128)(2,1)S(1)}, bf16[1024,1024]{1,0:T(8,128)(2,1)}, u32[]{:S(2)}) copy-start(bf16[1024,1024]{1,0:T(8,128)(2,1)} %param.7) | copy-start | bytes 6291460
  6.5 60.1 %all-gather.2.cloned.1.call-start = ((), (), s32[]{:S(2)}) async-start(), calls=%async_computation.1 | async-start | bytes 8912896 | tf_op jit(solution)/shard_map/all_gather | solution.py:66
  7.3 172.4 %reduce-scatter.2.cloned.1.call-start = ((), (), s32[]{:S(2)}) async-start(), calls=%async_computation.2 | async-start | bytes 9437184 | tf_op jit(solution)/shard_map/reduce_scatter | solution.py:68
  66.7 2.2 %copy-start.1 = (bf16[1,1,32,4,128,128]{5,4,3,2,1,0:T(8,128)(2,1)S(1)}, bf16[1,1,32,4,128,128]{5,4,3,2,1,0:T(8,128)(2,1)}, u32[]{:S(2)}) copy-start(bf16[1,1,32,4,128,128]{5,4,3,2,1,0:T(8,128)(2,1)} %param.9) | copy-start | bytes 12582916
  68.8 0.7 copy-start.2
  83.4 100.4 %copy-start.3 = (bf16[1024]{0:T(1024)(128)(2,1)S(1)}, bf16[1024]{0:T(1024)(128)(2,1)}, u32[]{:S(2)}) copy-start(bf16[1024]{0:T(1024)(128)(2,1)} %param.8) | copy-start | bytes 6148
  180.7 15.2 %collective-permute-start = (bf16[256,1024]{1,0:T(8,128)(2,1)S(1)}, bf16[256,1024]{1,0:T(8,128)(2,1)S(1)}, u32[]{:S(2)}, u32[]{:S(2)}) collective-permute-start(bf16[256,1024]{1,0:T(8,128)(2,1)S(1)} %constant_dynamic-slice_fusion), channel_id=1, source_target_pairs={{0,8},{8,0},{1,9},{9,1},{2,10},{10,2},{3,11},{11,3},{4,12},{12,4},... | collective-permute-start | bytes 1572872 | tf_op jit(solution)/shard_map/ppermute | solution.py:73
Sparse Core Ops, SparseCore 0:
  9.2 57.4 all-gather.1
  83.6 96.0 reduce-scatter.1

commit v9 on v7

--- a/solution.py
+++ b/solution.py
@@ -50,6 +50,9 @@
     )(cols.reshape(-1), counts, tiles, gathered)
 
 
+N_SWAP = 4
+
+
 def body(features, weight, bias, tile_vals, tile_col, tile_count):
     n_hi = lax.axis_size("yh")
     n_lo = lax.axis_size("z")
@@ -66,7 +69,14 @@
     rows = summed.shape[0] // n_hi
     mine = lax.dynamic_slice_in_dim(summed, hi * rows, rows, axis=0)
     theirs = lax.dynamic_slice_in_dim(summed, (1 - hi) * rows, rows, axis=0)
-    got = lax.ppermute(theirs, "yh", [(0, 1), (1, 0)])
+    quarter = theirs.shape[1] // N_SWAP
+    got = jnp.concatenate(
+        [
+            lax.ppermute(theirs[:, q * quarter:(q + 1) * quarter], "yh", [(0, 1), (1, 0)])
+            for q in range(N_SWAP)
+        ],
+        axis=1,
+    )
     summed = (mine.astype(jnp.float32) + got.astype(jnp.float32)).astype(jnp.bfloat16)
     mixed = jnp.dot(summed, weight, preferred_element_type=jnp.float32) + bias.astype(jnp.float32)
     return jnp.maximum(mixed, 0.0).astype(jnp.bfloat16)

time: 206 us -> 206 us (level)
  starting transfers between devices: 3.14 us -> 7.19 us
  waiting for transfers between devices: 167 us -> 163 us
    ppermute x1 -> x4, waiting for transfers between devices: 12.1 us -> 8.04 us  [body(): lax.ppermute(theirs[:, q * quarter:(q + 1) * quarter], 'yh', [(0, 1), (1,...]
    ppermute x1 -> x4, starting transfers between devices: 3.1 us -> 7.15 us  [body(): lax.ppermute(theirs[:, q * quarter:(q + 1) * quarter], 'yh', [(0, 1), (1,...]
  transfers between devices with their start and end apart: 3 -> 6, of which waited for: 3 -> 5; matrix products, arithmetic and copies ran while one was open for 0% -> 0% of each run, Pallas kernels for 0% -> 0%
where the time goes in v9:
time: 206 us
  waiting for transfers between devices  163 us (79%)
  Pallas kernels  14.7 us (7%)
  between operations  13.4 us (7%)
  starting transfers between devices  7.19 us (3%)
  local copies, waits for them, and re-layouts  4.85 us (2%)
  matrix products  2.58 us (1%)
    reduce_scatter x1, waiting for transfers between devices, body(): summed = lax.psum_scatter(partial, 'z', scatter_dimension=0, tiled=True)  96.1 us
    all_gather x1, waiting for transfers between devices, body(): gathered = lax.all_gather(features, 'rep', axis=0, tiled=True)  58.5 us
    pallas_call x1, Pallas kernels, sparse_partial(): pl.pallas_call(kernel, grid_spec=grid_spec, out_shape=jax.ShapeDtypeStruc...  14.7 us
    ppermute x4, waiting for transfers between devices, body(): lax.ppermute(theirs[:, q * quarter:(q + 1) * quarter], 'yh', [(0, 1), (1,...  8.04 us
    ppermute x4, starting transfers between devices, body(): lax.ppermute(theirs[:, q * quarter:(q + 1) * quarter], 'yh', [(0, 1), (1,...  7.15 us
  transfers between devices with their start and end apart: 6, of which 5 were waited for; matrix products, arithmetic and copies ran while one was open for 0% of the time, Pallas kernels for 0%

profile of v9, /device:TPU:2, one launch (start us, length us, event | category | flops | bytes accessed | tf_op | source)
XLA Modules:
  0.0 206.0 jit_solution(6599631325599732240)
XLA Ops:
  6.5 0.0 copy-start
  6.5 0.0 all-gather.2.cloned.1.call-start
  6.5 0.7 all-gather.2.cloned.1.call-update
  7.3 0.0 reduce-scatter.2.cloned.1.call-start
  7.3 0.8 copy.8
  8.1 0.1 reshape_squeeze.3.cols_ref
  8.2 58.5 %all-gather.2.cloned.1.call-done.src_ref = bf16[4096,1024]{1,0:T(8,128)(2,1)} async-done(((bf16[256,1024]{1,0:T(8,128)(2,1)}), bf16[4096,1024]{1,0:T(8,128)(2,1)}) %all-gather.2.cloned.1.call-update) | async-done | bytes 8388624 | tf_op jit(solution)/shard_map/all_gather | solution.py:65
  66.7 0.0 copy-start.1
  66.7 2.2 %copy-done.1 = bf16[1,1,32,4,128,128]{5,4,3,2,1,0:T(8,128)(2,1)S(1)} copy-done((bf16[1,1,32,4,128,128]{5,4,3,2,1,0:T(8,128)(2,1)S(1)}, bf16[1,1,32,4,128,128]{5,4,3,2,1,0:T(8,128)(2,1)}, u32[]{:S(2)}) %copy-start.1) | copy-done | bytes 4194328
  68.8 0.0 copy-start.2
  68.9 0.7 copy-done.2
  69.5 14.7 %shard_map.64 = bf16[4096,1024]{1,0:T(8,128)(2,1)} custom-call(s32[128]{0:T(128)S(1)} %reshape_squeeze.3.cols_ref, s32[32]{0:T(128)S(1)} %bitcast.6, bf16[32,4,128,128]{3,2,1,0:T(8,128)(2,1)S(1)} %bitcast.5, bf16[4096,1024]{1,0:T(8,128)(2,1)} %all-gather.2.cloned.1.call-done.src_ref), custom_call_target="tpu_custom_call" | custom-call | tf_op jit(solution)/shard_map/pallas_call | solution.py:43
  84.2 0.0 copy-start.3
  84.2 0.0 reduce-scatter.2.cloned.1.call-update
  84.2 96.1 %reduce-scatter.2.cloned.1.call-done = bf16[512,1024]{1,0:T(8,128)(2,1)} async-done(((bf16[4096,1024]{1,0:T(8,128)(2,1)}), bf16[512,1024]{1,0:T(8,128)(2,1)}) %reduce-scatter.2.cloned.1.call-update) | async-done | bytes 1048592 | tf_op jit(solution)/shard_map/reduce_scatter | solution.py:67
  180.3 1.1 constant_dynamic-slice_fusion
  181.4 3.1 %collective-permute-start.3 = (bf16[256,256]{1,0:T(8,128)(2,1)S(1)}, bf16[256,256]{1,0:T(8,128)(2,1)S(1)}, u32[]{:S(2)}, u32[]{:S(2)}) collective-permute-start(bf16[256,256]{1,0:T(8,128)(2,1)S(1)} %get-tuple-element.8), channel_id=1, source_target_pairs={{0,8},{8,0},{1,9},{9,1},{2,10},{10,2},{3,11},{11,3},{4,12},{12,4},... | collective-permute-start | bytes 393224 | tf_op jit(solution)/shard_map/ppermute | solution.py:75
  184.5 0.5 collective-permute-start.2
  185.0 3.0 %collective-permute-start.1 = (bf16[256,256]{1,0:T(8,128)(2,1)S(1)}, bf16[256,256]{1,0:T(8,128)(2,1)S(1)}, u32[]{:S(2)}, u32[]{:S(2)}) collective-permute-start(bf16[256,256]{1,0:T(8,128)(2,1)S(1)} %get-tuple-element.7), channel_id=1, source_target_pairs={{0,8},{8,0},{1,9},{9,1},{2,10},{10,2},{3,11},{11,3},{4,12},{12,4},... | collective-permute-start | bytes 393224 | tf_op jit(solution)/shard_map/ppermute | solution.py:75
  188.1 0.5 collective-permute-start
  188.6 0.0 copy-done.3
  188.6 0.0 collective-permute-done.3
  188.6 3.8 %collective-permute-done.2 = bf16[256,256]{1,0:T(8,128)(2,1)S(1)} collective-permute-done((bf16[256,256]{1,0:T(8,128)(2,1)S(1)}, bf16[256,256]{1,0:T(8,128)(2,1)S(1)}, u32[]{:S(2)}, u32[]{:S(2)}) %collective-permute-start.2) | collective-permute-done | bytes 131104 | tf_op jit(solution)/shard_map/ppermute | solution.py:75
  192.4 2.8 %collective-permute-done.1 = bf16[256,256]{1,0:T(8,128)(2,1)S(1)} collective-permute-done((bf16[256,256]{1,0:T(8,128)(2,1)S(1)}, bf16[256,256]{1,0:T(8,128)(2,1)S(1)}, u32[]{:S(2)}, u32[]{:S(2)}) %collective-permute-start.1) | collective-permute-done | bytes 131104 | tf_op jit(solution)/shard_map/ppermute | solution.py:75
  195.2 1.4 collective-permute-done
  196.6 0.0 copy-done
  196.6 2.6 %fusion.1 = bf16[256,1024]{1,0:T(8,128)(2,1)} fusion(bf16[1024,1024]{1,0:T(8,128)(2,1)S(1)} %copy-done, bf16[256,256]{1,0:T(8,128)(2,1)S(1)} %collective-permute-done.3, bf16[256,256]{1,0:T(8,128)(2,1)S(1)} %collective-permute-done.2, bf16[256,256]{1,0:T(8,128)(2,1)S(1)} %collective-permute-done.1, bf16[256,256]{1,0:T(8,128)(2,1)S(1)} %collective-permute-done, ...), kind=kOutput, calls=%fused_computation.2 | convolution fusion | flops 540540928 | bytes 3674116 | tf_op jit(solution)/shard_map/dot_general | solution.py:81
  (1 shorter events, 0.0 us)
Async XLA Ops:
  6.5 190.1 %copy-start = (bf16[1024,1024]{1,0:T(8,128)(2,1)S(1)}, bf16[1024,1024]{1,0:T(8,128)(2,1)}, u32[]{:S(2)}) copy-start(bf16[1024,1024]{1,0:T(8,128)(2,1)} %param.7) | copy-start | bytes 6291460
  6.5 60.1 %all-gather.2.cloned.1.call-start = ((), (), s32[]{:S(2)}) async-start(), calls=%async_computation.1 | async-start | bytes 8912896 | tf_op jit(solution)/shard_map/all_gather | solution.py:65
  7.3 173.0 %reduce-scatter.2.cloned.1.call-start = ((), (), s32[]{:S(2)}) async-start(), calls=%async_computation.2 | async-start | bytes 9437184 | tf_op jit(solution)/shard_map/reduce_scatter | solution.py:67
  66.7 2.2 %copy-start.1 = (bf16[1,1,32,4,128,128]{5,4,3,2,1,0:T(8,128)(2,1)S(1)}, bf16[1,1,32,4,128,128]{5,4,3,2,1,0:T(8,128)(2,1)}, u32[]{:S(2)}) copy-start(bf16[1,1,32,4,128,128]{5,4,3,2,1,0:T(8,128)(2,1)} %param.9) | copy-start | bytes 12582916
  68.8 0.7 copy-start.2
  84.2 104.4 %copy-start.3 = (bf16[1024]{0:T(1024)(128)(2,1)S(1)}, bf16[1024]{0:T(1024)(128)(2,1)}, u32[]{:S(2)}) copy-start(bf16[1024]{0:T(1024)(128)(2,1)} %param.8) | copy-start | bytes 6148
  181.4 7.2 %collective-permute-start.3 = (bf16[256,256]{1,0:T(8,128)(2,1)S(1)}, bf16[256,256]{1,0:T(8,128)(2,1)S(1)}, u32[]{:S(2)}, u32[]{:S(2)}) collective-permute-start(bf16[256,256]{1,0:T(8,128)(2,1)S(1)} %get-tuple-element.8), channel_id=1, source_target_pairs={{0,8},{8,0},{1,9},{9,1},{2,10},{10,2},{3,11},{11,3},{4,12},{12,4},... | collective-permute-start | bytes 393224 | tf_op jit(solution)/shard_map/ppermute | solution.py:75
  184.5 7.9 %collective-permute-start.2 = (bf16[256,256]{1,0:T(8,128)(2,1)S(1)}, bf16[256,256]{1,0:T(8,128)(2,1)S(1)}, u32[]{:S(2)}, u32[]{:S(2)}) collective-permute-start(bf16[256,256]{1,0:T(8,128)(2,1)S(1)} %get-tuple-element.6), channel_id=1, source_target_pairs={{0,8},{8,0},{1,9},{9,1},{2,10},{10,2},{3,11},{11,3},{4,12},{12,4},... | collective-permute-start | bytes 393224 | tf_op jit(solution)/shard_map/ppermute | solution.py:75
  185.0 10.2 %collective-permute-start.1 = (bf16[256,256]{1,0:T(8,128)(2,1)S(1)}, bf16[256,256]{1,0:T(8,128)(2,1)S(1)}, u32[]{:S(2)}, u32[]{:S(2)}) collective-permute-start(bf16[256,256]{1,0:T(8,128)(2,1)S(1)} %get-tuple-element.7), channel_id=1, source_target_pairs={{0,8},{8,0},{1,9},{9,1},{2,10},{10,2},{3,11},{11,3},{4,12},{12,4},... | collective-permute-start | bytes 393224 | tf_op jit(solution)/shard_map/ppermute | solution.py:75
  188.1 8.6 %collective-permute-start = (bf16[256,256]{1,0:T(8,128)(2,1)S(1)}, bf16[256,256]{1,0:T(8,128)(2,1)S(1)}, u32[]{:S(2)}, u32[]{:S(2)}) collective-permute-start(bf16[256,256]{1,0:T(8,128)(2,1)S(1)} %get-tuple-element.5), channel_id=1, source_target_pairs={{0,8},{8,0},{1,9},{9,1},{2,10},{10,2},{3,11},{11,3},{4,12},{12,4},... | collective-permute-start | bytes 393224 | tf_op jit(solution)/shard_map/ppermute | solution.py:75
Sparse Core Ops, SparseCore 0:
  9.2 57.4 all-gather.1
  84.3 95.9 reduce-scatter.1

commit v10 on v7

--- a/solution.py
+++ b/solution.py
@@ -10,8 +10,9 @@
     n_blocks, slots, side, _ = tiles.shape
     width = gathered.shape[1]
     n_src = gathered.shape[0]
+    half = width // 2
 
-    def kernel(cols_ref, counts_ref, tile_ref, src_ref, out_ref):
+    def kernel(cols_ref, counts_ref, tile_ref, src_ref, out_a, out_b):
         step = pl.program_id(0)
         for g in range(group):
             b = step * group + g
@@ -27,9 +28,9 @@
                 ],
                 axis=0,
             )
-            out_ref[pl.ds(g * side, side), :] = jnp.dot(
-                lhs, rhs, preferred_element_type=jnp.float32
-            ).astype(out_ref.dtype)
+            prod = jnp.dot(lhs, rhs, preferred_element_type=jnp.float32).astype(out_a.dtype)
+            out_a[pl.ds(g * side, side), :] = prod[:, :half]
+            out_b[pl.ds(g * side, side), :] = prod[:, half:]
 
     grid_spec = pltpu.PrefetchScalarGridSpec(
         num_scalar_prefetch=2,
@@ -38,12 +39,15 @@
             pl.BlockSpec((group, slots, side, side), lambda i, c, n: (i, 0, 0, 0)),
             pl.BlockSpec((n_src, width), lambda i, c, n: (0, 0)),
         ],
-        out_specs=pl.BlockSpec((group * side, width), lambda i, c, n: (out_pos(i * group) // group, 0)),
+        out_specs=[
+            pl.BlockSpec((group * side, half), lambda i, c, n: (out_pos(i * group) // group, 0)),
+            pl.BlockSpec((group * side, half), lambda i, c, n: (out_pos(i * group) // group, 0)),
+        ],
     )
     return pl.pallas_call(
         kernel,
         grid_spec=grid_spec,
-        out_shape=jax.ShapeDtypeStruct((n_blocks * side, width), jnp.bfloat16),
+        out_shape=[jax.ShapeDtypeStruct((n_blocks * side, half), jnp.bfloat16)] * 2,
         compiler_params=pltpu.CompilerParams(
             dimension_semantics=("arbitrary",), vmem_limit_bytes=48 * 1024 * 1024
         ),
@@ -60,14 +64,25 @@
         return ((j % n_lo) * n_hi + j // n_lo) * per_dev + b % per_dev
 
     gathered = lax.all_gather(features, "rep", axis=0, tiled=True)
-    partial = sparse_partial(gathered, tile_vals[0, 0], tile_col[0, 0], tile_count[0, 0], out_pos, per_dev)
-    summed = lax.psum_scatter(partial, "z", scatter_dimension=0, tiled=True)
+    part_a, part_b = sparse_partial(
+        gathered, tile_vals[0, 0], tile_col[0, 0], tile_count[0, 0], out_pos, per_dev
+    )
     hi = lax.axis_index("yh")
-    rows = summed.shape[0] // n_hi
-    mine = lax.dynamic_slice_in_dim(summed, hi * rows, rows, axis=0)
-    theirs = lax.dynamic_slice_in_dim(summed, (1 - hi) * rows, rows, axis=0)
-    got = lax.ppermute(theirs, "yh", [(0, 1), (1, 0)])
-    summed = (mine.astype(jnp.float32) + got.astype(jnp.float32)).astype(jnp.bfloat16)
+    swap = [(0, 1), (1, 0)]
+    grid_b = part_b.reshape(n_lo, n_hi, -1, part_b.shape[1])
+    mine_b = lax.dynamic_index_in_dim(grid_b, hi, axis=1, keepdims=False)
+    theirs_b = lax.dynamic_index_in_dim(grid_b, 1 - hi, axis=1, keepdims=False)
+    got_b = lax.ppermute(theirs_b, "yh", swap)
+    sum_b = (mine_b.astype(jnp.float32) + got_b.astype(jnp.float32)).astype(jnp.bfloat16)
+    sum_b = sum_b.reshape(-1, part_b.shape[1])
+    red_a = lax.psum_scatter(part_a, "z", scatter_dimension=0, tiled=True)
+    rows = red_a.shape[0] // n_hi
+    mine = lax.dynamic_slice_in_dim(red_a, hi * rows, rows, axis=0)
+    theirs = lax.dynamic_slice_in_dim(red_a, (1 - hi) * rows, rows, axis=0)
+    got = lax.ppermute(theirs, "yh", swap)
+    out_a = (mine.astype(jnp.float32) + got.astype(jnp.float32)).astype(jnp.bfloat16)
+    out_b = lax.psum_scatter(sum_b, "z", scatter_dimension=0, tiled=True)
+    summed = jnp.concatenate([out_a, out_b], axis=1)
     mixed = jnp.dot(summed, weight, preferred_element_type=jnp.float32) + bias.astype(jnp.float32)
     return jnp.maximum(mixed, 0.0).astype(jnp.bfloat16)
 

time: 206 us -> 196 us (0.951)
  waiting for transfers between devices: 167 us -> 145 us
  other arithmetic: 0.01 us -> 5.26 us
  starting transfers between devices: 3.14 us -> 6.18 us
  local copies, waits for them, and re-layouts: 4.79 us -> 7.51 us
    reduce_scatter x1 -> x2, waiting for transfers between devices: 96.1 us -> 32.7 us  [the longest x1 32.7 us: body(): out_b = lax.psum_scatter(sum_b, 'z', scatter_dimension=0, tiled=True)]
    ppermute x1 -> x2, waiting for transfers between devices: 12.1 us -> 52.6 us  [the longest x1 46.6 us: body(): got_b = lax.ppermute(theirs_b, 'yh', swap)]
    convert_element_type x0 -> x2, other arithmetic: none -> 5.25 us  [the longest x1 4.24 us: body(): (mine_b.astype(jnp.float32) + got_b.astype(jnp.float32)).astype(jnp.bfloa...]
    squeeze x0 -> x1, local copies, waits for them, and re-layouts: none -> 3.06 us  [body(): theirs_b = lax.dynamic_index_in_dim(grid_b, 1 - hi, axis=1, keepdims=False)]
    ppermute x1 -> x2, starting transfers between devices: 3.1 us -> 6.1 us  [the longest x1 3.1 us: body(): got = lax.ppermute(theirs, 'yh', swap)]
  transfers between devices with their start and end apart: 3 -> 5, of which waited for: 3 -> 4; matrix products, arithmetic and copies ran while one was open for 0% -> 5% of each run, Pallas kernels for 0% -> 0%
where the time goes in v10:
time: 196 us
  waiting for transfers between devices  145 us (74%)
  Pallas kernels  16.6 us (8%)
  between operations  13.1 us (7%)
  local copies, waits for them, and re-layouts  7.51 us (4%)
  starting transfers between devices  6.18 us (3%)
  other arithmetic  5.26 us (3%)
  matrix products  2.46 us (1%)
    all_gather x1, waiting for transfers between devices, body(): gathered = lax.all_gather(features, 'rep', axis=0, tiled=True)  58.5 us
    ppermute x1, waiting for transfers between devices, body(): got_b = lax.ppermute(theirs_b, 'yh', swap)  46.6 us
    reduce_scatter x1, waiting for transfers between devices, body(): out_b = lax.psum_scatter(sum_b, 'z', scatter_dimension=0, tiled=True)  32.7 us
    pallas_call x1, Pallas kernels, sparse_partial(): pl.pallas_call(kernel, grid_spec=grid_spec, out_shape=[jax.ShapeDtypeStru...  16.6 us
    ppermute x1, waiting for transfers between devices, body(): got = lax.ppermute(theirs, 'yh', swap)  6.07 us
    convert_element_type x1, other arithmetic, body(): (mine_b.astype(jnp.float32) + got_b.astype(jnp.float32)).astype(jnp.bfloa...  4.24 us
  transfers between devices with their start and end apart: 5, of which 4 were waited for; matrix products, arithmetic and copies ran while one was open for 5% of the time, Pallas kernels for 0%

profile of v10, /device:TPU:2, one launch (start us, length us, event | category | flops | bytes accessed | tf_op | source)
XLA Modules:
  0.0 195.8 jit_solution(11184651587993929437)
XLA Ops:
  6.5 0.0 copy-start
  6.5 0.0 all-gather.2.cloned.1.call-start
  6.5 0.7 all-gather.2.cloned.1.call-update
  7.3 0.0 reduce-scatter.3.cloned.1.call-start
  7.3 0.8 copy.8
  8.1 0.1 reshape_squeeze.3.cols_ref
  8.2 58.5 %all-gather.2.cloned.1.call-done.src_ref = bf16[4096,1024]{1,0:T(8,128)(2,1)} async-done(((bf16[256,1024]{1,0:T(8,128)(2,1)}), bf16[4096,1024]{1,0:T(8,128)(2,1)}) %all-gather.2.cloned.1.call-update) | async-done | bytes 8388624 | tf_op jit(solution)/shard_map/all_gather | solution.py:66
  66.7 0.0 copy-start.2
  66.7 0.7 copy-done.2
  67.3 16.6 %shard_map.64 = (bf16[4096,512]{1,0:T(8,128)(2,1)S(1)}, bf16[4096,512]{1,0:T(8,128)(2,1)}) custom-call(s32[128]{0:T(128)S(1)} %reshape_squeeze.3.cols_ref, s32[32]{0:T(128)S(1)} %bitcast.12, bf16[32,4,128,128]{3,2,1,0:T(8,128)(2,1)} %bitcast.14, bf16[4096,1024]{1,0:T(8,128)(2,1)} %all-gather.2.cloned.1.call-done.src_ref), custom_call_target="tpu_custom_call" | custom-call | tf_op jit(solution)/shard_map/pallas_call | solution.py:47
  84.0 0.0 copy-start.1
  84.0 1.9 copy-done.1
  85.9 0.0 reduce-scatter.3.cloned.1.call-update
  85.9 0.0 reduce-scatter.5.cloned.1.call-start
  86.0 3.1 %dynamic-slice_bitcast_fusion = bf16[8,256,512]{2,1,0:T(8,128)(2,1)} fusion(bf16[8,2,256,512]{3,2,1,0:T(8,128)(2,1)} %bitcast.15, s32[]{:T(128)S(6)} %select_n.16), kind=kLoop, calls=%fused_computation.2 | loop fusion | bytes 4194308 | tf_op jit(solution)/shard_map/jit(dynamic_index_in_dim)/squeeze | solution.py:74
  89.0 3.0 %collective-permute-start.1 = (bf16[8,256,512]{2,1,0:T(8,128)(2,1)}, bf16[8,256,512]{2,1,0:T(8,128)(2,1)}, u32[]{:S(2)}, u32[]{:S(2)}) collective-permute-start(bf16[8,256,512]{2,1,0:T(8,128)(2,1)} %dynamic-slice_bitcast_fusion), channel_id=1, source_target_pairs={{0,8},{8,0},{1,9},{9,1},{2,10},{10,2},{3,11},{11,3},{4,12},{12,4},... | collective-permute-start | bytes 6291464 | tf_op jit(solution)/shard_map/ppermute | solution.py:75
  92.1 46.6 %collective-permute-done.1 = bf16[8,256,512]{2,1,0:T(8,128)(2,1)} collective-permute-done((bf16[8,256,512]{2,1,0:T(8,128)(2,1)}, bf16[8,256,512]{2,1,0:T(8,128)(2,1)}, u32[]{:S(2)}, u32[]{:S(2)}) %collective-permute-start.1) | collective-permute-done | bytes 2097184 | tf_op jit(solution)/shard_map/ppermute | solution.py:75
  138.6 4.2 %fusion = bf16[8,256,512]{2,1,0:T(8,128)(2,1)} fusion(bf16[8,256,512]{2,1,0:T(8,128)(2,1)} %collective-permute-done.1, bf16[8,2,256,512]{3,2,1,0:T(8,128)(2,1)} %bitcast.16, s32[]{:T(128)S(6)} %select_n.15), kind=kLoop, calls=%fused_computation.1 | loop fusion | flops 4194304 | bytes 6291460 | tf_op jit(solution)/shard_map/convert_element_type | solution.py:76
  142.9 0.0 copy-start.3
  142.9 0.0 reduce-scatter.5.cloned.1.call-update
  142.9 0.0 reduce-scatter.3.cloned.1.call-done
  142.9 1.0 constant_dynamic-slice_fusion
  143.9 3.1 %collective-permute-start = (bf16[256,512]{1,0:T(8,128)(2,1)S(1)}, bf16[256,512]{1,0:T(8,128)(2,1)S(1)}, u32[]{:S(2)}, u32[]{:S(2)}) collective-permute-start(bf16[256,512]{1,0:T(8,128)(2,1)S(1)} %constant_dynamic-slice_fusion), channel_id=1, source_target_pairs={{0,8},{8,0},{1,9},{9,1},{2,10},{10,2},{3,11},{11,3},{4,12},{12,4},... | collective-permute-start | bytes 786440 | tf_op jit(solution)/shard_map/ppermute | solution.py:82
  147.0 0.0 copy-done.3
  147.0 6.1 %collective-permute-done = bf16[256,512]{1,0:T(8,128)(2,1)S(1)} collective-permute-done((bf16[256,512]{1,0:T(8,128)(2,1)S(1)}, bf16[256,512]{1,0:T(8,128)(2,1)S(1)}, u32[]{:S(2)}, u32[]{:S(2)}) %collective-permute-start) | collective-permute-done | bytes 262176 | tf_op jit(solution)/shard_map/ppermute | solution.py:82
  153.1 1.0 add_convert_fusion
  154.1 32.7 %reduce-scatter.5.cloned.1.call-done = bf16[256,512]{1,0:T(8,128)(2,1)} async-done(((bf16[2048,512]{1,0:T(8,128)(2,1)}), bf16[256,512]{1,0:T(8,128)(2,1)}) %reduce-scatter.5.cloned.1.call-update) | async-done | bytes 262160 | tf_op jit(solution)/shard_map/reduce_scatter | solution.py:84
  186.8 0.0 copy-done
  186.8 2.5 %fusion.2 = bf16[256,1024]{1,0:T(8,128)(2,1)} fusion(bf16[1024,1024]{1,0:T(8,128)(2,1)S(1)} %copy-done, bf16[256,512]{1,0:T(8,128)(2,1)} %reduce-scatter.5.cloned.1.call-done, bf16[256,512]{1,0:T(8,128)(2,1)S(1)} %add_convert_fusion, f32[1024]{0:T(1024)S(1)} %convert_element_type.34), kind=kOutput, calls=%fused_computation.5 | convolution fusion | flops 538705920 | bytes 3149824 | tf_op jit(solution)/shard_map/dot_general | solution.py:86
  (1 shorter events, 0.0 us)
Async XLA Ops:
  6.5 180.3 %copy-start = (bf16[1024,1024]{1,0:T(8,128)(2,1)S(1)}, bf16[1024,1024]{1,0:T(8,128)(2,1)}, u32[]{:S(2)}) copy-start(bf16[1024,1024]{1,0:T(8,128)(2,1)} %param.7) | copy-start | bytes 6291460
  6.5 60.1 %all-gather.2.cloned.1.call-start = ((), (), s32[]{:S(2)}) async-start(), calls=%async_computation.2 | async-start | bytes 8912896 | tf_op jit(solution)/shard_map/all_gather | solution.py:66
  7.3 135.7 %reduce-scatter.3.cloned.1.call-start = ((), (), s32[]{:S(2)}) async-start(), calls=%async_computation.3 | async-start | bytes 4718592 | tf_op jit(solution)/shard_map/reduce_scatter | solution.py:78
  66.7 0.7 copy-start.2
  84.0 1.9 copy-start.1
  85.9 100.9 %reduce-scatter.5.cloned.1.call-start = ((), (), s32[]{:S(2)}) async-start(), calls=%async_computation.4 | async-start | bytes 2359296 | tf_op jit(solution)/shard_map/reduce_scatter | solution.py:84
  89.0 49.6 %collective-permute-start.1 = (bf16[8,256,512]{2,1,0:T(8,128)(2,1)}, bf16[8,256,512]{2,1,0:T(8,128)(2,1)}, u32[]{:S(2)}, u32[]{:S(2)}) collective-permute-start(bf16[8,256,512]{2,1,0:T(8,128)(2,1)} %dynamic-slice_bitcast_fusion), channel_id=1, source_target_pairs={{0,8},{8,0},{1,9},{9,1},{2,10},{10,2},{3,11},{11,3},{4,12},{12,4},... | collective-permute-start | bytes 6291464 | tf_op jit(solution)/shard_map/ppermute | solution.py:75
  142.9 4.1 %copy-start.3 = (bf16[1024]{0:T(1024)(128)(2,1)S(1)}, bf16[1024]{0:T(1024)(128)(2,1)}, u32[]{:S(2)}) copy-start(bf16[1024]{0:T(1024)(128)(2,1)} %param.8) | copy-start | bytes 6148
  143.9 9.2 %collective-permute-start = (bf16[256,512]{1,0:T(8,128)(2,1)S(1)}, bf16[256,512]{1,0:T(8,128)(2,1)S(1)}, u32[]{:S(2)}, u32[]{:S(2)}) collective-permute-start(bf16[256,512]{1,0:T(8,128)(2,1)S(1)} %constant_dynamic-slice_fusion), channel_id=1, source_target_pairs={{0,8},{8,0},{1,9},{9,1},{2,10},{10,2},{3,11},{11,3},{4,12},{12,4},... | collective-permute-start | bytes 786440 | tf_op jit(solution)/shard_map/ppermute | solution.py:82
Sparse Core Ops, SparseCore 0:
  9.2 57.4 all-gather.1
  86.1 56.3 reduce-scatter.2
  145.0 41.8 reduce-scatter.4

commit v11 on v10

--- a/solution.py
+++ b/solution.py
@@ -6,16 +6,22 @@
 from jax.sharding import Mesh, PartitionSpec as P
 
 
-def sparse_partial(gathered, tiles, cols, counts, out_pos, group=2):
+def sparse_partial(gathered, tiles, cols, counts, hi, n_lo, out_pos, group=2):
     n_blocks, slots, side, _ = tiles.shape
     width = gathered.shape[1]
     n_src = gathered.shape[0]
     half = width // 2
 
-    def kernel(cols_ref, counts_ref, tile_ref, src_ref, out_a, out_b):
+    def dest(i, hi_ref):
+        h = hi_ref[0]
+        plane = jnp.where(i < n_lo, h, 1 - h)
+        return plane * n_lo + i % n_lo
+
+    def kernel(cols_ref, counts_ref, hi_ref, tile_ref, src_ref, out_a, out_bm, out_bt):
         step = pl.program_id(0)
+        j = dest(step, hi_ref)
         for g in range(group):
-            b = step * group + g
+            b = j * group + g
             live = counts_ref[b]
             lhs = jnp.concatenate(
                 [jnp.where(k < live, tile_ref[g, k], jnp.zeros_like(tile_ref[g, k])) for k in range(slots)],
@@ -29,29 +35,42 @@
                 axis=0,
             )
             prod = jnp.dot(lhs, rhs, preferred_element_type=jnp.float32).astype(out_a.dtype)
-            out_a[pl.ds(g * side, side), :] = prod[:, :half]
-            out_b[pl.ds(g * side, side), :] = prod[:, half:]
+            rows = pl.ds(g * side, side)
+            out_a[rows, :] = prod[:, :half]
+
+            @pl.when(step < n_lo)
+            def _():
+                out_bm[rows, :] = prod[:, half:]
+
+            @pl.when(step >= n_lo)
+            def _():
+                out_bt[rows, :] = prod[:, half:]
 
     grid_spec = pltpu.PrefetchScalarGridSpec(
-        num_scalar_prefetch=2,
+        num_scalar_prefetch=3,
         grid=(n_blocks // group,),
         in_specs=[
-            pl.BlockSpec((group, slots, side, side), lambda i, c, n: (i, 0, 0, 0)),
-            pl.BlockSpec((n_src, width), lambda i, c, n: (0, 0)),
+            pl.BlockSpec((group, slots, side, side), lambda i, c, n, h: (dest(i, h), 0, 0, 0)),
+            pl.BlockSpec((n_src, width), lambda i, c, n, h: (0, 0)),
         ],
         out_specs=[
-            pl.BlockSpec((group * side, half), lambda i, c, n: (out_pos(i * group) // group, 0)),
-            pl.BlockSpec((group * side, half), lambda i, c, n: (out_pos(i * group) // group, 0)),
+            pl.BlockSpec((group * side, half), lambda i, c, n, h: (out_pos(dest(i, h) * group) // group, 0)),
+            pl.BlockSpec((group * side, half), lambda i, c, n, h: (jnp.minimum(i, n_lo - 1), 0)),
+            pl.BlockSpec((group * side, half), lambda i, c, n, h: (jnp.maximum(i - n_lo, 0), 0)),
         ],
     )
     return pl.pallas_call(
         kernel,
         grid_spec=grid_spec,
-        out_shape=[jax.ShapeDtypeStruct((n_blocks * side, half), jnp.bfloat16)] * 2,
+        out_shape=[
+            jax.ShapeDtypeStruct((n_blocks * side, half), jnp.bfloat16),
+            jax.ShapeDtypeStruct((n_blocks * side // 2, half), jnp.bfloat16),
+            jax.ShapeDtypeStruct((n_blocks * side // 2, half), jnp.bfloat16),
+        ],
         compiler_params=pltpu.CompilerParams(
             dimension_semantics=("arbitrary",), vmem_limit_bytes=48 * 1024 * 1024
         ),
-    )(cols.reshape(-1), counts, tiles, gathered)
+    )(cols.reshape(-1), counts, hi.reshape(1), tiles, gathered)
 
 
 def body(features, weight, bias, tile_vals, tile_col, tile_count):
@@ -64,17 +83,13 @@
         return ((j % n_lo) * n_hi + j // n_lo) * per_dev + b % per_dev
 
     gathered = lax.all_gather(features, "rep", axis=0, tiled=True)
-    part_a, part_b = sparse_partial(
-        gathered, tile_vals[0, 0], tile_col[0, 0], tile_count[0, 0], out_pos, per_dev
-    )
     hi = lax.axis_index("yh")
     swap = [(0, 1), (1, 0)]
-    grid_b = part_b.reshape(n_lo, n_hi, -1, part_b.shape[1])
-    mine_b = lax.dynamic_index_in_dim(grid_b, hi, axis=1, keepdims=False)
-    theirs_b = lax.dynamic_index_in_dim(grid_b, 1 - hi, axis=1, keepdims=False)
+    part_a, mine_b, theirs_b = sparse_partial(
+        gathered, tile_vals[0, 0], tile_col[0, 0], tile_count[0, 0], hi.astype(jnp.int32), n_lo, out_pos, per_dev
+    )
     got_b = lax.ppermute(theirs_b, "yh", swap)
     sum_b = (mine_b.astype(jnp.float32) + got_b.astype(jnp.float32)).astype(jnp.bfloat16)
-    sum_b = sum_b.reshape(-1, part_b.shape[1])
     red_a = lax.psum_scatter(part_a, "z", scatter_dimension=0, tiled=True)
     rows = red_a.shape[0] // n_hi
     mine = lax.dynamic_slice_in_dim(red_a, hi * rows, rows, axis=0)

time: 196 us -> 199 us (1.015)
  waiting for transfers between devices: 145 us -> 148 us
  local copies, waits for them, and re-layouts: 7.51 us -> 5.14 us
  Pallas kernels: 16.6 us -> 18.6 us
    reduce_scatter x1, waiting for transfers between devices: 0.02 us -> 3.31 us  [body(): red_a = lax.psum_scatter(part_a, 'z', scatter_dimension=0, tiled=True)]
    squeeze x1 -> x0, local copies, waits for them, and re-layouts: 3.06 us -> none  [body(): theirs_b = lax.dynamic_index_in_dim(grid_b, 1 - hi, axis=1, keepdims=False)]
    unnamed x9 -> x11, local copies, waits for them, and re-layouts: 3.37 us -> 4.07 us
  transfers between devices with their start and end apart: 5 -> 5, of which waited for: 4 -> 5; matrix products, arithmetic and copies ran while one was open for 5% -> 3% of each run, Pallas kernels for 0% -> 0%
where the time goes in v11:
time: 199 us; the launch traced here: 198 us
  waiting for transfers between devices  148 us (74%)
  Pallas kernels  18.6 us (9%)
  between operations  13.1 us (7%)
  starting transfers between devices  6.25 us (3%)
  local copies, waits for them, and re-layouts  5.14 us (3%)
  other arithmetic  4.53 us (2%)
  matrix products  2.46 us (1%)
    all_gather x1, waiting for transfers between devices, body(): gathered = lax.all_gather(features, 'rep', axis=0, tiled=True)  58.5 us
    ppermute x1, waiting for transfers between devices, body(): got_b = lax.ppermute(theirs_b, 'yh', swap)  46.5 us
    reduce_scatter x1, waiting for transfers between devices, body(): out_b = lax.psum_scatter(sum_b, 'z', scatter_dimension=0, tiled=True)  32.5 us
    pallas_call x1, Pallas kernels, sparse_partial(): pl.pallas_call(kernel, grid_spec=grid_spec, out_shape=[jax.ShapeDtypeStru...  18.6 us
    ppermute x1, waiting for transfers between devices, body(): got = lax.ppermute(theirs, 'yh', swap)  6.49 us
    unnamed x11, local copies, waits for them, and re-layouts  4.07 us
  transfers between devices with their start and end apart: 5, of which 5 were waited for; matrix products, arithmetic and copies ran while one was open for 3% of the time, Pallas kernels for 0%

profile of v11, /device:TPU:2, one launch (start us, length us, event | category | flops | bytes accessed | tf_op | source)
XLA Modules:
  0.0 198.0 jit_solution(3418022041327135317)
XLA Ops:
  6.5 0.0 copy-start
  6.5 0.0 all-gather.2.cloned.1.call-start
  6.5 0.7 all-gather.2.cloned.1.call-update
  7.3 0.0 reduce-scatter.3.cloned.1.call-start
  7.3 0.8 copy.8
  8.1 0.1 reshape_squeeze.3.cols_ref
  8.2 58.5 %all-gather.2.cloned.1.call-done.src_ref = bf16[4096,1024]{1,0:T(8,128)(2,1)} async-done(((bf16[256,1024]{1,0:T(8,128)(2,1)}), bf16[4096,1024]{1,0:T(8,128)(2,1)}) %all-gather.2.cloned.1.call-update) | async-done | bytes 8388624 | tf_op jit(solution)/shard_map/all_gather | solution.py:85
  66.7 0.0 copy-start.2
  66.7 0.7 copy-done.2
  67.3 18.6 %shard_map.64 = (bf16[4096,512]{1,0:T(8,128)(2,1)}, bf16[2048,512]{1,0:T(8,128)(2,1)S(1)}, bf16[2048,512]{1,0:T(8,128)(2,1)S(1)}) custom-call(s32[128]{0:T(128)S(1)} %reshape_squeeze.3.cols_ref, s32[32]{0:T(128)S(1)} %bitcast.6, s32[1]{0:T(128)} %bitcast.1.hi_ref, bf16[32,4,128,128]{3,2,1,0:T(8,128)(2,1)} %bitcast.7, ...), custom_call_target="tpu_custom_call" | custom-call | tf_op jit(solution)/shard_map/pallas_call | solution.py:62
  85.9 0.0 copy-start.1
  85.9 1.3 copy-done.1
  87.2 0.0 copy-start.3
  87.2 1.3 copy-done.3
  88.5 0.0 reduce-scatter.3.cloned.1.call-update
  88.5 0.0 reduce-scatter.5.cloned.1.call-start
  88.6 3.1 %collective-permute-start.1 = (bf16[2048,512]{1,0:T(8,128)(2,1)}, bf16[2048,512]{1,0:T(8,128)(2,1)S(1)}, u32[]{:S(2)}, u32[]{:S(2)}) collective-permute-start(bf16[2048,512]{1,0:T(8,128)(2,1)} %copy-done.3), channel_id=1, source_target_pairs={{0,8},{8,0},{1,9},{9,1},{2,10},{10,2},{3,11},{11,3},{4,12},{12,4},... | collective-permute-start | bytes 6291464 | tf_op jit(solution)/shard_map/ppermute | solution.py:91
  91.7 46.5 %collective-permute-done.1 = bf16[2048,512]{1,0:T(8,128)(2,1)S(1)} collective-permute-done((bf16[2048,512]{1,0:T(8,128)(2,1)}, bf16[2048,512]{1,0:T(8,128)(2,1)S(1)}, u32[]{:S(2)}, u32[]{:S(2)}) %collective-permute-start.1) | collective-permute-done | bytes 2097184 | tf_op jit(solution)/shard_map/ppermute | solution.py:91
  138.1 3.5 %add_convert_fusion = bf16[2048,512]{1,0:T(8,128)(2,1)} fusion(bf16[2048,512]{1,0:T(8,128)(2,1)S(1)} %collective-permute-done.1, bf16[2048,512]{1,0:T(8,128)(2,1)} %copy-done.1), kind=kLoop, calls=%fused_computation | loop fusion | flops 4194304 | bytes 6291456 | tf_op jit(solution)/shard_map/convert_element_type | solution.py:92
  141.6 0.0 copy-start.4
  141.6 0.0 reduce-scatter.5.cloned.1.call-update
  141.7 3.3 %reduce-scatter.3.cloned.1.call-done = bf16[512,512]{1,0:T(8,128)(2,1)} async-done(((bf16[4096,512]{1,0:T(8,128)(2,1)}), bf16[512,512]{1,0:T(8,128)(2,1)}) %reduce-scatter.3.cloned.1.call-update) | async-done | bytes 524304 | tf_op jit(solution)/shard_map/reduce_scatter | solution.py:93
  145.0 1.0 constant_dynamic-slice_fusion
  146.0 3.1 %collective-permute-start = (bf16[256,512]{1,0:T(8,128)(2,1)S(1)}, bf16[256,512]{1,0:T(8,128)(2,1)S(1)}, u32[]{:S(2)}, u32[]{:S(2)}) collective-permute-start(bf16[256,512]{1,0:T(8,128)(2,1)S(1)} %constant_dynamic-slice_fusion), channel_id=1, source_target_pairs={{0,8},{8,0},{1,9},{9,1},{2,10},{10,2},{3,11},{11,3},{4,12},{12,4},... | collective-permute-start | bytes 786440 | tf_op jit(solution)/shard_map/ppermute | solution.py:97
  149.0 0.0 copy-done.4
  149.0 6.5 %collective-permute-done = bf16[256,512]{1,0:T(8,128)(2,1)S(1)} collective-permute-done((bf16[256,512]{1,0:T(8,128)(2,1)S(1)}, bf16[256,512]{1,0:T(8,128)(2,1)S(1)}, u32[]{:S(2)}, u32[]{:S(2)}) %collective-permute-start) | collective-permute-done | bytes 262176 | tf_op jit(solution)/shard_map/ppermute | solution.py:97
  155.5 1.0 add_convert_fusion.1
  156.6 32.5 %reduce-scatter.5.cloned.1.call-done = bf16[256,512]{1,0:T(8,128)(2,1)} async-done(((bf16[2048,512]{1,0:T(8,128)(2,1)}), bf16[256,512]{1,0:T(8,128)(2,1)}) %reduce-scatter.5.cloned.1.call-update) | async-done | bytes 262160 | tf_op jit(solution)/shard_map/reduce_scatter | solution.py:99
  189.0 0.0 copy-done
  189.0 2.5 %fusion.1 = bf16[256,1024]{1,0:T(8,128)(2,1)} fusion(bf16[1024,1024]{1,0:T(8,128)(2,1)S(1)} %copy-done, bf16[256,512]{1,0:T(8,128)(2,1)} %reduce-scatter.5.cloned.1.call-done, bf16[256,512]{1,0:T(8,128)(2,1)S(1)} %add_convert_fusion.1, f32[1024]{0:T(1024)S(1)} %convert_element_type.30), kind=kOutput, calls=%fused_computation.3 | convolution fusion | flops 538705920 | bytes 3149824 | tf_op jit(solution)/shard_map/dot_general | solution.py:101
  (1 shorter events, 0.0 us)
Async XLA Ops:
  6.5 182.5 %copy-start = (bf16[1024,1024]{1,0:T(8,128)(2,1)S(1)}, bf16[1024,1024]{1,0:T(8,128)(2,1)}, u32[]{:S(2)}) copy-start(bf16[1024,1024]{1,0:T(8,128)(2,1)} %param.7) | copy-start | bytes 6291460
  6.5 60.1 %all-gather.2.cloned.1.call-start = ((), (), s32[]{:S(2)}) async-start(), calls=%async_computation.2 | async-start | bytes 8912896 | tf_op jit(solution)/shard_map/all_gather | solution.py:85
  7.3 137.7 %reduce-scatter.3.cloned.1.call-start = ((), (), s32[]{:S(2)}) async-start(), calls=%async_computation.3 | async-start | bytes 4718592 | tf_op jit(solution)/shard_map/reduce_scatter | solution.py:93
  66.7 0.7 copy-start.2
  85.9 1.3 copy-start.1
  87.2 1.3 copy-start.3
  88.5 100.5 %reduce-scatter.5.cloned.1.call-start = ((), (), s32[]{:S(2)}) async-start(), calls=%async_computation.4 | async-start | bytes 2359296 | tf_op jit(solution)/shard_map/reduce_scatter | solution.py:99
  88.6 49.5 %collective-permute-start.1 = (bf16[2048,512]{1,0:T(8,128)(2,1)}, bf16[2048,512]{1,0:T(8,128)(2,1)S(1)}, u32[]{:S(2)}, u32[]{:S(2)}) collective-permute-start(bf16[2048,512]{1,0:T(8,128)(2,1)} %copy-done.3), channel_id=1, source_target_pairs={{0,8},{8,0},{1,9},{9,1},{2,10},{10,2},{3,11},{11,3},{4,12},{12,4},... | collective-permute-start | bytes 6291464 | tf_op jit(solution)/shard_map/ppermute | solution.py:91
  141.6 7.4 %copy-start.4 = (bf16[1024]{0:T(1024)(128)(2,1)S(1)}, bf16[1024]{0:T(1024)(128)(2,1)}, u32[]{:S(2)}) copy-start(bf16[1024]{0:T(1024)(128)(2,1)} %param.8) | copy-start | bytes 6148
  146.0 9.6 %collective-permute-start = (bf16[256,512]{1,0:T(8,128)(2,1)S(1)}, bf16[256,512]{1,0:T(8,128)(2,1)S(1)}, u32[]{:S(2)}, u32[]{:S(2)}) collective-permute-start(bf16[256,512]{1,0:T(8,128)(2,1)S(1)} %constant_dynamic-slice_fusion), channel_id=1, source_target_pairs={{0,8},{8,0},{1,9},{9,1},{2,10},{10,2},{3,11},{11,3},{4,12},{12,4},... | collective-permute-start | bytes 786440 | tf_op jit(solution)/shard_map/ppermute | solution.py:97
Sparse Core Ops, SparseCore 0:
  9.2 57.4 all-gather.1
  88.7 56.2 reduce-scatter.2
  147.5 41.4 reduce-scatter.4

commit v12 on v10

--- a/solution.py
+++ b/solution.py
@@ -12,8 +12,35 @@
     n_src = gathered.shape[0]
     half = width // 2
 
-    def kernel(cols_ref, counts_ref, tile_ref, src_ref, out_a, out_b):
+    n_steps = n_blocks // group
+    per_step = group * slots
+
+    def kernel(cols_ref, counts_ref, tile_ref, src_hbm, out_a, out_b, buf, sem):
         step = pl.program_id(0)
+
+        def copies(at, parity):
+            return [
+                pltpu.make_async_copy(
+                    src_hbm.at[pl.ds(pl.multiple_of(cols_ref[at * per_step + q] * side, side), side), :],
+                    buf.at[parity, q],
+                    sem.at[parity, q],
+                )
+                for q in range(per_step)
+            ]
+
+        @pl.when(step == 0)
+        def _():
+            for cp in copies(0, 0):
+                cp.start()
+
+        @pl.when(step + 1 < n_steps)
+        def _():
+            for cp in copies(step + 1, (step + 1) % 2):
+                cp.start()
+
+        parity = step % 2
+        for cp in copies(step, parity):
+            cp.wait()
         for g in range(group):
             b = step * group + g
             live = counts_ref[b]
@@ -21,13 +48,7 @@
                 [jnp.where(k < live, tile_ref[g, k], jnp.zeros_like(tile_ref[g, k])) for k in range(slots)],
                 axis=1,
             )
-            rhs = jnp.concatenate(
-                [
-                    src_ref[pl.ds(pl.multiple_of(cols_ref[b * slots + k] * side, side), side), :]
-                    for k in range(slots)
-                ],
-                axis=0,
-            )
+            rhs = jnp.concatenate([buf[parity, g * slots + k] for k in range(slots)], axis=0)
             prod = jnp.dot(lhs, rhs, preferred_element_type=jnp.float32).astype(out_a.dtype)
             out_a[pl.ds(g * side, side), :] = prod[:, :half]
             out_b[pl.ds(g * side, side), :] = prod[:, half:]
@@ -37,11 +58,15 @@
         grid=(n_blocks // group,),
         in_specs=[
             pl.BlockSpec((group, slots, side, side), lambda i, c, n: (i, 0, 0, 0)),
-            pl.BlockSpec((n_src, width), lambda i, c, n: (0, 0)),
+            pl.BlockSpec(memory_space=pl.ANY),
         ],
         out_specs=[
             pl.BlockSpec((group * side, half), lambda i, c, n: (out_pos(i * group) // group, 0)),
             pl.BlockSpec((group * side, half), lambda i, c, n: (out_pos(i * group) // group, 0)),
+        ],
+        scratch_shapes=[
+            pltpu.VMEM((2, per_step, side, width), gathered.dtype),
+            pltpu.SemaphoreType.DMA((2, per_step)),
         ],
     )
     return pl.pallas_call(

time: 196 us -> 202 us (1.031)
  Pallas kernels: 16.6 us -> 22.4 us
    pallas_call x1, Pallas kernels: 16.6 us -> 22.4 us  [sparse_partial(): pl.pallas_call(kernel, grid_spec=grid_spec, out_shape=[jax.ShapeDtypeStru...]
  transfers between devices with their start and end apart: 5 -> 5, of which waited for: 4 -> 5; matrix products, arithmetic and copies ran while one was open for 5% -> 5% of each run, Pallas kernels for 0% -> 0%
where the time goes in v12:
time: 202 us; the launch traced here: 201 us
  waiting for transfers between devices  144 us (71%)
  Pallas kernels  22.4 us (11%)
  between operations  13.1 us (6%)
  local copies, waits for them, and re-layouts  7.5 us (4%)
  starting transfers between devices  6.09 us (3%)
  other arithmetic  5.25 us (3%)
  matrix products  2.46 us (1%)
    all_gather x1, waiting for transfers between devices, body(): gathered = lax.all_gather(features, 'rep', axis=0, tiled=True)  58.5 us
    ppermute x1, waiting for transfers between devices, body(): got_b = lax.ppermute(theirs_b, 'yh', swap)  46.3 us
    reduce_scatter x1, waiting for transfers between devices, body(): out_b = lax.psum_scatter(sum_b, 'z', scatter_dimension=0, tiled=True)  32.5 us
    pallas_call x1, Pallas kernels, sparse_partial(): pl.pallas_call(kernel, grid_spec=grid_spec, out_shape=[jax.ShapeDtypeStru...  22.4 us
    ppermute x1, waiting for transfers between devices, body(): got = lax.ppermute(theirs, 'yh', swap)  6.29 us
    convert_element_type x1, other arithmetic, body(): (mine_b.astype(jnp.float32) + got_b.astype(jnp.float32)).astype(jnp.bfloa...  4.23 us
  transfers between devices with their start and end apart: 5, of which 5 were waited for; matrix products, arithmetic and copies ran while one was open for 5% of the time, Pallas kernels for 0%

profile of v12, /device:TPU:2, one launch (start us, length us, event | category | flops | bytes accessed | tf_op | source)
XLA Modules:
  0.0 201.2 jit_solution(11889458989989279646)
XLA Ops:
  6.5 0.0 copy-start
  6.5 0.0 all-gather.2.cloned.1.call-start
  6.5 0.7 all-gather.2.cloned.1.call-update
  7.3 0.0 reduce-scatter.3.cloned.1.call-start
  7.3 0.8 copy.8
  8.1 0.1 reshape_squeeze.3.cols_ref
  8.2 58.5 %all-gather.2.cloned.1.call-done.src_hbm = bf16[4096,1024]{1,0:T(8,128)(2,1)} async-done(((bf16[256,1024]{1,0:T(8,128)(2,1)}), bf16[4096,1024]{1,0:T(8,128)(2,1)}) %all-gather.2.cloned.1.call-update) | async-done | bytes 8388624 | tf_op jit(solution)/shard_map/all_gather | solution.py:91
  66.7 0.0 copy-start.2
  66.7 0.7 copy-done.2
  67.3 22.4 %shard_map.64 = (bf16[4096,512]{1,0:T(8,128)(2,1)S(1)}, bf16[4096,512]{1,0:T(8,128)(2,1)}) custom-call(s32[128]{0:T(128)S(1)} %reshape_squeeze.3.cols_ref, s32[32]{0:T(128)S(1)} %bitcast.12, bf16[32,4,128,128]{3,2,1,0:T(8,128)(2,1)} %bitcast.14, bf16[4096,1024]{1,0:T(8,128)(2,1)} %all-gather.2.cloned.1.call-done.src_hbm), custom_call_target="tpu_custom_call" | custom-call | tf_op jit(solution)/shard_map/pallas_call | solution.py:72
  89.7 0.0 copy-start.1
  89.7 1.9 copy-done.1
  91.7 0.0 reduce-scatter.3.cloned.1.call-update
  91.7 0.0 reduce-scatter.5.cloned.1.call-start
  91.8 3.1 %dynamic-slice_bitcast_fusion = bf16[8,256,512]{2,1,0:T(8,128)(2,1)} fusion(bf16[8,2,256,512]{3,2,1,0:T(8,128)(2,1)} %bitcast.15, s32[]{:T(128)S(6)} %select_n.16), kind=kLoop, calls=%fused_computation.2 | loop fusion | bytes 4194308 | tf_op jit(solution)/shard_map/jit(dynamic_index_in_dim)/squeeze | solution.py:99
  94.8 2.7 %collective-permute-start.1 = (bf16[8,256,512]{2,1,0:T(8,128)(2,1)}, bf16[8,256,512]{2,1,0:T(8,128)(2,1)}, u32[]{:S(2)}, u32[]{:S(2)}) collective-permute-start(bf16[8,256,512]{2,1,0:T(8,128)(2,1)} %dynamic-slice_bitcast_fusion), channel_id=1, source_target_pairs={{0,8},{8,0},{1,9},{9,1},{2,10},{10,2},{3,11},{11,3},{4,12},{12,4},... | collective-permute-start | bytes 6291464 | tf_op jit(solution)/shard_map/ppermute | solution.py:100
  97.5 46.3 %collective-permute-done.1 = bf16[8,256,512]{2,1,0:T(8,128)(2,1)} collective-permute-done((bf16[8,256,512]{2,1,0:T(8,128)(2,1)}, bf16[8,256,512]{2,1,0:T(8,128)(2,1)}, u32[]{:S(2)}, u32[]{:S(2)}) %collective-permute-start.1) | collective-permute-done | bytes 2097184 | tf_op jit(solution)/shard_map/ppermute | solution.py:100
  143.8 4.2 %fusion = bf16[8,256,512]{2,1,0:T(8,128)(2,1)} fusion(bf16[8,256,512]{2,1,0:T(8,128)(2,1)} %collective-permute-done.1, bf16[8,2,256,512]{3,2,1,0:T(8,128)(2,1)} %bitcast.16, s32[]{:T(128)S(6)} %select_n.15), kind=kLoop, calls=%fused_computation.1 | loop fusion | flops 4194304 | bytes 6291460 | tf_op jit(solution)/shard_map/convert_element_type | solution.py:101
  148.0 0.0 copy-start.3
  148.0 0.0 reduce-scatter.5.cloned.1.call-update
  148.1 0.1 reduce-scatter.3.cloned.1.call-done
  148.1 1.0 constant_dynamic-slice_fusion
  149.1 3.3 %collective-permute-start = (bf16[256,512]{1,0:T(8,128)(2,1)S(1)}, bf16[256,512]{1,0:T(8,128)(2,1)S(1)}, u32[]{:S(2)}, u32[]{:S(2)}) collective-permute-start(bf16[256,512]{1,0:T(8,128)(2,1)S(1)} %constant_dynamic-slice_fusion), channel_id=1, source_target_pairs={{0,8},{8,0},{1,9},{9,1},{2,10},{10,2},{3,11},{11,3},{4,12},{12,4},... | collective-permute-start | bytes 786440 | tf_op jit(solution)/shard_map/ppermute | solution.py:107
  152.4 0.0 copy-done.3
  152.4 6.3 %collective-permute-done = bf16[256,512]{1,0:T(8,128)(2,1)S(1)} collective-permute-done((bf16[256,512]{1,0:T(8,128)(2,1)S(1)}, bf16[256,512]{1,0:T(8,128)(2,1)S(1)}, u32[]{:S(2)}, u32[]{:S(2)}) %collective-permute-start) | collective-permute-done | bytes 262176 | tf_op jit(solution)/shard_map/ppermute | solution.py:107
  158.7 1.0 add_convert_fusion
  159.7 32.5 %reduce-scatter.5.cloned.1.call-done = bf16[256,512]{1,0:T(8,128)(2,1)} async-done(((bf16[2048,512]{1,0:T(8,128)(2,1)}), bf16[256,512]{1,0:T(8,128)(2,1)}) %reduce-scatter.5.cloned.1.call-update) | async-done | bytes 262160 | tf_op jit(solution)/shard_map/reduce_scatter | solution.py:109
  192.2 0.0 copy-done
  192.2 2.5 %fusion.2 = bf16[256,1024]{1,0:T(8,128)(2,1)} fusion(bf16[1024,1024]{1,0:T(8,128)(2,1)S(1)} %copy-done, bf16[256,512]{1,0:T(8,128)(2,1)} %reduce-scatter.5.cloned.1.call-done, bf16[256,512]{1,0:T(8,128)(2,1)S(1)} %add_convert_fusion, f32[1024]{0:T(1024)S(1)} %convert_element_type.34), kind=kOutput, calls=%fused_computation.5 | convolution fusion | flops 538705920 | bytes 3149824 | tf_op jit(solution)/shard_map/dot_general | solution.py:111
  (1 shorter events, 0.0 us)
Async XLA Ops:
  6.5 185.7 %copy-start = (bf16[1024,1024]{1,0:T(8,128)(2,1)S(1)}, bf16[1024,1024]{1,0:T(8,128)(2,1)}, u32[]{:S(2)}) copy-start(bf16[1024,1024]{1,0:T(8,128)(2,1)} %param.7) | copy-start | bytes 6291460
  6.5 60.1 %all-gather.2.cloned.1.call-start = ((), (), s32[]{:S(2)}) async-start(), calls=%async_computation.2 | async-start | bytes 8912896 | tf_op jit(solution)/shard_map/all_gather | solution.py:91
  7.3 140.9 %reduce-scatter.3.cloned.1.call-start = ((), (), s32[]{:S(2)}) async-start(), calls=%async_computation.3 | async-start | bytes 4718592 | tf_op jit(solution)/shard_map/reduce_scatter | solution.py:103
  66.7 0.7 copy-start.2
  89.7 1.9 copy-start.1
  91.7 100.5 %reduce-scatter.5.cloned.1.call-start = ((), (), s32[]{:S(2)}) async-start(), calls=%async_computation.4 | async-start | bytes 2359296 | tf_op jit(solution)/shard_map/reduce_scatter | solution.py:109
  94.8 49.0 %collective-permute-start.1 = (bf16[8,256,512]{2,1,0:T(8,128)(2,1)}, bf16[8,256,512]{2,1,0:T(8,128)(2,1)}, u32[]{:S(2)}, u32[]{:S(2)}) collective-permute-start(bf16[8,256,512]{2,1,0:T(8,128)(2,1)} %dynamic-slice_bitcast_fusion), channel_id=1, source_target_pairs={{0,8},{8,0},{1,9},{9,1},{2,10},{10,2},{3,11},{11,3},{4,12},{12,4},... | collective-permute-start | bytes 6291464 | tf_op jit(solution)/shard_map/ppermute | solution.py:100
  148.0 4.4 %copy-start.3 = (bf16[1024]{0:T(1024)(128)(2,1)S(1)}, bf16[1024]{0:T(1024)(128)(2,1)}, u32[]{:S(2)}) copy-start(bf16[1024]{0:T(1024)(128)(2,1)} %param.8) | copy-start | bytes 6148
  149.1 9.6 %collective-permute-start = (bf16[256,512]{1,0:T(8,128)(2,1)S(1)}, bf16[256,512]{1,0:T(8,128)(2,1)S(1)}, u32[]{:S(2)}, u32[]{:S(2)}) collective-permute-start(bf16[256,512]{1,0:T(8,128)(2,1)S(1)} %constant_dynamic-slice_fusion), channel_id=1, source_target_pairs={{0,8},{8,0},{1,9},{9,1},{2,10},{10,2},{3,11},{11,3},{4,12},{12,4},... | collective-permute-start | bytes 786440 | tf_op jit(solution)/shard_map/ppermute | solution.py:107
Sparse Core Ops, SparseCore 0:
  9.2 57.4 all-gather.1
  91.8 56.2 reduce-scatter.2
  150.7 41.4 reduce-scatter.4

commit v13 on v12

--- a/solution.py
+++ b/solution.py
@@ -20,38 +20,48 @@
 
         def copies(at, parity):
             return [
-                pltpu.make_async_copy(
-                    src_hbm.at[pl.ds(pl.multiple_of(cols_ref[at * per_step + q] * side, side), side), :],
-                    buf.at[parity, q],
-                    sem.at[parity, q],
+                (
+                    q % slots < counts_ref[at * group + q // slots],
+                    pltpu.make_async_copy(
+                        src_hbm.at[pl.ds(pl.multiple_of(cols_ref[at * per_step + q] * side, side), side), :],
+                        buf.at[parity, q],
+                        sem.at[parity, q],
+                    ),
                 )
                 for q in range(per_step)
             ]
 
+        def start_all(at, parity):
+            for live_q, cp in copies(at, parity):
+                pl.when(live_q)(cp.start)
+
         @pl.when(step == 0)
         def _():
-            for cp in copies(0, 0):
-                cp.start()
+            start_all(0, 0)
 
         @pl.when(step + 1 < n_steps)
         def _():
-            for cp in copies(step + 1, (step + 1) % 2):
-                cp.start()
+            start_all(step + 1, (step + 1) % 2)
 
         parity = step % 2
-        for cp in copies(step, parity):
-            cp.wait()
+        for live_q, cp in copies(step, parity):
+            pl.when(live_q)(cp.wait)
         for g in range(group):
             b = step * group + g
             live = counts_ref[b]
-            lhs = jnp.concatenate(
-                [jnp.where(k < live, tile_ref[g, k], jnp.zeros_like(tile_ref[g, k])) for k in range(slots)],
-                axis=1,
-            )
-            rhs = jnp.concatenate([buf[parity, g * slots + k] for k in range(slots)], axis=0)
-            prod = jnp.dot(lhs, rhs, preferred_element_type=jnp.float32).astype(out_a.dtype)
-            out_a[pl.ds(g * side, side), :] = prod[:, :half]
-            out_b[pl.ds(g * side, side), :] = prod[:, half:]
+            rows = pl.ds(g * side, side)
+            for n in range(slots + 1):
+                @pl.when(live == n)
+                def _(n=n, g=g, rows=rows):
+                    if n == 0:
+                        out_a[rows, :] = jnp.zeros((side, half), out_a.dtype)
+                        out_b[rows, :] = jnp.zeros((side, half), out_b.dtype)
+                        return
+                    lhs = jnp.concatenate([tile_ref[g, k] for k in range(n)], axis=1)
+                    rhs = jnp.concatenate([buf[parity, g * slots + k] for k in range(n)], axis=0)
+                    prod = jnp.dot(lhs, rhs, preferred_element_type=jnp.float32).astype(out_a.dtype)
+                    out_a[rows, :] = prod[:, :half]
+                    out_b[rows, :] = prod[:, half:]
 
     grid_spec = pltpu.PrefetchScalarGridSpec(
         num_scalar_prefetch=2,

time: 202 us -> 197 us (0.975)
  Pallas kernels: 22.4 us -> 16.1 us
  starting transfers between devices: 6.09 us -> 8.79 us
    pallas_call x1, Pallas kernels: 22.4 us -> 16.1 us  [sparse_partial(): pl.pallas_call(kernel, grid_spec=grid_spec, out_shape=[jax.ShapeDtypeStru...]
    ppermute x1, starting transfers between devices: 2.72 us -> 5.6 us  [body(): got_b = lax.ppermute(theirs_b, 'yh', swap)]
    ppermute x1, waiting for transfers between devices: 46.3 us -> 43.9 us  [body(): got_b = lax.ppermute(theirs_b, 'yh', swap)]
where the time goes in v13:
time: 197 us; the launch traced here: 196 us
  waiting for transfers between devices  143 us (73%)
  Pallas kernels  16.1 us (8%)
  between operations  13.1 us (7%)
  starting transfers between devices  8.79 us (4%)
  local copies, waits for them, and re-layouts  7.5 us (4%)
  other arithmetic  5.25 us (3%)
  matrix products  2.46 us (1%)
    all_gather x1, waiting for transfers between devices, body(): gathered = lax.all_gather(features, 'rep', axis=0, tiled=True)  58.5 us
    ppermute x1, waiting for transfers between devices, body(): got_b = lax.ppermute(theirs_b, 'yh', swap)  43.9 us
    reduce_scatter x1, waiting for transfers between devices, body(): out_b = lax.psum_scatter(sum_b, 'z', scatter_dimension=0, tiled=True)  32.5 us
    pallas_call x1, Pallas kernels, sparse_partial(): pl.pallas_call(kernel, grid_spec=grid_spec, out_shape=[jax.ShapeDtypeStru...  16.1 us
    ppermute x1, waiting for transfers between devices, body(): got = lax.ppermute(theirs, 'yh', swap)  6.46 us
    ppermute x1, starting transfers between devices, body(): got_b = lax.ppermute(theirs_b, 'yh', swap)  5.6 us
    convert_element_type x1, other arithmetic, body(): (mine_b.astype(jnp.float32) + got_b.astype(jnp.float32)).astype(jnp.bfloa...  4.23 us
  transfers between devices with their start and end apart: 5, of which 5 were waited for; matrix products, arithmetic and copies ran while one was open for 5% of the time, Pallas kernels for 0%

profile of v13, /device:TPU:2, one launch (start us, length us, event | category | flops | bytes accessed | tf_op | source)
XLA Modules:
  0.0 196.5 jit_solution(3274005457660091075)
XLA Ops:
  6.5 0.0 copy-start
  6.5 0.0 all-gather.2.cloned.1.call-start
  6.5 0.7 all-gather.2.cloned.1.call-update
  7.3 0.0 reduce-scatter.3.cloned.1.call-start
  7.3 0.8 copy.8
  8.1 0.1 reshape_squeeze.3.cols_ref
  8.2 58.5 %all-gather.2.cloned.1.call-done.src_hbm = bf16[4096,1024]{1,0:T(8,128)(2,1)} async-done(((bf16[256,1024]{1,0:T(8,128)(2,1)}), bf16[4096,1024]{1,0:T(8,128)(2,1)}) %all-gather.2.cloned.1.call-update) | async-done | bytes 8388624 | tf_op jit(solution)/shard_map/all_gather | solution.py:101
  66.7 0.0 copy-start.2
  66.7 0.7 copy-done.2
  67.3 16.1 %shard_map.64 = (bf16[4096,512]{1,0:T(8,128)(2,1)S(1)}, bf16[4096,512]{1,0:T(8,128)(2,1)}) custom-call(s32[128]{0:T(128)S(1)} %reshape_squeeze.3.cols_ref, s32[32]{0:T(128)S(1)} %bitcast.12, bf16[32,4,128,128]{3,2,1,0:T(8,128)(2,1)} %bitcast.14, bf16[4096,1024]{1,0:T(8,128)(2,1)} %all-gather.2.cloned.1.call-done.src_hbm), custom_call_target="tpu_custom_call" | custom-call | tf_op jit(solution)/shard_map/pallas_call | solution.py:82
  83.4 0.0 copy-start.1
  83.4 1.9 copy-done.1
  85.3 0.0 reduce-scatter.3.cloned.1.call-update
  85.4 0.0 reduce-scatter.5.cloned.1.call-start
  85.4 3.1 %dynamic-slice_bitcast_fusion = bf16[8,256,512]{2,1,0:T(8,128)(2,1)} fusion(bf16[8,2,256,512]{3,2,1,0:T(8,128)(2,1)} %bitcast.15, s32[]{:T(128)S(6)} %select_n.16), kind=kLoop, calls=%fused_computation.2 | loop fusion | bytes 4194308 | tf_op jit(solution)/shard_map/jit(dynamic_index_in_dim)/squeeze | solution.py:109
  88.5 5.6 %collective-permute-start.1 = (bf16[8,256,512]{2,1,0:T(8,128)(2,1)}, bf16[8,256,512]{2,1,0:T(8,128)(2,1)}, u32[]{:S(2)}, u32[]{:S(2)}) collective-permute-start(bf16[8,256,512]{2,1,0:T(8,128)(2,1)} %dynamic-slice_bitcast_fusion), channel_id=1, source_target_pairs={{0,8},{8,0},{1,9},{9,1},{2,10},{10,2},{3,11},{11,3},{4,12},{12,4},... | collective-permute-start | bytes 6291464 | tf_op jit(solution)/shard_map/ppermute | solution.py:110
  94.1 43.9 %collective-permute-done.1 = bf16[8,256,512]{2,1,0:T(8,128)(2,1)} collective-permute-done((bf16[8,256,512]{2,1,0:T(8,128)(2,1)}, bf16[8,256,512]{2,1,0:T(8,128)(2,1)}, u32[]{:S(2)}, u32[]{:S(2)}) %collective-permute-start.1) | collective-permute-done | bytes 2097184 | tf_op jit(solution)/shard_map/ppermute | solution.py:110
  138.0 4.2 %fusion = bf16[8,256,512]{2,1,0:T(8,128)(2,1)} fusion(bf16[8,256,512]{2,1,0:T(8,128)(2,1)} %collective-permute-done.1, bf16[8,2,256,512]{3,2,1,0:T(8,128)(2,1)} %bitcast.16, s32[]{:T(128)S(6)} %select_n.15), kind=kLoop, calls=%fused_computation.1 | loop fusion | flops 4194304 | bytes 6291460 | tf_op jit(solution)/shard_map/convert_element_type | solution.py:111
  142.2 0.0 copy-start.3
  142.3 0.0 reduce-scatter.5.cloned.1.call-update
  142.3 1.2 reduce-scatter.3.cloned.1.call-done
  143.5 1.0 constant_dynamic-slice_fusion
  144.4 3.1 %collective-permute-start = (bf16[256,512]{1,0:T(8,128)(2,1)S(1)}, bf16[256,512]{1,0:T(8,128)(2,1)S(1)}, u32[]{:S(2)}, u32[]{:S(2)}) collective-permute-start(bf16[256,512]{1,0:T(8,128)(2,1)S(1)} %constant_dynamic-slice_fusion), channel_id=1, source_target_pairs={{0,8},{8,0},{1,9},{9,1},{2,10},{10,2},{3,11},{11,3},{4,12},{12,4},... | collective-permute-start | bytes 786440 | tf_op jit(solution)/shard_map/ppermute | solution.py:117
  147.6 0.0 copy-done.3
  147.6 6.5 %collective-permute-done = bf16[256,512]{1,0:T(8,128)(2,1)S(1)} collective-permute-done((bf16[256,512]{1,0:T(8,128)(2,1)S(1)}, bf16[256,512]{1,0:T(8,128)(2,1)S(1)}, u32[]{:S(2)}, u32[]{:S(2)}) %collective-permute-start) | collective-permute-done | bytes 262176 | tf_op jit(solution)/shard_map/ppermute | solution.py:117
  154.0 1.0 add_convert_fusion
  155.0 32.5 %reduce-scatter.5.cloned.1.call-done = bf16[256,512]{1,0:T(8,128)(2,1)} async-done(((bf16[2048,512]{1,0:T(8,128)(2,1)}), bf16[256,512]{1,0:T(8,128)(2,1)}) %reduce-scatter.5.cloned.1.call-update) | async-done | bytes 262160 | tf_op jit(solution)/shard_map/reduce_scatter | solution.py:119
  187.5 0.0 copy-done
  187.5 2.5 %fusion.2 = bf16[256,1024]{1,0:T(8,128)(2,1)} fusion(bf16[1024,1024]{1,0:T(8,128)(2,1)S(1)} %copy-done, bf16[256,512]{1,0:T(8,128)(2,1)} %reduce-scatter.5.cloned.1.call-done, bf16[256,512]{1,0:T(8,128)(2,1)S(1)} %add_convert_fusion, f32[1024]{0:T(1024)S(1)} %convert_element_type.34), kind=kOutput, calls=%fused_computation.5 | convolution fusion | flops 538705920 | bytes 3149824 | tf_op jit(solution)/shard_map/dot_general | solution.py:121
  (1 shorter events, 0.0 us)
Async XLA Ops:
  6.5 181.0 %copy-start = (bf16[1024,1024]{1,0:T(8,128)(2,1)S(1)}, bf16[1024,1024]{1,0:T(8,128)(2,1)}, u32[]{:S(2)}) copy-start(bf16[1024,1024]{1,0:T(8,128)(2,1)} %param.7) | copy-start | bytes 6291460
  6.5 60.1 %all-gather.2.cloned.1.call-start = ((), (), s32[]{:S(2)}) async-start(), calls=%async_computation.2 | async-start | bytes 8912896 | tf_op jit(solution)/shard_map/all_gather | solution.py:101
  7.3 136.2 %reduce-scatter.3.cloned.1.call-start = ((), (), s32[]{:S(2)}) async-start(), calls=%async_computation.3 | async-start | bytes 4718592 | tf_op jit(solution)/shard_map/reduce_scatter | solution.py:113
  66.7 0.7 copy-start.2
  83.4 1.9 copy-start.1
  85.4 102.1 %reduce-scatter.5.cloned.1.call-start = ((), (), s32[]{:S(2)}) async-start(), calls=%async_computation.4 | async-start | bytes 2359296 | tf_op jit(solution)/shard_map/reduce_scatter | solution.py:119
  88.5 49.5 %collective-permute-start.1 = (bf16[8,256,512]{2,1,0:T(8,128)(2,1)}, bf16[8,256,512]{2,1,0:T(8,128)(2,1)}, u32[]{:S(2)}, u32[]{:S(2)}) collective-permute-start(bf16[8,256,512]{2,1,0:T(8,128)(2,1)} %dynamic-slice_bitcast_fusion), channel_id=1, source_target_pairs={{0,8},{8,0},{1,9},{9,1},{2,10},{10,2},{3,11},{11,3},{4,12},{12,4},... | collective-permute-start | bytes 6291464 | tf_op jit(solution)/shard_map/ppermute | solution.py:110
  142.2 5.3 %copy-start.3 = (bf16[1024]{0:T(1024)(128)(2,1)S(1)}, bf16[1024]{0:T(1024)(128)(2,1)}, u32[]{:S(2)}) copy-start(bf16[1024]{0:T(1024)(128)(2,1)} %param.8) | copy-start | bytes 6148
  144.4 9.6 %collective-permute-start = (bf16[256,512]{1,0:T(8,128)(2,1)S(1)}, bf16[256,512]{1,0:T(8,128)(2,1)S(1)}, u32[]{:S(2)}, u32[]{:S(2)}) collective-permute-start(bf16[256,512]{1,0:T(8,128)(2,1)S(1)} %constant_dynamic-slice_fusion), channel_id=1, source_target_pairs={{0,8},{8,0},{1,9},{9,1},{2,10},{10,2},{3,11},{11,3},{4,12},{12,4},... | collective-permute-start | bytes 786440 | tf_op jit(solution)/shard_map/ppermute | solution.py:117
Sparse Core Ops, SparseCore 0:
  9.2 57.4 all-gather.1
  85.5 57.9 reduce-scatter.2
  146.0 41.4 reduce-scatter.4

commit v14 on v10

--- a/solution.py
+++ b/solution.py
@@ -6,42 +6,47 @@
 from jax.sharding import Mesh, PartitionSpec as P
 
 
-def sparse_partial(gathered, tiles, cols, counts, out_pos, group=2):
+def sparse_partial(gathered, tiles, cols, counts, n_hi, n_lo, group=2):
     n_blocks, slots, side, _ = tiles.shape
     width = gathered.shape[1]
     n_src = gathered.shape[0]
     half = width // 2
 
-    def kernel(cols_ref, counts_ref, tile_ref, src_ref, out_a, out_b):
-        step = pl.program_id(0)
-        for g in range(group):
-            b = step * group + g
-            live = counts_ref[b]
-            lhs = jnp.concatenate(
-                [jnp.where(k < live, tile_ref[g, k], jnp.zeros_like(tile_ref[g, k])) for k in range(slots)],
-                axis=1,
-            )
-            rhs = jnp.concatenate(
-                [
-                    src_ref[pl.ds(pl.multiple_of(cols_ref[b * slots + k] * side, side), side), :]
-                    for k in range(slots)
-                ],
-                axis=0,
-            )
-            prod = jnp.dot(lhs, rhs, preferred_element_type=jnp.float32).astype(out_a.dtype)
-            out_a[pl.ds(g * side, side), :] = prod[:, :half]
-            out_b[pl.ds(g * side, side), :] = prod[:, half:]
+    def kernel(cols_ref, counts_ref, *refs):
+        tile_refs = refs[:n_hi]
+        src_ref, out_a, out_b = refs[n_hi:]
+        lo = pl.program_id(0)
+        for hh in range(n_hi):
+            for g in range(group):
+                b = (hh * n_lo + lo) * group + g
+                live = counts_ref[b]
+                tref = tile_refs[hh]
+                lhs = jnp.concatenate(
+                    [jnp.where(k < live, tref[g, k], jnp.zeros_like(tref[g, k])) for k in range(slots)],
+                    axis=1,
+                )
+                rhs = jnp.concatenate(
+                    [
+                        src_ref[pl.ds(pl.multiple_of(cols_ref[b * slots + k] * side, side), side), :]
+                        for k in range(slots)
+                    ],
+                    axis=0,
+                )
+                prod = jnp.dot(lhs, rhs, preferred_element_type=jnp.float32).astype(out_a.dtype)
+                rows = pl.ds((hh * group + g) * side, side)
+                out_a[rows, :] = prod[:, :half]
+                out_b[rows, :] = prod[:, half:]
+
+    def tile_spec(hh):
+        return pl.BlockSpec((group, slots, side, side), lambda i, c, n: (hh * n_lo + i, 0, 0, 0))
 
     grid_spec = pltpu.PrefetchScalarGridSpec(
         num_scalar_prefetch=2,
-        grid=(n_blocks // group,),
-        in_specs=[
-            pl.BlockSpec((group, slots, side, side), lambda i, c, n: (i, 0, 0, 0)),
-            pl.BlockSpec((n_src, width), lambda i, c, n: (0, 0)),
-        ],
+        grid=(n_lo,),
+        in_specs=[tile_spec(hh) for hh in range(n_hi)] + [pl.BlockSpec((n_src, width), lambda i, c, n: (0, 0))],
         out_specs=[
-            pl.BlockSpec((group * side, half), lambda i, c, n: (out_pos(i * group) // group, 0)),
-            pl.BlockSpec((group * side, half), lambda i, c, n: (out_pos(i * group) // group, 0)),
+            pl.BlockSpec((n_hi * group * side, half), lambda i, c, n: (i, 0)),
+            pl.BlockSpec((n_hi * group * side, half), lambda i, c, n: (i, 0)),
         ],
     )
     return pl.pallas_call(
@@ -51,7 +56,7 @@
         compiler_params=pltpu.CompilerParams(
             dimension_semantics=("arbitrary",), vmem_limit_bytes=48 * 1024 * 1024
         ),
-    )(cols.reshape(-1), counts, tiles, gathered)
+    )(cols.reshape(-1), counts, *([tiles] * n_hi), gathered)
 
 
 def body(features, weight, bias, tile_vals, tile_col, tile_count):
@@ -65,7 +70,7 @@
 
     gathered = lax.all_gather(features, "rep", axis=0, tiled=True)
     part_a, part_b = sparse_partial(
-        gathered, tile_vals[0, 0], tile_col[0, 0], tile_count[0, 0], out_pos, per_dev
+        gathered, tile_vals[0, 0], tile_col[0, 0], tile_count[0, 0], n_hi, n_lo, per_dev
     )
     hi = lax.axis_index("yh")
     swap = [(0, 1), (1, 0)]

time: 196 us -> 192 us (0.980)
  Pallas kernels: 16.6 us -> 12.4 us
    pallas_call x1, Pallas kernels: 16.6 us -> 12.4 us  [sparse_partial(): pl.pallas_call(kernel, grid_spec=grid_spec, out_shape=[jax.ShapeDtypeStru...]
where the time goes in v14:
time: 192 us
  waiting for transfers between devices  145 us (76%)
  between operations  13.1 us (7%)
  Pallas kernels  12.4 us (6%)
  local copies, waits for them, and re-layouts  7.51 us (4%)
  starting transfers between devices  6.18 us (3%)
  other arithmetic  5.26 us (3%)
  matrix products  2.46 us (1%)
    all_gather x1, waiting for transfers between devices, body(): gathered = lax.all_gather(features, 'rep', axis=0, tiled=True)  58.5 us
    ppermute x1, waiting for transfers between devices, body(): got_b = lax.ppermute(theirs_b, 'yh', swap)  46.6 us
    reduce_scatter x1, waiting for transfers between devices, body(): out_b = lax.psum_scatter(sum_b, 'z', scatter_dimension=0, tiled=True)  32.8 us
    pallas_call x1, Pallas kernels, sparse_partial(): pl.pallas_call(kernel, grid_spec=grid_spec, out_shape=[jax.ShapeDtypeStru...  12.4 us
    ppermute x1, waiting for transfers between devices, body(): got = lax.ppermute(theirs, 'yh', swap)  6.07 us
    convert_element_type x1, other arithmetic, body(): (mine_b.astype(jnp.float32) + got_b.astype(jnp.float32)).astype(jnp.bfloa...  4.24 us
  transfers between devices with their start and end apart: 5, of which 4 were waited for; matrix products, arithmetic and copies ran while one was open for 5% of the time, Pallas kernels for 0%

profile of v14, /device:TPU:2, one launch (start us, length us, event | category | flops | bytes accessed | tf_op | source)
XLA Modules:
  0.0 191.7 jit_solution(4004642876324929246)
XLA Ops:
  6.5 0.0 copy-start
  6.5 0.0 all-gather.2.cloned.1.call-start
  6.5 0.7 all-gather.2.cloned.1.call-update
  7.3 0.0 reduce-scatter.3.cloned.1.call-start
  7.3 0.8 copy.8
  8.1 0.1 reshape_squeeze.3.cols_ref
  8.2 58.5 %all-gather.2.cloned.1.call-done.refs_2_ = bf16[4096,1024]{1,0:T(8,128)(2,1)} async-done(((bf16[256,1024]{1,0:T(8,128)(2,1)}), bf16[4096,1024]{1,0:T(8,128)(2,1)}) %all-gather.2.cloned.1.call-update) | async-done | bytes 8388624 | tf_op jit(solution)/shard_map/all_gather | solution.py:71
  66.7 0.0 copy-start.2
  66.7 0.7 copy-done.2
  67.3 12.4 %shard_map.64 = (bf16[4096,512]{1,0:T(8,128)(2,1)S(1)}, bf16[4096,512]{1,0:T(8,128)(2,1)}) custom-call(s32[128]{0:T(128)S(1)} %reshape_squeeze.3.cols_ref, s32[32]{0:T(128)S(1)} %bitcast.12, bf16[32,4,128,128]{3,2,1,0:T(8,128)(2,1)} %bitcast.13, bf16[32,4,128,128]{3,2,1,0:T(8,128)(2,1)} %bitcast.14, bf16[4096,1024]{1,0:T(8,128)(2,1)} %all-gather.2.cloned.1.call-done.refs_2_), custom_call_target="tpu_custom_call" | custom-call | tf_op jit(solution)/shard_map/pallas_call | solution.py:52
  79.8 0.0 copy-start.1
  79.8 1.9 %copy-done.1 = bf16[4096,512]{1,0:T(8,128)(2,1)} copy-done((bf16[4096,512]{1,0:T(8,128)(2,1)}, bf16[4096,512]{1,0:T(8,128)(2,1)S(1)}, u32[]{:S(2)}) %copy-start.1) | copy-done | bytes 4194328
  81.7 0.0 reduce-scatter.3.cloned.1.call-update
  81.7 0.0 reduce-scatter.5.cloned.1.call-start
  81.8 3.1 %dynamic-slice_bitcast_fusion = bf16[8,256,512]{2,1,0:T(8,128)(2,1)} fusion(bf16[8,2,256,512]{3,2,1,0:T(8,128)(2,1)} %bitcast.16, s32[]{:T(128)S(6)} %select_n.16), kind=kLoop, calls=%fused_computation.2 | loop fusion | bytes 4194308 | tf_op jit(solution)/shard_map/jit(dynamic_index_in_dim)/squeeze | solution.py:79
  84.8 3.0 %collective-permute-start.1 = (bf16[8,256,512]{2,1,0:T(8,128)(2,1)}, bf16[8,256,512]{2,1,0:T(8,128)(2,1)}, u32[]{:S(2)}, u32[]{:S(2)}) collective-permute-start(bf16[8,256,512]{2,1,0:T(8,128)(2,1)} %dynamic-slice_bitcast_fusion), channel_id=1, source_target_pairs={{0,8},{8,0},{1,9},{9,1},{2,10},{10,2},{3,11},{11,3},{4,12},{12,4},... | collective-permute-start | bytes 6291464 | tf_op jit(solution)/shard_map/ppermute | solution.py:80
  87.9 46.6 %collective-permute-done.1 = bf16[8,256,512]{2,1,0:T(8,128)(2,1)} collective-permute-done((bf16[8,256,512]{2,1,0:T(8,128)(2,1)}, bf16[8,256,512]{2,1,0:T(8,128)(2,1)}, u32[]{:S(2)}, u32[]{:S(2)}) %collective-permute-start.1) | collective-permute-done | bytes 2097184 | tf_op jit(solution)/shard_map/ppermute | solution.py:80
  134.4 4.2 %fusion = bf16[8,256,512]{2,1,0:T(8,128)(2,1)} fusion(bf16[8,256,512]{2,1,0:T(8,128)(2,1)} %collective-permute-done.1, bf16[8,2,256,512]{3,2,1,0:T(8,128)(2,1)} %bitcast.17, s32[]{:T(128)S(6)} %select_n.15), kind=kLoop, calls=%fused_computation.1 | loop fusion | flops 4194304 | bytes 6291460 | tf_op jit(solution)/shard_map/convert_element_type | solution.py:81
  138.7 0.0 copy-start.3
  138.7 0.0 reduce-scatter.5.cloned.1.call-update
  138.7 0.0 reduce-scatter.3.cloned.1.call-done
  138.7 1.0 constant_dynamic-slice_fusion
  139.7 3.1 %collective-permute-start = (bf16[256,512]{1,0:T(8,128)(2,1)S(1)}, bf16[256,512]{1,0:T(8,128)(2,1)S(1)}, u32[]{:S(2)}, u32[]{:S(2)}) collective-permute-start(bf16[256,512]{1,0:T(8,128)(2,1)S(1)} %constant_dynamic-slice_fusion), channel_id=1, source_target_pairs={{0,8},{8,0},{1,9},{9,1},{2,10},{10,2},{3,11},{11,3},{4,12},{12,4},... | collective-permute-start | bytes 786440 | tf_op jit(solution)/shard_map/ppermute | solution.py:87
  142.8 0.0 copy-done.3
  142.8 6.1 %collective-permute-done = bf16[256,512]{1,0:T(8,128)(2,1)S(1)} collective-permute-done((bf16[256,512]{1,0:T(8,128)(2,1)S(1)}, bf16[256,512]{1,0:T(8,128)(2,1)S(1)}, u32[]{:S(2)}, u32[]{:S(2)}) %collective-permute-start) | collective-permute-done | bytes 262176 | tf_op jit(solution)/shard_map/ppermute | solution.py:87
  148.9 1.0 add_convert_fusion
  149.9 32.8 %reduce-scatter.5.cloned.1.call-done = bf16[256,512]{1,0:T(8,128)(2,1)} async-done(((bf16[2048,512]{1,0:T(8,128)(2,1)}), bf16[256,512]{1,0:T(8,128)(2,1)}) %reduce-scatter.5.cloned.1.call-update) | async-done | bytes 262160 | tf_op jit(solution)/shard_map/reduce_scatter | solution.py:89
  182.7 0.0 copy-done
  182.7 2.5 %fusion.2 = bf16[256,1024]{1,0:T(8,128)(2,1)} fusion(bf16[1024,1024]{1,0:T(8,128)(2,1)S(1)} %copy-done, bf16[256,512]{1,0:T(8,128)(2,1)} %reduce-scatter.5.cloned.1.call-done, bf16[256,512]{1,0:T(8,128)(2,1)S(1)} %add_convert_fusion, f32[1024]{0:T(1024)S(1)} %convert_element_type.34), kind=kOutput, calls=%fused_computation.5 | convolution fusion | flops 538705920 | bytes 3149824 | tf_op jit(solution)/shard_map/dot_general | solution.py:91
  (1 shorter events, 0.0 us)
Async XLA Ops:
  6.5 176.2 %copy-start = (bf16[1024,1024]{1,0:T(8,128)(2,1)S(1)}, bf16[1024,1024]{1,0:T(8,128)(2,1)}, u32[]{:S(2)}) copy-start(bf16[1024,1024]{1,0:T(8,128)(2,1)} %param.7) | copy-start | bytes 6291460
  6.5 60.1 %all-gather.2.cloned.1.call-start = ((), (), s32[]{:S(2)}) async-start(), calls=%async_computation.2 | async-start | bytes 8912896 | tf_op jit(solution)/shard_map/all_gather | solution.py:71
  7.3 131.5 %reduce-scatter.3.cloned.1.call-start = ((), (), s32[]{:S(2)}) async-start(), calls=%async_computation.3 | async-start | bytes 4718592 | tf_op jit(solution)/shard_map/reduce_scatter | solution.py:83
  66.7 0.7 copy-start.2
  79.8 1.9 %copy-start.1 = (bf16[4096,512]{1,0:T(8,128)(2,1)}, bf16[4096,512]{1,0:T(8,128)(2,1)S(1)}, u32[]{:S(2)}) copy-start(bf16[4096,512]{1,0:T(8,128)(2,1)S(1)} %get-tuple-element.7) | copy-start | bytes 12582916
  81.7 101.0 %reduce-scatter.5.cloned.1.call-start = ((), (), s32[]{:S(2)}) async-start(), calls=%async_computation.4 | async-start | bytes 2359296 | tf_op jit(solution)/shard_map/reduce_scatter | solution.py:89
  84.8 49.6 %collective-permute-start.1 = (bf16[8,256,512]{2,1,0:T(8,128)(2,1)}, bf16[8,256,512]{2,1,0:T(8,128)(2,1)}, u32[]{:S(2)}, u32[]{:S(2)}) collective-permute-start(bf16[8,256,512]{2,1,0:T(8,128)(2,1)} %dynamic-slice_bitcast_fusion), channel_id=1, source_target_pairs={{0,8},{8,0},{1,9},{9,1},{2,10},{10,2},{3,11},{11,3},{4,12},{12,4},... | collective-permute-start | bytes 6291464 | tf_op jit(solution)/shard_map/ppermute | solution.py:80
  138.7 4.1 %copy-start.3 = (bf16[1024]{0:T(1024)(128)(2,1)S(1)}, bf16[1024]{0:T(1024)(128)(2,1)}, u32[]{:S(2)}) copy-start(bf16[1024]{0:T(1024)(128)(2,1)} %param.8) | copy-start | bytes 6148
  139.7 9.2 %collective-permute-start = (bf16[256,512]{1,0:T(8,128)(2,1)S(1)}, bf16[256,512]{1,0:T(8,128)(2,1)S(1)}, u32[]{:S(2)}, u32[]{:S(2)}) collective-permute-start(bf16[256,512]{1,0:T(8,128)(2,1)S(1)} %constant_dynamic-slice_fusion), channel_id=1, source_target_pairs={{0,8},{8,0},{1,9},{9,1},{2,10},{10,2},{3,11},{11,3},{4,12},{12,4},... | collective-permute-start | bytes 786440 | tf_op jit(solution)/shard_map/ppermute | solution.py:87
Sparse Core Ops, SparseCore 0:
  9.2 57.4 all-gather.1
  81.8 56.3 reduce-scatter.2
  140.8 41.8 reduce-scatter.4

commit v15 on v14

--- a/solution.py
+++ b/solution.py
@@ -6,21 +6,22 @@
 from jax.sharding import Mesh, PartitionSpec as P
 
 
-def sparse_partial(gathered, tiles, cols, counts, n_hi, n_lo, group=2):
+def sparse_partial(gathered, tiles, cols, counts, n_hi, n_lo, group=2, lo_step=2):
     n_blocks, slots, side, _ = tiles.shape
     width = gathered.shape[1]
     n_src = gathered.shape[0]
     half = width // 2
 
     def kernel(cols_ref, counts_ref, *refs):
-        tile_refs = refs[:n_hi]
-        src_ref, out_a, out_b = refs[n_hi:]
-        lo = pl.program_id(0)
-        for hh in range(n_hi):
+        tile_refs = refs[: n_hi * lo_step]
+        src_ref, out_a, out_b = refs[n_hi * lo_step:]
+        step = pl.program_id(0)
+        for l in range(lo_step):
+          for hh in range(n_hi):
             for g in range(group):
-                b = (hh * n_lo + lo) * group + g
+                b = (hh * n_lo + step * lo_step + l) * group + g
                 live = counts_ref[b]
-                tref = tile_refs[hh]
+                tref = tile_refs[l * n_hi + hh]
                 lhs = jnp.concatenate(
                     [jnp.where(k < live, tref[g, k], jnp.zeros_like(tref[g, k])) for k in range(slots)],
                     axis=1,
@@ -33,20 +34,20 @@
                     axis=0,
                 )
                 prod = jnp.dot(lhs, rhs, preferred_element_type=jnp.float32).astype(out_a.dtype)
-                rows = pl.ds((hh * group + g) * side, side)
+                rows = pl.ds(((l * n_hi + hh) * group + g) * side, side)
                 out_a[rows, :] = prod[:, :half]
                 out_b[rows, :] = prod[:, half:]
 
-    def tile_spec(hh):
-        return pl.BlockSpec((group, slots, side, side), lambda i, c, n: (hh * n_lo + i, 0, 0, 0))
+    def tile_spec(l, hh):
+        return pl.BlockSpec((group, slots, side, side), lambda i, c, n: (hh * n_lo + i * lo_step + l, 0, 0, 0))
 
     grid_spec = pltpu.PrefetchScalarGridSpec(
         num_scalar_prefetch=2,
-        grid=(n_lo,),
-        in_specs=[tile_spec(hh) for hh in range(n_hi)] + [pl.BlockSpec((n_src, width), lambda i, c, n: (0, 0))],
+        grid=(n_lo // lo_step,),
+        in_specs=[tile_spec(l, hh) for l in range(lo_step) for hh in range(n_hi)] + [pl.BlockSpec((n_src, width), lambda i, c, n: (0, 0))],
         out_specs=[
-            pl.BlockSpec((n_hi * group * side, half), lambda i, c, n: (i, 0)),
-            pl.BlockSpec((n_hi * group * side, half), lambda i, c, n: (i, 0)),
+            pl.BlockSpec((lo_step * n_hi * group * side, half), lambda i, c, n: (i, 0)),
+            pl.BlockSpec((lo_step * n_hi * group * side, half), lambda i, c, n: (i, 0)),
         ],
     )
     return pl.pallas_call(
@@ -56,7 +57,7 @@
         compiler_params=pltpu.CompilerParams(
             dimension_semantics=("arbitrary",), vmem_limit_bytes=48 * 1024 * 1024
         ),
-    )(cols.reshape(-1), counts, *([tiles] * n_hi), gathered)
+    )(cols.reshape(-1), counts, *([tiles] * (n_hi * lo_step)), gathered)
 
 
 def body(features, weight, bias, tile_vals, tile_col, tile_count):

time: 192 us -> 190 us (0.990)
  no operation moved by 1% of the time
where the time goes in v15:
time: 190 us
  waiting for transfers between devices  145 us (76%)
  between operations  13.1 us (7%)
  Pallas kernels  10.9 us (6%)
  local copies, waits for them, and re-layouts  7.51 us (4%)
  starting transfers between devices  6.19 us (3%)
  other arithmetic  5.26 us (3%)
  matrix products  2.46 us (1%)
    all_gather x1, waiting for transfers between devices, body(): gathered = lax.all_gather(features, 'rep', axis=0, tiled=True)  58.5 us
    ppermute x1, waiting for transfers between devices, body(): got_b = lax.ppermute(theirs_b, 'yh', swap)  46.6 us
    reduce_scatter x1, waiting for transfers between devices, body(): out_b = lax.psum_scatter(sum_b, 'z', scatter_dimension=0, tiled=True)  32.8 us
    pallas_call x1, Pallas kernels, sparse_partial(): pl.pallas_call(kernel, grid_spec=grid_spec, out_shape=[jax.ShapeDtypeStru...  10.9 us
    ppermute x1, waiting for transfers between devices, body(): got = lax.ppermute(theirs, 'yh', swap)  6.06 us
    convert_element_type x1, other arithmetic, body(): (mine_b.astype(jnp.float32) + got_b.astype(jnp.float32)).astype(jnp.bfloa...  4.24 us
  transfers between devices with their start and end apart: 5, of which 4 were waited for; matrix products, arithmetic and copies ran while one was open for 5% of the time, Pallas kernels for 0%

profile of v15, /device:TPU:2, one launch (start us, length us, event | category | flops | bytes accessed | tf_op | source)
XLA Modules:
  0.0 190.1 jit_solution(5526228712481798669)
XLA Ops:
  6.5 0.0 copy-start
  6.5 0.0 all-gather.2.cloned.1.call-start
  6.5 0.7 all-gather.2.cloned.1.call-update
  7.3 0.0 reduce-scatter.3.cloned.1.call-start
  7.3 0.8 copy.8
  8.1 0.1 reshape_squeeze.3.cols_ref
  8.2 58.5 %all-gather.2.cloned.1.call-done.refs_4_ = bf16[4096,1024]{1,0:T(8,128)(2,1)} async-done(((bf16[256,1024]{1,0:T(8,128)(2,1)}), bf16[4096,1024]{1,0:T(8,128)(2,1)}) %all-gather.2.cloned.1.call-update) | async-done | bytes 8388624 | tf_op jit(solution)/shard_map/all_gather | solution.py:72
  66.7 0.0 copy-start.2
  66.7 0.7 copy-done.2
  67.3 10.9 %shard_map.64 = (bf16[4096,512]{1,0:T(8,128)(2,1)S(1)}, bf16[4096,512]{1,0:T(8,128)(2,1)}) custom-call(s32[128]{0:T(128)S(1)} %reshape_squeeze.3.cols_ref, s32[32]{0:T(128)S(1)} %bitcast.12, bf16[32,4,128,128]{3,2,1,0:T(8,128)(2,1)} %bitcast.13, bf16[32,4,128,128]{3,2,1,0:T(8,128)(2,1)} %bitcast.14, bf16[32,4,128,128]{3,2,1,0:T(8,128)(2,1)} %bitcast.15, ...), custom_call_target="tpu_custom_call" | custom-call | tf_op jit(solution)/shard_map/pallas_call | solution.py:53
  78.2 0.0 copy-start.1
  78.2 1.9 %copy-done.1 = bf16[4096,512]{1,0:T(8,128)(2,1)} copy-done((bf16[4096,512]{1,0:T(8,128)(2,1)}, bf16[4096,512]{1,0:T(8,128)(2,1)S(1)}, u32[]{:S(2)}) %copy-start.1) | copy-done | bytes 4194328
  80.2 0.0 reduce-scatter.3.cloned.1.call-update
  80.2 0.0 reduce-scatter.5.cloned.1.call-start
  80.2 3.1 %dynamic-slice_bitcast_fusion = bf16[8,256,512]{2,1,0:T(8,128)(2,1)} fusion(bf16[8,2,256,512]{3,2,1,0:T(8,128)(2,1)} %bitcast.18, s32[]{:T(128)S(6)} %select_n.16), kind=kLoop, calls=%fused_computation.2 | loop fusion | bytes 4194308 | tf_op jit(solution)/shard_map/jit(dynamic_index_in_dim)/squeeze | solution.py:80
  83.3 3.0 %collective-permute-start.1 = (bf16[8,256,512]{2,1,0:T(8,128)(2,1)}, bf16[8,256,512]{2,1,0:T(8,128)(2,1)}, u32[]{:S(2)}, u32[]{:S(2)}) collective-permute-start(bf16[8,256,512]{2,1,0:T(8,128)(2,1)} %dynamic-slice_bitcast_fusion), channel_id=1, source_target_pairs={{0,8},{8,0},{1,9},{9,1},{2,10},{10,2},{3,11},{11,3},{4,12},{12,4},... | collective-permute-start | bytes 6291464 | tf_op jit(solution)/shard_map/ppermute | solution.py:81
  86.3 46.6 %collective-permute-done.1 = bf16[8,256,512]{2,1,0:T(8,128)(2,1)} collective-permute-done((bf16[8,256,512]{2,1,0:T(8,128)(2,1)}, bf16[8,256,512]{2,1,0:T(8,128)(2,1)}, u32[]{:S(2)}, u32[]{:S(2)}) %collective-permute-start.1) | collective-permute-done | bytes 2097184 | tf_op jit(solution)/shard_map/ppermute | solution.py:81
  132.9 4.2 %fusion = bf16[8,256,512]{2,1,0:T(8,128)(2,1)} fusion(bf16[8,256,512]{2,1,0:T(8,128)(2,1)} %collective-permute-done.1, bf16[8,2,256,512]{3,2,1,0:T(8,128)(2,1)} %bitcast.19, s32[]{:T(128)S(6)} %select_n.15), kind=kLoop, calls=%fused_computation.1 | loop fusion | flops 4194304 | bytes 6291460 | tf_op jit(solution)/shard_map/convert_element_type | solution.py:82
  137.1 0.0 copy-start.3
  137.1 0.0 reduce-scatter.5.cloned.1.call-update
  137.2 0.0 reduce-scatter.3.cloned.1.call-done
  137.2 1.0 constant_dynamic-slice_fusion
  138.2 3.1 %collective-permute-start = (bf16[256,512]{1,0:T(8,128)(2,1)S(1)}, bf16[256,512]{1,0:T(8,128)(2,1)S(1)}, u32[]{:S(2)}, u32[]{:S(2)}) collective-permute-start(bf16[256,512]{1,0:T(8,128)(2,1)S(1)} %constant_dynamic-slice_fusion), channel_id=1, source_target_pairs={{0,8},{8,0},{1,9},{9,1},{2,10},{10,2},{3,11},{11,3},{4,12},{12,4},... | collective-permute-start | bytes 786440 | tf_op jit(solution)/shard_map/ppermute | solution.py:88
  141.3 0.0 copy-done.3
  141.3 6.1 %collective-permute-done = bf16[256,512]{1,0:T(8,128)(2,1)S(1)} collective-permute-done((bf16[256,512]{1,0:T(8,128)(2,1)S(1)}, bf16[256,512]{1,0:T(8,128)(2,1)S(1)}, u32[]{:S(2)}, u32[]{:S(2)}) %collective-permute-start) | collective-permute-done | bytes 262176 | tf_op jit(solution)/shard_map/ppermute | solution.py:88
  147.3 1.0 add_convert_fusion
  148.3 32.8 %reduce-scatter.5.cloned.1.call-done = bf16[256,512]{1,0:T(8,128)(2,1)} async-done(((bf16[2048,512]{1,0:T(8,128)(2,1)}), bf16[256,512]{1,0:T(8,128)(2,1)}) %reduce-scatter.5.cloned.1.call-update) | async-done | bytes 262160 | tf_op jit(solution)/shard_map/reduce_scatter | solution.py:90
  181.2 0.0 copy-done
  181.2 2.5 %fusion.2 = bf16[256,1024]{1,0:T(8,128)(2,1)} fusion(bf16[1024,1024]{1,0:T(8,128)(2,1)S(1)} %copy-done, bf16[256,512]{1,0:T(8,128)(2,1)} %reduce-scatter.5.cloned.1.call-done, bf16[256,512]{1,0:T(8,128)(2,1)S(1)} %add_convert_fusion, f32[1024]{0:T(1024)S(1)} %convert_element_type.34), kind=kOutput, calls=%fused_computation.5 | convolution fusion | flops 538705920 | bytes 3149824 | tf_op jit(solution)/shard_map/dot_general | solution.py:92
  (1 shorter events, 0.0 us)
Async XLA Ops:
  6.5 174.6 %copy-start = (bf16[1024,1024]{1,0:T(8,128)(2,1)S(1)}, bf16[1024,1024]{1,0:T(8,128)(2,1)}, u32[]{:S(2)}) copy-start(bf16[1024,1024]{1,0:T(8,128)(2,1)} %param.7) | copy-start | bytes 6291460
  6.5 60.1 %all-gather.2.cloned.1.call-start = ((), (), s32[]{:S(2)}) async-start(), calls=%async_computation.2 | async-start | bytes 8912896 | tf_op jit(solution)/shard_map/all_gather | solution.py:72
  7.3 129.9 %reduce-scatter.3.cloned.1.call-start = ((), (), s32[]{:S(2)}) async-start(), calls=%async_computation.3 | async-start | bytes 4718592 | tf_op jit(solution)/shard_map/reduce_scatter | solution.py:84
  66.7 0.7 copy-start.2
  78.2 1.9 %copy-start.1 = (bf16[4096,512]{1,0:T(8,128)(2,1)}, bf16[4096,512]{1,0:T(8,128)(2,1)S(1)}, u32[]{:S(2)}) copy-start(bf16[4096,512]{1,0:T(8,128)(2,1)S(1)} %get-tuple-element.7) | copy-start | bytes 12582916
  80.2 101.0 %reduce-scatter.5.cloned.1.call-start = ((), (), s32[]{:S(2)}) async-start(), calls=%async_computation.4 | async-start | bytes 2359296 | tf_op jit(solution)/shard_map/reduce_scatter | solution.py:90
  83.3 49.6 %collective-permute-start.1 = (bf16[8,256,512]{2,1,0:T(8,128)(2,1)}, bf16[8,256,512]{2,1,0:T(8,128)(2,1)}, u32[]{:S(2)}, u32[]{:S(2)}) collective-permute-start(bf16[8,256,512]{2,1,0:T(8,128)(2,1)} %dynamic-slice_bitcast_fusion), channel_id=1, source_target_pairs={{0,8},{8,0},{1,9},{9,1},{2,10},{10,2},{3,11},{11,3},{4,12},{12,4},... | collective-permute-start | bytes 6291464 | tf_op jit(solution)/shard_map/ppermute | solution.py:81
  137.1 4.1 %copy-start.3 = (bf16[1024]{0:T(1024)(128)(2,1)S(1)}, bf16[1024]{0:T(1024)(128)(2,1)}, u32[]{:S(2)}) copy-start(bf16[1024]{0:T(1024)(128)(2,1)} %param.8) | copy-start | bytes 6148
  138.2 9.2 %collective-permute-start = (bf16[256,512]{1,0:T(8,128)(2,1)S(1)}, bf16[256,512]{1,0:T(8,128)(2,1)S(1)}, u32[]{:S(2)}, u32[]{:S(2)}) collective-permute-start(bf16[256,512]{1,0:T(8,128)(2,1)S(1)} %constant_dynamic-slice_fusion), channel_id=1, source_target_pairs={{0,8},{8,0},{1,9},{9,1},{2,10},{10,2},{3,11},{11,3},{4,12},{12,4},... | collective-permute-start | bytes 786440 | tf_op jit(solution)/shard_map/ppermute | solution.py:88
Sparse Core Ops, SparseCore 0:
  9.2 57.4 all-gather.1
  80.3 56.3 reduce-scatter.2
  139.2 41.8 reduce-scatter.4

commit v16 on v15

--- a/solution.py
+++ b/solution.py
@@ -6,7 +6,7 @@
 from jax.sharding import Mesh, PartitionSpec as P
 
 
-def sparse_partial(gathered, tiles, cols, counts, n_hi, n_lo, group=2, lo_step=2):
+def sparse_partial(gathered, tiles, cols, counts, n_hi, n_lo, group=2, lo_step=4):
     n_blocks, slots, side, _ = tiles.shape
     width = gathered.shape[1]
     n_src = gathered.shape[0]

time: 190 us -> 191 us (level)
  no operation moved by 1% of the time
where the time goes in v16:
time: 191 us; the launch traced here: 190 us
  waiting for transfers between devices  145 us (76%)
  between operations  13.1 us (7%)
  Pallas kernels  11.1 us (6%)
  local copies, waits for them, and re-layouts  7.51 us (4%)
  starting transfers between devices  6.18 us (3%)
  other arithmetic  5.26 us (3%)
  matrix products  2.46 us (1%)
    all_gather x1, waiting for transfers between devices, body(): gathered = lax.all_gather(features, 'rep', axis=0, tiled=True)  58.5 us
    ppermute x1, waiting for transfers between devices, body(): got_b = lax.ppermute(theirs_b, 'yh', swap)  46.6 us
    reduce_scatter x1, waiting for transfers between devices, body(): out_b = lax.psum_scatter(sum_b, 'z', scatter_dimension=0, tiled=True)  32.7 us
    pallas_call x1, Pallas kernels, sparse_partial(): pl.pallas_call(kernel, grid_spec=grid_spec, out_shape=[jax.ShapeDtypeStru...  11.1 us
    ppermute x1, waiting for transfers between devices, body(): got = lax.ppermute(theirs, 'yh', swap)  6.07 us
    convert_element_type x1, other arithmetic, body(): (mine_b.astype(jnp.float32) + got_b.astype(jnp.float32)).astype(jnp.bfloa...  4.24 us
  transfers between devices with their start and end apart: 5, of which 4 were waited for; matrix products, arithmetic and copies ran while one was open for 5% of the time, Pallas kernels for 0%

profile of v16, /device:TPU:2, one launch (start us, length us, event | category | flops | bytes accessed | tf_op | source)
XLA Modules:
  0.0 190.2 jit_solution(17661612500002972736)
XLA Ops:
  6.5 0.0 copy-start
  6.5 0.0 all-gather.2.cloned.1.call-start
  6.5 0.7 all-gather.2.cloned.1.call-update
  7.3 0.0 reduce-scatter.3.cloned.1.call-start
  7.3 0.8 copy.8
  8.1 0.1 reshape_squeeze.3.cols_ref
  8.2 58.5 %all-gather.2.cloned.1.call-done.refs_8_ = bf16[4096,1024]{1,0:T(8,128)(2,1)} async-done(((bf16[256,1024]{1,0:T(8,128)(2,1)}), bf16[4096,1024]{1,0:T(8,128)(2,1)}) %all-gather.2.cloned.1.call-update) | async-done | bytes 8388624 | tf_op jit(solution)/shard_map/all_gather | solution.py:72
  66.7 0.0 copy-start.2
  66.7 0.7 copy-done.2
  67.3 11.1 %shard_map.64 = (bf16[4096,512]{1,0:T(8,128)(2,1)S(1)}, bf16[4096,512]{1,0:T(8,128)(2,1)}) custom-call(s32[128]{0:T(128)S(1)} %reshape_squeeze.3.cols_ref, s32[32]{0:T(128)S(1)} %bitcast.12, bf16[32,4,128,128]{3,2,1,0:T(8,128)(2,1)} %bitcast.13, bf16[32,4,128,128]{3,2,1,0:T(8,128)(2,1)} %bitcast.14, bf16[32,4,128,128]{3,2,1,0:T(8,128)(2,1)} %bitcast.15, ...), custom_call_target="tpu_custom_call" | custom-call | tf_op jit(solution)/shard_map/pallas_call | solution.py:53
  78.4 0.0 copy-start.1
  78.4 1.9 %copy-done.1 = bf16[4096,512]{1,0:T(8,128)(2,1)} copy-done((bf16[4096,512]{1,0:T(8,128)(2,1)}, bf16[4096,512]{1,0:T(8,128)(2,1)S(1)}, u32[]{:S(2)}) %copy-start.1) | copy-done | bytes 4194328
  80.3 0.0 reduce-scatter.3.cloned.1.call-update
  80.4 0.0 reduce-scatter.5.cloned.1.call-start
  80.4 3.1 %dynamic-slice_bitcast_fusion = bf16[8,256,512]{2,1,0:T(8,128)(2,1)} fusion(bf16[8,2,256,512]{3,2,1,0:T(8,128)(2,1)} %bitcast.22, s32[]{:T(128)S(6)} %select_n.16), kind=kLoop, calls=%fused_computation.2 | loop fusion | bytes 4194308 | tf_op jit(solution)/shard_map/jit(dynamic_index_in_dim)/squeeze | solution.py:80
  83.5 3.0 %collective-permute-start.1 = (bf16[8,256,512]{2,1,0:T(8,128)(2,1)}, bf16[8,256,512]{2,1,0:T(8,128)(2,1)}, u32[]{:S(2)}, u32[]{:S(2)}) collective-permute-start(bf16[8,256,512]{2,1,0:T(8,128)(2,1)} %dynamic-slice_bitcast_fusion), channel_id=1, source_target_pairs={{0,8},{8,0},{1,9},{9,1},{2,10},{10,2},{3,11},{11,3},{4,12},{12,4},... | collective-permute-start | bytes 6291464 | tf_op jit(solution)/shard_map/ppermute | solution.py:81
  86.5 46.6 %collective-permute-done.1 = bf16[8,256,512]{2,1,0:T(8,128)(2,1)} collective-permute-done((bf16[8,256,512]{2,1,0:T(8,128)(2,1)}, bf16[8,256,512]{2,1,0:T(8,128)(2,1)}, u32[]{:S(2)}, u32[]{:S(2)}) %collective-permute-start.1) | collective-permute-done | bytes 2097184 | tf_op jit(solution)/shard_map/ppermute | solution.py:81
  133.1 4.2 %fusion = bf16[8,256,512]{2,1,0:T(8,128)(2,1)} fusion(bf16[8,256,512]{2,1,0:T(8,128)(2,1)} %collective-permute-done.1, bf16[8,2,256,512]{3,2,1,0:T(8,128)(2,1)} %bitcast.23, s32[]{:T(128)S(6)} %select_n.15), kind=kLoop, calls=%fused_computation.1 | loop fusion | flops 4194304 | bytes 6291460 | tf_op jit(solution)/shard_map/convert_element_type | solution.py:82
  137.3 0.0 copy-start.3
  137.3 0.0 reduce-scatter.5.cloned.1.call-update
  137.3 0.0 reduce-scatter.3.cloned.1.call-done
  137.4 1.0 constant_dynamic-slice_fusion
  138.3 3.1 %collective-permute-start = (bf16[256,512]{1,0:T(8,128)(2,1)S(1)}, bf16[256,512]{1,0:T(8,128)(2,1)S(1)}, u32[]{:S(2)}, u32[]{:S(2)}) collective-permute-start(bf16[256,512]{1,0:T(8,128)(2,1)S(1)} %constant_dynamic-slice_fusion), channel_id=1, source_target_pairs={{0,8},{8,0},{1,9},{9,1},{2,10},{10,2},{3,11},{11,3},{4,12},{12,4},... | collective-permute-start | bytes 786440 | tf_op jit(solution)/shard_map/ppermute | solution.py:88
  141.4 0.0 copy-done.3
  141.4 6.1 %collective-permute-done = bf16[256,512]{1,0:T(8,128)(2,1)S(1)} collective-permute-done((bf16[256,512]{1,0:T(8,128)(2,1)S(1)}, bf16[256,512]{1,0:T(8,128)(2,1)S(1)}, u32[]{:S(2)}, u32[]{:S(2)}) %collective-permute-start) | collective-permute-done | bytes 262176 | tf_op jit(solution)/shard_map/ppermute | solution.py:88
  147.5 1.0 add_convert_fusion
  148.5 32.7 %reduce-scatter.5.cloned.1.call-done = bf16[256,512]{1,0:T(8,128)(2,1)} async-done(((bf16[2048,512]{1,0:T(8,128)(2,1)}), bf16[256,512]{1,0:T(8,128)(2,1)}) %reduce-scatter.5.cloned.1.call-update) | async-done | bytes 262160 | tf_op jit(solution)/shard_map/reduce_scatter | solution.py:90
  181.3 0.0 copy-done
  181.3 2.5 %fusion.2 = bf16[256,1024]{1,0:T(8,128)(2,1)} fusion(bf16[1024,1024]{1,0:T(8,128)(2,1)S(1)} %copy-done, bf16[256,512]{1,0:T(8,128)(2,1)} %reduce-scatter.5.cloned.1.call-done, bf16[256,512]{1,0:T(8,128)(2,1)S(1)} %add_convert_fusion, f32[1024]{0:T(1024)S(1)} %convert_element_type.34), kind=kOutput, calls=%fused_computation.5 | convolution fusion | flops 538705920 | bytes 3149824 | tf_op jit(solution)/shard_map/dot_general | solution.py:92
  (1 shorter events, 0.0 us)
Async XLA Ops:
  6.5 174.7 %copy-start = (bf16[1024,1024]{1,0:T(8,128)(2,1)S(1)}, bf16[1024,1024]{1,0:T(8,128)(2,1)}, u32[]{:S(2)}) copy-start(bf16[1024,1024]{1,0:T(8,128)(2,1)} %param.7) | copy-start | bytes 6291460
  6.5 60.1 %all-gather.2.cloned.1.call-start = ((), (), s32[]{:S(2)}) async-start(), calls=%async_computation.2 | async-start | bytes 8912896 | tf_op jit(solution)/shard_map/all_gather | solution.py:72
  7.3 130.1 %reduce-scatter.3.cloned.1.call-start = ((), (), s32[]{:S(2)}) async-start(), calls=%async_computation.3 | async-start | bytes 4718592 | tf_op jit(solution)/shard_map/reduce_scatter | solution.py:84
  66.7 0.7 copy-start.2
  78.4 1.9 %copy-start.1 = (bf16[4096,512]{1,0:T(8,128)(2,1)}, bf16[4096,512]{1,0:T(8,128)(2,1)S(1)}, u32[]{:S(2)}) copy-start(bf16[4096,512]{1,0:T(8,128)(2,1)S(1)} %get-tuple-element.7) | copy-start | bytes 12582916
  80.4 100.9 %reduce-scatter.5.cloned.1.call-start = ((), (), s32[]{:S(2)}) async-start(), calls=%async_computation.4 | async-start | bytes 2359296 | tf_op jit(solution)/shard_map/reduce_scatter | solution.py:90
  83.5 49.6 %collective-permute-start.1 = (bf16[8,256,512]{2,1,0:T(8,128)(2,1)}, bf16[8,256,512]{2,1,0:T(8,128)(2,1)}, u32[]{:S(2)}, u32[]{:S(2)}) collective-permute-start(bf16[8,256,512]{2,1,0:T(8,128)(2,1)} %dynamic-slice_bitcast_fusion), channel_id=1, source_target_pairs={{0,8},{8,0},{1,9},{9,1},{2,10},{10,2},{3,11},{11,3},{4,12},{12,4},... | collective-permute-start | bytes 6291464 | tf_op jit(solution)/shard_map/ppermute | solution.py:81
  137.3 4.1 %copy-start.3 = (bf16[1024]{0:T(1024)(128)(2,1)S(1)}, bf16[1024]{0:T(1024)(128)(2,1)}, u32[]{:S(2)}) copy-start(bf16[1024]{0:T(1024)(128)(2,1)} %param.8) | copy-start | bytes 6148
  138.3 9.2 %collective-permute-start = (bf16[256,512]{1,0:T(8,128)(2,1)S(1)}, bf16[256,512]{1,0:T(8,128)(2,1)S(1)}, u32[]{:S(2)}, u32[]{:S(2)}) collective-permute-start(bf16[256,512]{1,0:T(8,128)(2,1)S(1)} %constant_dynamic-slice_fusion), channel_id=1, source_target_pairs={{0,8},{8,0},{1,9},{9,1},{2,10},{10,2},{3,11},{11,3},{4,12},{12,4},... | collective-permute-start | bytes 786440 | tf_op jit(solution)/shard_map/ppermute | solution.py:88
Sparse Core Ops, SparseCore 0:
  9.2 57.4 all-gather.1
  80.5 56.3 reduce-scatter.2
  139.4 41.8 reduce-scatter.4

commit v17 on v16

--- a/solution.py
+++ b/solution.py
@@ -88,8 +88,9 @@
     got = lax.ppermute(theirs, "yh", swap)
     out_a = (mine.astype(jnp.float32) + got.astype(jnp.float32)).astype(jnp.bfloat16)
     out_b = lax.psum_scatter(sum_b, "z", scatter_dimension=0, tiled=True)
-    summed = jnp.concatenate([out_a, out_b], axis=1)
-    mixed = jnp.dot(summed, weight, preferred_element_type=jnp.float32) + bias.astype(jnp.float32)
+    cut = out_a.shape[1]
+    mixed = jnp.dot(out_a, weight[:cut], preferred_element_type=jnp.float32) + bias.astype(jnp.float32)
+    mixed = mixed + jnp.dot(out_b, weight[cut:], preferred_element_type=jnp.float32)
     return jnp.maximum(mixed, 0.0).astype(jnp.bfloat16)
 
 

time: 191 us -> 190 us (level)
    reduce_scatter x1, waiting for transfers between devices: 32.7 us -> 39.3 us  [body(): out_b = lax.psum_scatter(sum_b, 'z', scatter_dimension=0, tiled=True)]
    ppermute x1, waiting for transfers between devices: 6.07 us -> 0.01 us  [body(): got = lax.ppermute(theirs, 'yh', swap)]
    unnamed x9 -> x11, local copies, waits for them, and re-layouts: 3.37 us -> 4.03 us
  transfers between devices with their start and end apart: 5 -> 5, of which waited for: 4 -> 3; matrix products, arithmetic and copies ran while one was open for 5% -> 5% of each run, Pallas kernels for 0% -> 0%
where the time goes in v17:
time: 190 us
  waiting for transfers between devices  145 us (76%)
  between operations  13.2 us (7%)
  Pallas kernels  11.1 us (6%)
  local copies, waits for them, and re-layouts  8.23 us (4%)
  starting transfers between devices  6.19 us (3%)
  other arithmetic  3.51 us (2%)
  matrix products  2.63 us (1%)
    all_gather x1, waiting for transfers between devices, body(): gathered = lax.all_gather(features, 'rep', axis=0, tiled=True)  58.5 us
    ppermute x1, waiting for transfers between devices, body(): got_b = lax.ppermute(theirs_b, 'yh', swap)  46.5 us
    reduce_scatter x1, waiting for transfers between devices, body(): out_b = lax.psum_scatter(sum_b, 'z', scatter_dimension=0, tiled=True)  39.3 us
    pallas_call x1, Pallas kernels, sparse_partial(): pl.pallas_call(kernel, grid_spec=grid_spec, out_shape=[jax.ShapeDtypeStru...  11.1 us
    unnamed x11, local copies, waits for them, and re-layouts  4.03 us
  transfers between devices with their start and end apart: 5, of which 3 were waited for; matrix products, arithmetic and copies ran while one was open for 5% of the time, Pallas kernels for 0%

profile of v17, /device:TPU:2, one launch (start us, length us, event | category | flops | bytes accessed | tf_op | source)
XLA Modules:
  0.0 189.7 jit_solution(9621540852473136155)
XLA Ops:
  6.5 0.0 all-gather.2.cloned.1.call-start
  6.5 0.7 all-gather.2.cloned.1.call-update
  7.3 0.0 reduce-scatter.3.cloned.1.call-start
  7.3 0.8 copy.8
  8.1 0.1 reshape_squeeze.3.cols_ref
  8.2 58.5 %all-gather.2.cloned.1.call-done.refs_8_ = bf16[4096,1024]{1,0:T(8,128)(2,1)} async-done(((bf16[256,1024]{1,0:T(8,128)(2,1)}), bf16[4096,1024]{1,0:T(8,128)(2,1)}) %all-gather.2.cloned.1.call-update) | async-done | bytes 8388624 | tf_op jit(solution)/shard_map/all_gather | solution.py:72
  66.7 0.0 copy-start.1
  66.7 0.7 copy-done.1
  67.3 11.1 %shard_map.64 = (bf16[4096,512]{1,0:T(8,128)(2,1)S(1)}, bf16[4096,512]{1,0:T(8,128)(2,1)}) custom-call(s32[128]{0:T(128)S(1)} %reshape_squeeze.3.cols_ref, s32[32]{0:T(128)S(1)} %bitcast.12, bf16[32,4,128,128]{3,2,1,0:T(8,128)(2,1)} %bitcast.13, bf16[32,4,128,128]{3,2,1,0:T(8,128)(2,1)} %bitcast.14, bf16[32,4,128,128]{3,2,1,0:T(8,128)(2,1)} %bitcast.15, ...), custom_call_target="tpu_custom_call" | custom-call | tf_op jit(solution)/shard_map/pallas_call | solution.py:53
  78.4 0.0 copy-start
  78.4 2.0 %copy-done = bf16[4096,512]{1,0:T(8,128)(2,1)} copy-done((bf16[4096,512]{1,0:T(8,128)(2,1)}, bf16[4096,512]{1,0:T(8,128)(2,1)S(1)}, u32[]{:S(2)}) %copy-start) | copy-done | bytes 4194328
  80.3 0.0 reduce-scatter.3.cloned.1.call-update
  80.4 0.0 reduce-scatter.5.cloned.1.call-start
  80.4 3.1 %dynamic-slice_bitcast_fusion = bf16[8,256,512]{2,1,0:T(8,128)(2,1)} fusion(bf16[8,2,256,512]{3,2,1,0:T(8,128)(2,1)} %bitcast.22, s32[]{:T(128)S(6)} %select_n.16), kind=kLoop, calls=%fused_computation.2 | loop fusion | bytes 4194308 | tf_op jit(solution)/shard_map/jit(dynamic_index_in_dim)/squeeze | solution.py:80
  83.5 3.0 %collective-permute-start.1 = (bf16[8,256,512]{2,1,0:T(8,128)(2,1)}, bf16[8,256,512]{2,1,0:T(8,128)(2,1)S(1)}, u32[]{:S(2)}, u32[]{:S(2)}) collective-permute-start(bf16[8,256,512]{2,1,0:T(8,128)(2,1)} %dynamic-slice_bitcast_fusion), channel_id=1, source_target_pairs={{0,8},{8,0},{1,9},{9,1},{2,10},{10,2},{3,11},{11,3},{4,12},{12,4},... | collective-permute-start | bytes 6291464 | tf_op jit(solution)/shard_map/ppermute | solution.py:81
  86.5 46.5 %collective-permute-done.1 = bf16[8,256,512]{2,1,0:T(8,128)(2,1)S(1)} collective-permute-done((bf16[8,256,512]{2,1,0:T(8,128)(2,1)}, bf16[8,256,512]{2,1,0:T(8,128)(2,1)S(1)}, u32[]{:S(2)}, u32[]{:S(2)}) %collective-permute-start.1) | collective-permute-done | bytes 2097184 | tf_op jit(solution)/shard_map/ppermute | solution.py:81
  132.9 3.5 %fusion = bf16[8,256,512]{2,1,0:T(8,128)(2,1)} fusion(bf16[8,256,512]{2,1,0:T(8,128)(2,1)S(1)} %collective-permute-done.1, bf16[8,2,256,512]{3,2,1,0:T(8,128)(2,1)} %bitcast.23, s32[]{:T(128)S(6)} %select_n.15), kind=kLoop, calls=%fused_computation.1 | loop fusion | flops 4194304 | bytes 6291460 | tf_op jit(solution)/shard_map/convert_element_type | solution.py:82
  136.5 0.0 copy-start.4
  136.5 0.0 copy-start.2
  136.5 0.0 reduce-scatter.5.cloned.1.call-update
  136.5 0.6 copy-done.4
  137.1 0.0 reduce-scatter.3.cloned.1.call-done
  137.1 0.0 copy-start.3
  137.1 1.0 constant_dynamic-slice_fusion
  138.2 3.1 %collective-permute-start = (bf16[256,512]{1,0:T(8,128)(2,1)S(1)}, bf16[256,512]{1,0:T(8,128)(2,1)S(1)}, u32[]{:S(2)}, u32[]{:S(2)}) collective-permute-start(bf16[256,512]{1,0:T(8,128)(2,1)S(1)} %constant_dynamic-slice_fusion), channel_id=1, source_target_pairs={{0,8},{8,0},{1,9},{9,1},{2,10},{10,2},{3,11},{11,3},{4,12},{12,4},... | collective-permute-start | bytes 786440 | tf_op jit(solution)/shard_map/ppermute | solution.py:88
  141.3 39.3 %reduce-scatter.5.cloned.1.call-done = bf16[256,512]{1,0:T(8,128)(2,1)} async-done(((bf16[2048,512]{1,0:T(8,128)(2,1)}), bf16[256,512]{1,0:T(8,128)(2,1)}) %reduce-scatter.5.cloned.1.call-update) | async-done | bytes 262160 | tf_op jit(solution)/shard_map/reduce_scatter | solution.py:90
  180.5 0.0 copy-done.2
  180.5 1.4 fusion.4
  181.9 0.0 collective-permute-done
  181.9 0.0 copy-done.3
  182.0 1.2 fusion.3
  (1 shorter events, 0.0 us)
Async XLA Ops:
  6.5 60.1 %all-gather.2.cloned.1.call-start = ((), (), s32[]{:S(2)}) async-start(), calls=%async_computation.2 | async-start | bytes 8912896 | tf_op jit(solution)/shard_map/all_gather | solution.py:72
  7.3 129.9 %reduce-scatter.3.cloned.1.call-start = ((), (), s32[]{:S(2)}) async-start(), calls=%async_computation.3 | async-start | bytes 4718592 | tf_op jit(solution)/shard_map/reduce_scatter | solution.py:84
  66.7 0.7 copy-start.1
  78.4 2.0 %copy-start = (bf16[4096,512]{1,0:T(8,128)(2,1)}, bf16[4096,512]{1,0:T(8,128)(2,1)S(1)}, u32[]{:S(2)}) copy-start(bf16[4096,512]{1,0:T(8,128)(2,1)S(1)} %get-tuple-element.7) | copy-start | bytes 12582916
  80.4 100.2 %reduce-scatter.5.cloned.1.call-start = ((), (), s32[]{:S(2)}) async-start(), calls=%async_computation.4 | async-start | bytes 2359296 | tf_op jit(solution)/shard_map/reduce_scatter | solution.py:90
  83.5 49.5 %collective-permute-start.1 = (bf16[8,256,512]{2,1,0:T(8,128)(2,1)}, bf16[8,256,512]{2,1,0:T(8,128)(2,1)S(1)}, u32[]{:S(2)}, u32[]{:S(2)}) collective-permute-start(bf16[8,256,512]{2,1,0:T(8,128)(2,1)} %dynamic-slice_bitcast_fusion), channel_id=1, source_target_pairs={{0,8},{8,0},{1,9},{9,1},{2,10},{10,2},{3,11},{11,3},{4,12},{12,4},... | collective-permute-start | bytes 6291464 | tf_op jit(solution)/shard_map/ppermute | solution.py:81
  136.5 0.7 copy-start.4
  136.5 44.1 %copy-start.2 = (bf16[1024,1024]{1,0:T(8,128)(2,1)S(1)}, bf16[1024,1024]{1,0:T(8,128)(2,1)}, u32[]{:S(2)}) copy-start(bf16[1024,1024]{1,0:T(8,128)(2,1)} %param.7) | copy-start | bytes 6291460
  137.1 44.8 %copy-start.3 = (bf16[512,512]{1,0:T(8,128)(2,1)S(1)}, bf16[512,512]{1,0:T(8,128)(2,1)}, u32[]{:S(2)}) copy-start(bf16[512,512]{1,0:T(8,128)(2,1)} %reduce-scatter.3.cloned.1.call-done) | copy-start | bytes 1572868
  138.2 43.7 %collective-permute-start = (bf16[256,512]{1,0:T(8,128)(2,1)S(1)}, bf16[256,512]{1,0:T(8,128)(2,1)S(1)}, u32[]{:S(2)}, u32[]{:S(2)}) collective-permute-start(bf16[256,512]{1,0:T(8,128)(2,1)S(1)} %constant_dynamic-slice_fusion), channel_id=1, source_target_pairs={{0,8},{8,0},{1,9},{9,1},{2,10},{10,2},{3,11},{11,3},{4,12},{12,4},... | collective-permute-start | bytes 786440 | tf_op jit(solution)/shard_map/ppermute | solution.py:88
Sparse Core Ops, SparseCore 0:
  9.2 57.4 all-gather.1
  80.5 56.3 reduce-scatter.2
  139.4 41.1 reduce-scatter.4

commit v18 on v16

--- a/solution.py
+++ b/solution.py
@@ -6,7 +6,7 @@
 from jax.sharding import Mesh, PartitionSpec as P
 
 
-def sparse_partial(gathered, tiles, cols, counts, n_hi, n_lo, group=2, lo_step=4):
+def sparse_partial(gathered, tiles, cols, counts, n_hi, n_lo, group=2, lo_step=8):
     n_blocks, slots, side, _ = tiles.shape
     width = gathered.shape[1]
     n_src = gathered.shape[0]

time: 191 us -> 191 us (level)
  no operation moved by 1% of the time
where the time goes in v18:
time: 191 us
  waiting for transfers between devices  145 us (76%)
  between operations  13.1 us (7%)
  Pallas kernels  11.7 us (6%)
  local copies, waits for them, and re-layouts  7.51 us (4%)
  starting transfers between devices  6.2 us (3%)
  other arithmetic  5.26 us (3%)
  matrix products  2.46 us (1%)
    all_gather x1, waiting for transfers between devices, body(): gathered = lax.all_gather(features, 'rep', axis=0, tiled=True)  58.5 us
    ppermute x1, waiting for transfers between devices, body(): got_b = lax.ppermute(theirs_b, 'yh', swap)  46.6 us
    reduce_scatter x1, waiting for transfers between devices, body(): out_b = lax.psum_scatter(sum_b, 'z', scatter_dimension=0, tiled=True)  32.8 us
    pallas_call x1, Pallas kernels, sparse_partial(): pl.pallas_call(kernel, grid_spec=grid_spec, out_shape=[jax.ShapeDtypeStru...  11.7 us
    ppermute x1, waiting for transfers between devices, body(): got = lax.ppermute(theirs, 'yh', swap)  6.07 us
    convert_element_type x1, other arithmetic, body(): (mine_b.astype(jnp.float32) + got_b.astype(jnp.float32)).astype(jnp.bfloa...  4.24 us
  transfers between devices with their start and end apart: 5, of which 4 were waited for; matrix products, arithmetic and copies ran while one was open for 5% of the time, Pallas kernels for 0%

profile of v18, /device:TPU:2, one launch (start us, length us, event | category | flops | bytes accessed | tf_op | source)
XLA Modules:
  0.0 191.0 jit_solution(12438609849676922137)
XLA Ops:
  6.5 0.0 copy-start
  6.5 0.0 all-gather.2.cloned.1.call-start
  6.5 0.7 all-gather.2.cloned.1.call-update
  7.3 0.0 reduce-scatter.3.cloned.1.call-start
  7.3 0.8 copy.8
  8.1 0.1 reshape_squeeze.3.cols_ref
  8.2 58.5 %all-gather.2.cloned.1.call-done.refs_16_ = bf16[4096,1024]{1,0:T(8,128)(2,1)} async-done(((bf16[256,1024]{1,0:T(8,128)(2,1)}), bf16[4096,1024]{1,0:T(8,128)(2,1)}) %all-gather.2.cloned.1.call-update) | async-done | bytes 8388624 | tf_op jit(solution)/shard_map/all_gather | solution.py:72
  66.7 0.0 copy-start.2
  66.7 0.7 copy-done.2
  67.3 11.7 %shard_map.64 = (bf16[4096,512]{1,0:T(8,128)(2,1)S(1)}, bf16[4096,512]{1,0:T(8,128)(2,1)}) custom-call(s32[128]{0:T(128)S(1)} %reshape_squeeze.3.cols_ref, s32[32]{0:T(128)S(1)} %bitcast.12, bf16[32,4,128,128]{3,2,1,0:T(8,128)(2,1)} %bitcast.13, bf16[32,4,128,128]{3,2,1,0:T(8,128)(2,1)} %bitcast.14, bf16[32,4,128,128]{3,2,1,0:T(8,128)(2,1)} %bitcast.15, ...), custom_call_target="tpu_custom_call" | custom-call | tf_op jit(solution)/shard_map/pallas_call | solution.py:53
  79.1 0.0 copy-start.1
  79.1 1.9 %copy-done.1 = bf16[4096,512]{1,0:T(8,128)(2,1)} copy-done((bf16[4096,512]{1,0:T(8,128)(2,1)}, bf16[4096,512]{1,0:T(8,128)(2,1)S(1)}, u32[]{:S(2)}) %copy-start.1) | copy-done | bytes 4194328
  81.0 0.0 reduce-scatter.3.cloned.1.call-update
  81.0 0.0 reduce-scatter.5.cloned.1.call-start
  81.1 3.1 %dynamic-slice_bitcast_fusion = bf16[8,256,512]{2,1,0:T(8,128)(2,1)} fusion(bf16[8,2,256,512]{3,2,1,0:T(8,128)(2,1)} %bitcast.30, s32[]{:T(128)S(6)} %select_n.16), kind=kLoop, calls=%fused_computation.2 | loop fusion | bytes 4194308 | tf_op jit(solution)/shard_map/jit(dynamic_index_in_dim)/squeeze | solution.py:80
  84.1 3.0 %collective-permute-start.1 = (bf16[8,256,512]{2,1,0:T(8,128)(2,1)}, bf16[8,256,512]{2,1,0:T(8,128)(2,1)}, u32[]{:S(2)}, u32[]{:S(2)}) collective-permute-start(bf16[8,256,512]{2,1,0:T(8,128)(2,1)} %dynamic-slice_bitcast_fusion), channel_id=1, source_target_pairs={{0,8},{8,0},{1,9},{9,1},{2,10},{10,2},{3,11},{11,3},{4,12},{12,4},... | collective-permute-start | bytes 6291464 | tf_op jit(solution)/shard_map/ppermute | solution.py:81
  87.2 46.6 %collective-permute-done.1 = bf16[8,256,512]{2,1,0:T(8,128)(2,1)} collective-permute-done((bf16[8,256,512]{2,1,0:T(8,128)(2,1)}, bf16[8,256,512]{2,1,0:T(8,128)(2,1)}, u32[]{:S(2)}, u32[]{:S(2)}) %collective-permute-start.1) | collective-permute-done | bytes 2097184 | tf_op jit(solution)/shard_map/ppermute | solution.py:81
  133.7 4.2 %fusion = bf16[8,256,512]{2,1,0:T(8,128)(2,1)} fusion(bf16[8,256,512]{2,1,0:T(8,128)(2,1)} %collective-permute-done.1, bf16[8,2,256,512]{3,2,1,0:T(8,128)(2,1)} %bitcast.31, s32[]{:T(128)S(6)} %select_n.15), kind=kLoop, calls=%fused_computation.1 | loop fusion | flops 4194304 | bytes 6291460 | tf_op jit(solution)/shard_map/convert_element_type | solution.py:82
  138.0 0.0 copy-start.3
  138.0 0.0 reduce-scatter.5.cloned.1.call-update
  138.0 0.0 reduce-scatter.3.cloned.1.call-done
  138.0 1.0 constant_dynamic-slice_fusion
  139.0 3.1 %collective-permute-start = (bf16[256,512]{1,0:T(8,128)(2,1)S(1)}, bf16[256,512]{1,0:T(8,128)(2,1)S(1)}, u32[]{:S(2)}, u32[]{:S(2)}) collective-permute-start(bf16[256,512]{1,0:T(8,128)(2,1)S(1)} %constant_dynamic-slice_fusion), channel_id=1, source_target_pairs={{0,8},{8,0},{1,9},{9,1},{2,10},{10,2},{3,11},{11,3},{4,12},{12,4},... | collective-permute-start | bytes 786440 | tf_op jit(solution)/shard_map/ppermute | solution.py:88
  142.1 0.0 copy-done.3
  142.1 6.1 %collective-permute-done = bf16[256,512]{1,0:T(8,128)(2,1)S(1)} collective-permute-done((bf16[256,512]{1,0:T(8,128)(2,1)S(1)}, bf16[256,512]{1,0:T(8,128)(2,1)S(1)}, u32[]{:S(2)}, u32[]{:S(2)}) %collective-permute-start) | collective-permute-done | bytes 262176 | tf_op jit(solution)/shard_map/ppermute | solution.py:88
  148.2 1.0 add_convert_fusion
  149.2 32.8 %reduce-scatter.5.cloned.1.call-done = bf16[256,512]{1,0:T(8,128)(2,1)} async-done(((bf16[2048,512]{1,0:T(8,128)(2,1)}), bf16[256,512]{1,0:T(8,128)(2,1)}) %reduce-scatter.5.cloned.1.call-update) | async-done | bytes 262160 | tf_op jit(solution)/shard_map/reduce_scatter | solution.py:90
  182.0 0.0 copy-done
  182.0 2.5 %fusion.2 = bf16[256,1024]{1,0:T(8,128)(2,1)} fusion(bf16[1024,1024]{1,0:T(8,128)(2,1)S(1)} %copy-done, bf16[256,512]{1,0:T(8,128)(2,1)} %reduce-scatter.5.cloned.1.call-done, bf16[256,512]{1,0:T(8,128)(2,1)S(1)} %add_convert_fusion, f32[1024]{0:T(1024)S(1)} %convert_element_type.34), kind=kOutput, calls=%fused_computation.5 | convolution fusion | flops 538705920 | bytes 3149824 | tf_op jit(solution)/shard_map/dot_general | solution.py:92
  (1 shorter events, 0.0 us)
Async XLA Ops:
  6.5 175.5 %copy-start = (bf16[1024,1024]{1,0:T(8,128)(2,1)S(1)}, bf16[1024,1024]{1,0:T(8,128)(2,1)}, u32[]{:S(2)}) copy-start(bf16[1024,1024]{1,0:T(8,128)(2,1)} %param.7) | copy-start | bytes 6291460
  6.5 60.1 %all-gather.2.cloned.1.call-start = ((), (), s32[]{:S(2)}) async-start(), calls=%async_computation.2 | async-start | bytes 8912896 | tf_op jit(solution)/shard_map/all_gather | solution.py:72
  7.3 130.8 %reduce-scatter.3.cloned.1.call-start = ((), (), s32[]{:S(2)}) async-start(), calls=%async_computation.3 | async-start | bytes 4718592 | tf_op jit(solution)/shard_map/reduce_scatter | solution.py:84
  66.7 0.7 copy-start.2
  79.1 1.9 %copy-start.1 = (bf16[4096,512]{1,0:T(8,128)(2,1)}, bf16[4096,512]{1,0:T(8,128)(2,1)S(1)}, u32[]{:S(2)}) copy-start(bf16[4096,512]{1,0:T(8,128)(2,1)S(1)} %get-tuple-element.7) | copy-start | bytes 12582916
  81.0 101.0 %reduce-scatter.5.cloned.1.call-start = ((), (), s32[]{:S(2)}) async-start(), calls=%async_computation.4 | async-start | bytes 2359296 | tf_op jit(solution)/shard_map/reduce_scatter | solution.py:90
  84.1 49.6 %collective-permute-start.1 = (bf16[8,256,512]{2,1,0:T(8,128)(2,1)}, bf16[8,256,512]{2,1,0:T(8,128)(2,1)}, u32[]{:S(2)}, u32[]{:S(2)}) collective-permute-start(bf16[8,256,512]{2,1,0:T(8,128)(2,1)} %dynamic-slice_bitcast_fusion), channel_id=1, source_target_pairs={{0,8},{8,0},{1,9},{9,1},{2,10},{10,2},{3,11},{11,3},{4,12},{12,4},... | collective-permute-start | bytes 6291464 | tf_op jit(solution)/shard_map/ppermute | solution.py:81
  138.0 4.1 %copy-start.3 = (bf16[1024]{0:T(1024)(128)(2,1)S(1)}, bf16[1024]{0:T(1024)(128)(2,1)}, u32[]{:S(2)}) copy-start(bf16[1024]{0:T(1024)(128)(2,1)} %param.8) | copy-start | bytes 6148
  139.0 9.2 %collective-permute-start = (bf16[256,512]{1,0:T(8,128)(2,1)S(1)}, bf16[256,512]{1,0:T(8,128)(2,1)S(1)}, u32[]{:S(2)}, u32[]{:S(2)}) collective-permute-start(bf16[256,512]{1,0:T(8,128)(2,1)S(1)} %constant_dynamic-slice_fusion), channel_id=1, source_target_pairs={{0,8},{8,0},{1,9},{9,1},{2,10},{10,2},{3,11},{11,3},{4,12},{12,4},... | collective-permute-start | bytes 786440 | tf_op jit(solution)/shard_map/ppermute | solution.py:88
Sparse Core Ops, SparseCore 0:
  9.2 57.4 all-gather.1
  81.1 56.3 reduce-scatter.2
  140.1 41.9 reduce-scatter.4
